TPU v7x, 512 devices: a whole 4x8x8 slice. The times are simulated.
512 devices in a mesh: row: 16 (over y, core), col: 32 (over x, z).
Axes of the slice: x: 4, y: 8, z: 8, core: 2. Of those that a mesh axis runs over, the one named last changes fastest.
Arguments:
- blocks: bfloat16 [16, 64, 8, 128, 128], P('row', 'col'), may hold values from -0.375 to 0.375
- sources: int32 [16, 64, 8], P('row', 'col'), may hold values from 0 to 4
- targets: int32 [16, 64, 8], P('row', 'col'), may hold values from 0 to 4
- counts: int32 [16, 64], P('row', 'col'), may hold values from 1 to 8, as said below
- environment: bfloat16 [16, 64, 5, 128, 128], P('row', 'col'), may hold values from -6 to 6
- top_boundary: bfloat16 [64, 5, 128, 128], P('col'), may hold values from -6 to 6
- decays: float32 [16, 64, 5, 128], P('row', 'col'), may hold values from 0.3 to 1
- weights: float32 [16, 64, 5, 128, 128], P('row', 'col'), may hold values from -0.6 to 0.6
Outputs:
- grad_blocks: bfloat16 [16, 64, 8, 128, 128], P('row', 'col')
- grad_env: bfloat16 [16, 64, 5, 128, 128], P('row', 'col')
- grad_decays: float32 [16, 64, 5, 128], P('row', 'col')
Inputs may be any that keep to these rules, and one draw needn't show every extreme that they name: Slots from counts on are ignored; some site has exactly 8 live slots.
All inputs are finite; a program needn't handle non-finite values.
Results may differ from a plain program's by a relative error of at most 0.0049.
Values may be sent and summed in bfloat16 or wider, within the bound.
No kernel may reach another device: no remote copies, remote signals or barrier semaphores. Data moves between devices by JAX's collectives and lax.ppermute only.
A program may use at most 64 MiB of HBM per device.

v0:
```python
import jax
import jax.numpy as jnp
from jax import lax
from jax.sharding import PartitionSpec as P


def carried_in(value, axis, combine, identity, reverse):
    length, place = (lax.axis_size(axis), lax.axis_index(axis))
    everything = jax.tree.map(lambda part: lax.all_gather(part, axis), value)
    start = jax.tree.map(
        lambda part, zero: jnp.broadcast_to(jnp.asarray(zero, part.dtype), part.shape),
        value,
        identity,
    )

    def lap(k, before):
        at = length - 1 - k if reverse else k
        reached = at > place if reverse else at < place
        new = combine(before, jax.tree.map(lambda part: part[at], everything))
        return jax.tree.map(lambda a, b: jnp.where(reached, a, b), new, before)

    return lax.fori_loop(0, length, lap, start)


def from_behind(value, axis, steps):
    count = lax.axis_size(axis)
    initial, last = (max(0, -steps), min(count, count - steps))
    return lax.ppermute(value, axis, [(source, source + steps) for source in range(initial, last)])


def slot_tables(sources, targets, counts, sector_count):
    active_slot_list = lax.broadcasted_iota(jnp.int32, sources.shape, 2) < counts[:, :, None]
    sector_ids = lax.broadcasted_iota(jnp.int32, sources.shape + (sector_count,), 3)
    src_pick = sources[..., None] == sector_ids
    dst_pick = targets[..., None] == sector_ids
    return (src_pick, dst_pick, active_slot_list)


def forward_blocks(blocks, above_env, src_pick, dst_pick, active_slot_list):
    placed = (dst_pick & active_slot_list[..., None]).astype(jnp.float32)
    src_bf = src_pick.astype(jnp.bfloat16)
    gathered = jnp.einsum(
        "rckn,rcnbj->rckbj", src_bf, above_env, preferred_element_type=jnp.float32
    ).astype(jnp.bfloat16)
    products = jnp.einsum(
        "rckab,rckbj->rckaj", blocks, gathered, preferred_element_type=jnp.float32
    )
    return jnp.einsum("rckn,rckaj->rcnaj", placed, products, precision=lax.Precision.HIGHEST)


def backward_blocks(blocks, above_env, rounded, src_pick, dst_pick, active_slot_list):
    taken = (src_pick & active_slot_list[..., None]).astype(jnp.float32)
    src_bf = src_pick.astype(jnp.bfloat16)
    dst_bf = dst_pick.astype(jnp.bfloat16)
    slot_live = active_slot_list.astype(jnp.float32)
    gathered = jnp.einsum(
        "rckn,rcnbj->rckbj", src_bf, above_env, preferred_element_type=jnp.float32
    ).astype(jnp.bfloat16)
    picked = jnp.einsum(
        "rckn,rcnaj->rckaj", dst_bf, rounded, preferred_element_type=jnp.float32
    ).astype(jnp.bfloat16)
    grads = (
        jnp.einsum("rckaj,rckbj->rckab", picked, gathered, preferred_element_type=jnp.float32)
        * slot_live[..., None, None]
    ).astype(jnp.bfloat16)
    contrib = jnp.einsum("rckab,rckaj->rckbj", blocks, picked, preferred_element_type=jnp.float32)
    returned = jnp.einsum(
        "rckn,rckbj->rcnbj", taken, contrib, precision=lax.Precision.HIGHEST
    ).astype(jnp.bfloat16)
    return (grads, returned)


def affine_join(earlier, latter):
    return (earlier[0] * latter[0], latter[0][..., None] * earlier[1] + latter[1])


def chain_scan(fresh, decay_rows, cotangent):
    row_count, col_count, flat_rows, channel_count = fresh.shape
    identity = (
        jnp.ones((row_count, flat_rows), jnp.float32),
        jnp.zeros((row_count, flat_rows, channel_count), jnp.float32),
    )
    states_now = identity[1]
    passed = identity[0]
    local_states = []
    reach_decay = []
    for column in range(col_count):
        states_now = decay_rows[:, column, :, None] * states_now + fresh[:, column]
        passed = passed * decay_rows[:, column]
        local_states.append(states_now)
        reach_decay.append(passed)
    entering = carried_in((passed, states_now), "col", affine_join, identity, False)
    full_states = [
        local_states[column] + reach_decay[column][..., None] * entering[1]
        for column in range(col_count)
    ]
    before_states = [entering[1]] + full_states[:-1]
    carried = identity[1]
    tail_decay = identity[0]
    local_grads = [None] * col_count
    tail_list = [None] * col_count
    for column in reversed(range(col_count)):
        local_grads[column] = cotangent[:, column] + carried
        tail_list[column] = tail_decay
        carried = decay_rows[:, column, :, None] * local_grads[column]
        tail_decay = tail_decay * decay_rows[:, column]
    arriving = carried_in((tail_decay, carried), "col", affine_join, identity, True)
    full_grads = [
        local_grads[column] + tail_list[column][..., None] * arriving[1]
        for column in range(col_count)
    ]
    condition_derivative = jnp.stack(full_grads, 1)
    gate_grad = jnp.stack(
        [jnp.sum(full_grads[column] * before_states[column], -1) for column in range(col_count)], 1
    )
    return (condition_derivative, gate_grad)


def local(blocks, sources, targets, counts, environment, top_boundary, decays, weights):
    row_count, col_count, sector_count, block_rows, channel_count = environment.shape
    flat_rows = sector_count * block_rows
    bottom = environment[row_count - 1]
    upper_env = from_behind(bottom, "row", 1)
    upper_env = jnp.where(lax.axis_index("row") == 0, top_boundary, upper_env)
    above_env = jnp.concatenate([upper_env[None], environment[: row_count - 1]], 0)
    src_pick, dst_pick, active_slot_list = slot_tables(sources, targets, counts, sector_count)
    transferred = forward_blocks(blocks, above_env, src_pick, dst_pick, active_slot_list)
    fresh = (environment.astype(jnp.float32) + transferred).reshape(
        row_count, col_count, flat_rows, channel_count
    )
    decay_rows = decays.reshape(row_count, col_count, flat_rows)
    cotangent = weights.reshape(row_count, col_count, flat_rows, channel_count)
    condition_derivative, gate_grad = chain_scan(fresh, decay_rows, cotangent)
    condition_derivative = condition_derivative.reshape(environment.shape)
    rounded = condition_derivative.astype(jnp.bfloat16)
    grad_blocks, returned = backward_blocks(
        blocks, above_env, rounded, src_pick, dst_pick, active_slot_list
    )
    below_rows = from_behind(returned[0], "row", -1)
    following_horizontals = jnp.concatenate([returned[1:], below_rows[None]], 0)
    grad_env = (condition_derivative + following_horizontals.astype(jnp.float32)).astype(
        jnp.bfloat16
    )
    grad_decays = gate_grad.reshape(decays.shape)
    return (grad_blocks, grad_env, grad_decays)


def solution(mesh):
    in_specs = (
        P("row", "col", None, None, None),
        P("row", "col", None),
        P("row", "col", None),
        P("row", "col"),
        P("row", "col", None, None, None),
        P("col", None, None, None),
        P("row", "col", None, None),
        P("row", "col", None, None, None),
    )
    out_specs = (
        P("row", "col", None, None, None),
        P("row", "col", None, None, None),
        P("row", "col", None, None),
    )
    return jax.shard_map(local, mesh=mesh, in_specs=in_specs, out_specs=out_specs, check_vma=False)
```

profile of v0, /device:TPU:1, one launch (start us, length us, event | category | flops | bytes accessed | tf_op | source)
XLA Modules:
  0.0 326.6 jit_solution(7247512039786172115)
XLA Ops:
  7.2 4.7 %collective-permute-start = (bf16[2,5,128,128]{3,2,1,0:T(8,128)(2,1)}, bf16[2,5,128,128]{3,2,1,0:T(8,128)(2,1)S(1)}, u32[]{:S(2)}, u32[]{:S(2)}) collective-permute-start(bf16[2,5,128,128]{3,2,1,0:T(8,128)(2,1)} %bitcast.90), channel_id=1, source_target_pairs={{0,32},{32,64},{64,96},{96,128},{128,160},{160,192},{192,224},{224... | collective-permute-start | bytes 983048 | tf_op jit(solution)/shard_map/ppermute | solution.py:28
  13.5 3.4 %collective-permute-done = bf16[2,5,128,128]{3,2,1,0:T(8,128)(2,1)S(1)} collective-permute-done((bf16[2,5,128,128]{3,2,1,0:T(8,128)(2,1)}, bf16[2,5,128,128]{3,2,1,0:T(8,128)(2,1)S(1)}, u32[]{:S(2)}, u32[]{:S(2)}) %collective-permute-start) | collective-permute-done | bytes 327712 | tf_op jit(solution)/shard_map/ppermute | solution.py:28
  19.2 1.3 fusion.20
  21.7 2.2 add_multiply_fusion
  24.7 39.7 %all_gather.6 = f32[32,1,640]{2,1,0:T(1,128)S(1)} all-gather(f32[1,1,640]{2,1,0:T(1,128)S(1)} %get-tuple-element.305), channel_id=1, replica_groups=mesh['row'=16,'col'=32] {'col'}, dimensions={0}, use_global_device_ids=true | all-gather | bytes 84480 | tf_op jit(solution)/shard_map/all_gather | solution.py:9
  64.4 80.5 %all-gather.5.cloned.1.call-done = f32[32,1,640,128]{3,2,1,0:T(8,128)} async-done(((f32[1,1,640,128]{3,2,1,0:T(8,128)}), f32[32,1,640,128]{3,2,1,0:T(8,128)}) %all-gather.5.cloned.1.call-update) | async-done | bytes 10485776 | tf_op jit(solution)/shard_map/all_gather | solution.py:9
  144.9 39.7 %while.31 = (s32[]{:T(128)}, f32[1,640,128]{2,1,0:T(8,128)S(1)}, s32[]{:T(128)}, f32[32,1,640]{2,1,0:T(1,128)S(1)}, f32[32,1,640,128]{3,2,1,0:T(8,128)}, /*index=5*/s32[]{:T(128)}, s32[]{:T(128)}) while((s32[]{:T(128)}, f32[1,640,128]{2,1,0:T(8,128)S(1)}, s32[]{:T(128)}, f32[32,1,640]{2,1,0:T(1,128)S(1)}, ...), condition=%wide.region_3.4_spmd.clone, body=%wide.region_2.3_spmd.clone.sunk | while | flops 327684 | bytes 990833 | solution.py:22
  159.9 1.2 fusion.42
  161.1 1.2 fusion.42
  163.6 1.2 fusion.42
  167.3 1.2 fusion.42
  168.6 1.2 fusion.42
  176.0 1.2 fusion.42
  177.3 1.2 fusion.42
  178.5 1.2 fusion.42
  184.7 75.9 %all-gather.3.cloned.1.call-done = f32[32,1,640,128]{3,2,1,0:T(8,128)} async-done(((f32[1,1,640,128]{3,2,1,0:T(8,128)}), f32[32,1,640,128]{3,2,1,0:T(8,128)}) %all-gather.3.cloned.1.call-update) | async-done | bytes 10485776 | tf_op jit(solution)/shard_map/all_gather | solution.py:9
  260.5 40.0 %while.30 = (s32[]{:T(128)}, f32[1,640,128]{2,1,0:T(8,128)S(1)}, s32[]{:T(128)}, f32[32,1,640]{2,1,0:T(1,128)S(1)}, f32[32,1,640,128]{3,2,1,0:T(8,128)}, /*index=5*/s32[]{:T(128)}, s32[]{:T(128)}, s32[]{:T(128)}, s32[]{:T(128)}) while((s32[]{:T(128)}, f32[1,640,128]{2,1,0:T(8,128)S(1)}, s32[]{:T(128)}, ...), condition=%wide.region_1.2_spmd.clone, body=%wide.region_0.1_spmd.clone.sunk | while | flops 327688 | bytes 990895 | solution.py:22
  260.6 1.2 fusion.41
  261.8 1.2 fusion.41
  263.1 1.2 fusion.41
  264.3 1.2 fusion.41
  265.6 1.2 fusion.41
  266.8 1.2 fusion.41
  268.1 1.2 fusion.41
  269.3 1.2 fusion.41
  270.6 1.2 fusion.41
  271.8 1.2 fusion.41
  273.1 1.2 fusion.41
  274.3 1.2 fusion.41
  275.6 1.2 fusion.41
  276.8 1.2 fusion.41
  278.1 1.2 fusion.41
  279.3 1.2 fusion.41
  280.6 1.2 fusion.41
  281.8 1.2 fusion.41
  283.1 1.2 fusion.41
  284.3 1.2 fusion.41
  285.6 1.2 fusion.41
  286.8 1.2 fusion.41
  288.1 1.2 fusion.41
  289.3 1.2 fusion.41
  293.1 1.2 fusion.41
  296.8 1.2 fusion.41
  302.2 1.3 convolution_bitcast_fusion.1
  303.5 2.6 copy.56
  306.1 1.8 convolution_convert_fusion.2
  307.9 3.0 collective-permute-start.1
  312.6 6.2 %collective-permute-done.1 = bf16[2,5,128,128]{3,1,2,0:T(8,128)(2,1)S(1)} collective-permute-done((bf16[2,5,128,128]{3,1,2,0:T(8,128)(2,1)S(1)}, bf16[2,5,128,128]{3,1,2,0:T(8,128)(2,1)S(1)}, u32[]{:S(2)}, u32[]{:S(2)}) %collective-permute-start.1) | collective-permute-done | bytes 327712 | tf_op jit(solution)/shard_map/ppermute | solution.py:28
  (127 shorter events, 46.9 us)
Async XLA Ops:
  7.2 11.2 %copy-start = (bf16[1,2,8,128,128]{4,3,2,1,0:T(8,128)(2,1)S(1)}, bf16[1,2,8,128,128]{4,3,2,1,0:T(8,128)(2,1)}, u32[]{:S(2)}) copy-start(bf16[1,2,8,128,128]{4,3,2,1,0:T(8,128)(2,1)} %param.12) | copy-start | bytes 1572868
  7.2 137.8 %all-gather.5.cloned.1.call-start = ((), (), s32[]{:S(2)}) async-start(), calls=%async_computation.1 | async-start | bytes 10813440 | tf_op jit(solution)/shard_map/all_gather | solution.py:9
  7.2 9.6 %collective-permute-start = (bf16[2,5,128,128]{3,2,1,0:T(8,128)(2,1)}, bf16[2,5,128,128]{3,2,1,0:T(8,128)(2,1)S(1)}, u32[]{:S(2)}, u32[]{:S(2)}) collective-permute-start(bf16[2,5,128,128]{3,2,1,0:T(8,128)(2,1)} %bitcast.90), channel_id=1, source_target_pairs={{0,32},{32,64},{64,96},{96,128},{128,160},{160,192},{192,224},{224... | collective-permute-start | bytes 983048 | tf_op jit(solution)/shard_map/ppermute | solution.py:28
  19.2 281.3 %copy-start.1 = (f32[1,2,5,128,128]{4,3,2,1,0:T(8,128)S(1)}, f32[1,2,5,128,128]{4,3,2,1,0:T(8,128)}, u32[]{:S(2)}) copy-start(f32[1,2,5,128,128]{4,3,2,1,0:T(8,128)} %param.19) | copy-start | bytes 1966084
  19.2 282.2 %copy-start.3 = (s32[1,2,8]{2,1,0:T(2,128)S(1)}, s32[1,2,8]{2,1,0:T(2,128)}, u32[]{:S(2)}) copy-start(s32[1,2,8]{2,1,0:T(2,128)} %param.14) | copy-start | bytes 196
  24.0 236.6 %all-gather.3.cloned.1.call-start = ((), (), s32[]{:S(2)}) async-start(), calls=%async_computation | async-start | bytes 10813440 | tf_op jit(solution)/shard_map/all_gather | solution.py:9
  144.9 161.1 %copy-start.2 = (s32[1,2,8]{2,1,0:T(2,128)S(1)}, s32[1,2,8]{2,1,0:T(2,128)}, u32[]{:S(2)}) copy-start(s32[1,2,8]{2,1,0:T(2,128)} %param.13) | copy-start | bytes 196
  307.9 10.9 %collective-permute-start.1 = (bf16[2,5,128,128]{3,1,2,0:T(8,128)(2,1)S(1)}, bf16[2,5,128,128]{3,1,2,0:T(8,128)(2,1)S(1)}, u32[]{:S(2)}, u32[]{:S(2)}) collective-permute-start(bf16[2,5,128,128]{3,1,2,0:T(8,128)(2,1)S(1)} %convolution_convert_fusion.2), channel_id=1, source_target_pairs={{32,0},{64,32},{96,64},{128,96},{160,128},{192,160},{224,192},{256... | collective-permute-start | bytes 983048 | tf_op jit(solution)/shard_map/ppermute | solution.py:28
Sparse Core Ops, SparseCore 0:
  24.1 120.8 all-gather.4
  148.7 111.8 all-gather.2
where the time goes:
time: 329 us; the launch traced here: 327 us
  waiting for transfers between devices  167 us (51%)
  other arithmetic  81.6 us (25%)
  blocking collectives  39.7 us (12%)
  between operations  14.2 us (4%)
  starting transfers between devices  7.76 us (2%)
  matrix products  7.46 us (2%)
  local copies, waits for them, and re-layouts  6.71 us (2%)
    all_gather x2, waiting for transfers between devices, carried_in(): everything = jax.tree.map(lambda part: lax.all_gather(part, axis), value)  156 us
    select_n x64, other arithmetic, lap(): return jax.tree.map(lambda a, b: jnp.where(reached, a, b), new, before)  76.1 us
    all_gather x1, blocking collectives, carried_in(): everything = jax.tree.map(lambda part: lax.all_gather(part, axis), value)  39.7 us
    ppermute x2, waiting for transfers between devices, from_behind(): lax.ppermute(value, axis, [(source, source + steps) for source in range(i...  9.54 us
    ppermute x2, starting transfers between devices, from_behind(): lax.ppermute(value, axis, [(source, source + steps) for source in range(i...  7.68 us
  transfers between devices with their start and end apart: 4, of which 4 were waited for; matrix products, arithmetic and copies ran while one was open for 13% of the time, Pallas kernels for 0%

commit v1 on v0

--- a/solution.py
+++ b/solution.py
@@ -4,22 +4,36 @@
 from jax.sharding import PartitionSpec as P
 
 
-def carried_in(value, axis, combine, identity, reverse):
-    length, place = (lax.axis_size(axis), lax.axis_index(axis))
-    everything = jax.tree.map(lambda part: lax.all_gather(part, axis), value)
-    start = jax.tree.map(
-        lambda part, zero: jnp.broadcast_to(jnp.asarray(zero, part.dtype), part.shape),
-        value,
-        identity,
-    )
-
-    def lap(k, before):
-        at = length - 1 - k if reverse else k
-        reached = at > place if reverse else at < place
-        new = combine(before, jax.tree.map(lambda part: part[at], everything))
-        return jax.tree.map(lambda a, b: jnp.where(reached, a, b), new, before)
-
-    return lax.fori_loop(0, length, lap, start)
+def scan_over(axis, passed, carried, reverse):
+    count = lax.axis_size(axis)
+    row_count, flat_rows, channel_count = carried.shape
+    packed_rows = flat_rows // channel_count
+    together = flat_rows % channel_count == 0
+    window_a, window_b = passed, carried
+    enter_a = jnp.ones_like(passed)
+    enter_b = jnp.zeros_like(carried)
+    distance = 1
+    while distance < count:
+        if reverse:
+            pairs = [(source, source - distance) for source in range(distance, count)]
+        else:
+            pairs = [(source, source + distance) for source in range(count - distance)]
+        if together:
+            sent = jnp.concatenate(
+                [window_b, window_a.reshape(row_count, packed_rows, channel_count)], 1
+            )
+            got = lax.ppermute(sent, axis, pairs)
+            got_b = got[:, :flat_rows]
+            got_a = got[:, flat_rows:].reshape(row_count, flat_rows)
+        else:
+            got_a, got_b = lax.ppermute((window_a, window_b), axis, pairs)
+        enter_b = enter_a[..., None] * got_b + enter_b
+        enter_a = enter_a * got_a
+        if 2 * distance < count:
+            window_b = window_a[..., None] * got_b + window_b
+            window_a = window_a * got_a
+        distance *= 2
+    return enter_b
 
 
 def from_behind(value, axis, steps):
@@ -70,10 +84,6 @@
     return (grads, returned)
 
 
-def affine_join(earlier, latter):
-    return (earlier[0] * latter[0], latter[0][..., None] * earlier[1] + latter[1])
-
-
 def chain_scan(fresh, decay_rows, cotangent):
     row_count, col_count, flat_rows, channel_count = fresh.shape
     identity = (
@@ -89,12 +99,12 @@
         passed = passed * decay_rows[:, column]
         local_states.append(states_now)
         reach_decay.append(passed)
-    entering = carried_in((passed, states_now), "col", affine_join, identity, False)
+    entering = scan_over("col", passed, states_now, False)
     full_states = [
-        local_states[column] + reach_decay[column][..., None] * entering[1]
+        local_states[column] + reach_decay[column][..., None] * entering
         for column in range(col_count)
     ]
-    before_states = [entering[1]] + full_states[:-1]
+    before_states = [entering] + full_states[:-1]
     carried = identity[1]
     tail_decay = identity[0]
     local_grads = [None] * col_count
@@ -104,9 +114,9 @@
         tail_list[column] = tail_decay
         carried = decay_rows[:, column, :, None] * local_grads[column]
         tail_decay = tail_decay * decay_rows[:, column]
-    arriving = carried_in((tail_decay, carried), "col", affine_join, identity, True)
+    arriving = scan_over("col", tail_decay, carried, True)
     full_grads = [
-        local_grads[column] + tail_list[column][..., None] * arriving[1]
+        local_grads[column] + tail_list[column][..., None] * arriving
         for column in range(col_count)
     ]
     condition_derivative = jnp.stack(full_grads, 1)

time: 329 us -> 143 us (0.43)
  the two profiles are of different devices: /device:TPU:1 before, /device:TPU:195 now
where the time goes in v1:
time: 143 us; the launch traced here: 142 us
  waiting for transfers between devices  81.9 us (57%)
  starting transfers between devices  41.2 us (29%)
  local copies, waits for them, and re-layouts  8.8 us (6%)
  matrix products  6.04 us (4%)
  other arithmetic  3.33 us (2%)
    ppermute x10, waiting for transfers between devices, scan_over(): got = lax.ppermute(sent, axis, pairs)  50.5 us
    ppermute x10, starting transfers between devices, scan_over(): got = lax.ppermute(sent, axis, pairs)  32.9 us
    ppermute x2, waiting for transfers between devices, from_behind(): lax.ppermute(value, axis, [(source, source + steps) for source in range(i...  31.4 us
    ppermute x2, starting transfers between devices, from_behind(): lax.ppermute(value, axis, [(source, source + steps) for source in range(i...  8.34 us
    unnamed x17, local copies, waits for them, and re-layouts  4.89 us
  transfers between devices with their start and end apart: 12, of which 10 were waited for; matrix products, arithmetic and copies ran while one was open for 2% of the time, Pallas kernels for 0%

profile of v1, /device:TPU:195, one launch (start us, length us, event | category | flops | bytes accessed | tf_op | source)
XLA Modules:
  0.0 142.4 jit_solution(10803456986164944924)
XLA Ops:
  0.6 3.9 %collective-permute-start.5 = (bf16[2,5,128,128]{3,2,1,0:T(8,128)(2,1)}, bf16[2,5,128,128]{3,2,1,0:T(8,128)(2,1)S(1)}, u32[]{:S(2)}, u32[]{:S(2)}) collective-permute-start(bf16[2,5,128,128]{3,2,1,0:T(8,128)(2,1)} %bitcast.130), channel_id=1, source_target_pairs={{0,32},{32,64},{64,96},{96,128},{128,160},{160,192},{192,224},{224... | collective-permute-start | bytes 983048 | tf_op jit(solution)/shard_map/ppermute | solution.py:42
  4.6 0.6 copy-done.6
  5.3 3.5 %collective-permute-done.5 = bf16[2,5,128,128]{3,2,1,0:T(8,128)(2,1)S(1)} collective-permute-done((bf16[2,5,128,128]{3,2,1,0:T(8,128)(2,1)}, bf16[2,5,128,128]{3,2,1,0:T(8,128)(2,1)S(1)}, u32[]{:S(2)}, u32[]{:S(2)}) %collective-permute-start.5) | collective-permute-done | bytes 327712 | tf_op jit(solution)/shard_map/ppermute | solution.py:42
  8.9 0.7 copy-done.4
  9.6 0.4 convolution_convert_fusion
  10.0 0.4 copy.38
  10.4 0.5 convolution_bitcast_fusion
  10.8 0.4 copy.39
  11.3 0.7 copy-done.5
  11.9 0.6 fusion.19
  12.5 0.4 copy-done.2
  13.0 0.9 copy-done.1
  14.0 0.3 broadcast_multiply_fusion
  14.4 5.2 %collective-permute-start.7 = (f32[1,645,128]{2,1,0:T(8,128)S(1)}, f32[1,645,128]{2,1,0:T(8,128)S(1)}, u32[]{:S(2)}, u32[]{:S(2)}) collective-permute-start(f32[1,645,128]{2,1,0:T(8,128)S(1)} %get-tuple-element.38), channel_id=1, source_target_pairs={{0,1},{1,2},{2,3},{3,4},{4,5},{5,6},{6,7},{7,8},{8,9},{9,10},{10,1... | collective-permute-start | bytes 990728 | tf_op jit(solution)/shard_map/ppermute | solution.py:25
  19.6 1.9 %collective-permute-start = (f32[1,645,128]{2,1,0:T(8,128)S(1)}, f32[1,645,128]{2,1,0:T(8,128)S(1)}, u32[]{:S(2)}, u32[]{:S(2)}) collective-permute-start(f32[1,645,128]{2,1,0:T(8,128)S(1)} %get-tuple-element.37), channel_id=1, source_target_pairs={{1,0},{2,1},{3,2},{4,3},{5,4},{6,5},{7,6},{8,7},{9,8},{10,9},{11,1... | collective-permute-start | bytes 990728 | tf_op jit(solution)/shard_map/ppermute | solution.py:25
  21.5 2.9 %collective-permute-done.7 = f32[1,645,128]{2,1,0:T(8,128)S(1)} collective-permute-done((f32[1,645,128]{2,1,0:T(8,128)S(1)}, f32[1,645,128]{2,1,0:T(8,128)S(1)}, u32[]{:S(2)}, u32[]{:S(2)}) %collective-permute-start.7) | collective-permute-done | bytes 330272 | tf_op jit(solution)/shard_map/ppermute | solution.py:25
  24.4 5.3 %collective-permute-done = f32[1,645,128]{2,1,0:T(8,128)S(1)} collective-permute-done((f32[1,645,128]{2,1,0:T(8,128)S(1)}, f32[1,645,128]{2,1,0:T(8,128)S(1)}, u32[]{:S(2)}, u32[]{:S(2)}) %collective-permute-start) | collective-permute-done | bytes 330272 | tf_op jit(solution)/shard_map/ppermute | solution.py:25
  29.7 0.2 multiply_add_fusion.8
  29.9 2.8 %collective-permute-start.8 = (f32[1,645,128]{2,1,0:T(8,128)S(1)}, f32[1,645,128]{2,1,0:T(8,128)S(1)}, u32[]{:S(2)}, u32[]{:S(2)}) collective-permute-start(f32[1,645,128]{2,1,0:T(8,128)S(1)} %pad_maximum_fusion.6), channel_id=1, source_target_pairs={{0,2},{1,3},{2,4},{3,5},{4,6},{5,7},{6,8},{7,9},{8,10},{9,11},{10,... | collective-permute-start | bytes 990728 | tf_op jit(solution)/shard_map/ppermute | solution.py:25
  32.8 3.4 %collective-permute-start.1 = (f32[1,645,128]{2,1,0:T(8,128)S(1)}, f32[1,645,128]{2,1,0:T(8,128)S(1)}, u32[]{:S(2)}, u32[]{:S(2)}) collective-permute-start(f32[1,645,128]{2,1,0:T(8,128)S(1)} %pad_maximum_fusion.2), channel_id=1, source_target_pairs={{2,0},{3,1},{4,2},{5,3},{6,4},{7,5},{8,6},{9,7},{10,8},{11,9},{12,... | collective-permute-start | bytes 990728 | tf_op jit(solution)/shard_map/ppermute | solution.py:25
  36.2 10.0 %collective-permute-done.8 = f32[1,645,128]{2,1,0:T(8,128)S(1)} collective-permute-done((f32[1,645,128]{2,1,0:T(8,128)S(1)}, f32[1,645,128]{2,1,0:T(8,128)S(1)}, u32[]{:S(2)}, u32[]{:S(2)}) %collective-permute-start.8) | collective-permute-done | bytes 330272 | tf_op jit(solution)/shard_map/ppermute | solution.py:25
  46.3 6.7 %collective-permute-start.9 = (f32[1,645,128]{2,1,0:T(8,128)S(1)}, f32[1,645,128]{2,1,0:T(8,128)S(1)}, u32[]{:S(2)}, u32[]{:S(2)}) collective-permute-start(f32[1,645,128]{2,1,0:T(8,128)S(1)} %pad_maximum_fusion.7), channel_id=1, source_target_pairs={{0,4},{1,5},{2,6},{3,7},{4,8},{5,9},{6,10},{7,11},{8,12},{9,13},{1... | collective-permute-start | bytes 990728 | tf_op jit(solution)/shard_map/ppermute | solution.py:25
  53.1 0.2 multiply_add_fusion.7
  53.3 3.4 %collective-permute-start.2 = (f32[1,645,128]{2,1,0:T(8,128)S(1)}, f32[1,645,128]{2,1,0:T(8,128)S(1)}, u32[]{:S(2)}, u32[]{:S(2)}) collective-permute-start(f32[1,645,128]{2,1,0:T(8,128)S(1)} %pad_maximum_fusion.3), channel_id=1, source_target_pairs={{4,0},{5,1},{6,2},{7,3},{8,4},{9,5},{10,6},{11,7},{12,8},{13,9},{1... | collective-permute-start | bytes 990728 | tf_op jit(solution)/shard_map/ppermute | solution.py:25
  56.7 9.4 %collective-permute-done.9 = f32[1,645,128]{2,1,0:T(8,128)S(1)} collective-permute-done((f32[1,645,128]{2,1,0:T(8,128)S(1)}, f32[1,645,128]{2,1,0:T(8,128)S(1)}, u32[]{:S(2)}, u32[]{:S(2)}) %collective-permute-start.9) | collective-permute-done | bytes 330272 | tf_op jit(solution)/shard_map/ppermute | solution.py:25
  66.1 0.2 multiply_add_fusion.1
  66.3 3.4 %collective-permute-start.10 = (f32[1,645,128]{2,1,0:T(8,128)S(1)}, f32[1,645,128]{2,1,0:T(8,128)S(1)}, u32[]{:S(2)}, u32[]{:S(2)}) collective-permute-start(f32[1,645,128]{2,1,0:T(8,128)S(1)} %pad_maximum_fusion.8), channel_id=1, source_target_pairs={{0,8},{1,9},{2,10},{3,11},{4,12},{5,13},{6,14},{7,15},{8,16},{9,17... | collective-permute-start | bytes 990728 | tf_op jit(solution)/shard_map/ppermute | solution.py:25
  69.7 7.7 %collective-permute-done.2 = f32[1,645,128]{2,1,0:T(8,128)S(1)} collective-permute-done((f32[1,645,128]{2,1,0:T(8,128)S(1)}, f32[1,645,128]{2,1,0:T(8,128)S(1)}, u32[]{:S(2)}, u32[]{:S(2)}) %collective-permute-start.2) | collective-permute-done | bytes 330272 | tf_op jit(solution)/shard_map/ppermute | solution.py:25
  77.4 0.2 multiply_add_fusion.6
  77.6 1.9 %collective-permute-start.3 = (f32[1,645,128]{2,1,0:T(8,128)S(1)}, f32[1,645,128]{2,1,0:T(8,128)S(1)}, u32[]{:S(2)}, u32[]{:S(2)}) collective-permute-start(f32[1,645,128]{2,1,0:T(8,128)S(1)} %pad_maximum_fusion.4), channel_id=1, source_target_pairs={{8,0},{9,1},{10,2},{11,3},{12,4},{13,5},{14,6},{15,7},{16,8},{17,9... | collective-permute-start | bytes 990728 | tf_op jit(solution)/shard_map/ppermute | solution.py:25
  79.8 2.9 %collective-permute-start.11 = (f32[1,645,128]{2,1,0:T(8,128)S(1)}, f32[1,645,128]{2,1,0:T(8,128)S(1)}, u32[]{:S(2)}, u32[]{:S(2)}) collective-permute-start(f32[1,645,128]{2,1,0:T(8,128)S(1)} %pad_maximum_fusion.9), channel_id=1, source_target_pairs={{0,16},{1,17},{2,18},{3,19},{4,20},{5,21},{6,22},{7,23},{8,24},{9,... | collective-permute-start | bytes 990728 | tf_op jit(solution)/shard_map/ppermute | solution.py:25
  82.7 5.5 %collective-permute-done.3 = f32[1,645,128]{2,1,0:T(8,128)S(1)} collective-permute-done((f32[1,645,128]{2,1,0:T(8,128)S(1)}, f32[1,645,128]{2,1,0:T(8,128)S(1)}, u32[]{:S(2)}, u32[]{:S(2)}) %collective-permute-start.3) | collective-permute-done | bytes 330272 | tf_op jit(solution)/shard_map/ppermute | solution.py:25
  88.3 1.3 collective-permute-start.4
  89.6 3.7 %collective-permute-done.11 = f32[1,645,128]{2,1,0:T(8,128)S(1)} collective-permute-done((f32[1,645,128]{2,1,0:T(8,128)S(1)}, f32[1,645,128]{2,1,0:T(8,128)S(1)}, u32[]{:S(2)}, u32[]{:S(2)}) %collective-permute-start.11) | collective-permute-done | bytes 330272 | tf_op jit(solution)/shard_map/ppermute | solution.py:25
  93.3 6.1 %collective-permute-done.4 = f32[1,645,128]{2,1,0:T(8,128)S(1)} collective-permute-done((f32[1,645,128]{2,1,0:T(8,128)S(1)}, f32[1,645,128]{2,1,0:T(8,128)S(1)}, u32[]{:S(2)}, u32[]{:S(2)}) %collective-permute-start.4) | collective-permute-done | bytes 330272 | tf_op jit(solution)/shard_map/ppermute | solution.py:25
  99.4 1.2 multiply_reduce_fusion.1
  100.6 0.2 copy_dynamic-update-slice_fusion.1
  100.8 0.2 copy_dynamic-update-slice_fusion
  101.0 0.3 convolution_convert_fusion.1
  101.4 0.4 copy.36
  101.8 1.3 convolution_bitcast_fusion.1
  103.0 2.6 %copy.37 = f32[2,8,128,128]{3,1,2,0:T(8,128)} copy(f32[2,8,128,128]{2,3,1,0:T(8,128)} %convolution_bitcast_fusion.1) | data formatting | bytes 2097152 | tf_op jit(solution)/shard_map/rckab,rckaj->rckbj/dot_general | solution.py:80
  105.6 1.8 %convolution_convert_fusion.2 = bf16[2,5,128,128]{3,1,2,0:T(8,128)(2,1)S(1)} fusion(f32[2,8,128,128]{3,1,2,0:T(8,128)} %copy.37, s32[2,8]{1,0:T(2,128)S(1)} %bitcast.136, pred[2,8]{1,0:T(4,128)(4,1)S(1)} %get-tuple-element.42), kind=kOutput, calls=%fused_computation.6 | convolution fusion | flops 15892640 | bytes 1376336 | tf_op jit(solution)/shard_map/rckn,rckbj->rcnbj/dot_general | solution.py:81
  107.4 4.4 %collective-permute-start.6 = (bf16[2,5,128,128]{3,1,2,0:T(8,128)(2,1)S(1)}, bf16[2,5,128,128]{3,1,2,0:T(8,128)(2,1)S(1)}, u32[]{:S(2)}, u32[]{:S(2)}) collective-permute-start(bf16[2,5,128,128]{3,1,2,0:T(8,128)(2,1)S(1)} %convolution_convert_fusion.2), channel_id=1, source_target_pairs={{32,0},{64,32},{96,64},{128,96},{160,128},{192,160},{224,192},{256... | collective-permute-start | bytes 983048 | tf_op jit(solution)/shard_map/ppermute | solution.py:42
  111.9 0.6 copy.42
  112.5 1.1 fusion.1
  113.6 27.8 %collective-permute-done.6 = bf16[2,5,128,128]{3,1,2,0:T(8,128)(2,1)S(1)} collective-permute-done((bf16[2,5,128,128]{3,1,2,0:T(8,128)(2,1)S(1)}, bf16[2,5,128,128]{3,1,2,0:T(8,128)(2,1)S(1)}, u32[]{:S(2)}, u32[]{:S(2)}) %collective-permute-start.6) | collective-permute-done | bytes 327712 | tf_op jit(solution)/shard_map/ppermute | solution.py:42
  141.6 0.8 copy.41
  (44 shorter events, 1.2 us)
Async XLA Ops:
  0.6 9.7 %copy-start = (bf16[1,2,8,128,128]{4,3,2,1,0:T(8,128)(2,1)S(1)}, bf16[1,2,8,128,128]{4,3,2,1,0:T(8,128)(2,1)}, u32[]{:S(2)}) copy-start(bf16[1,2,8,128,128]{4,3,2,1,0:T(8,128)(2,1)} %param.8) | copy-start | bytes 1572868
  0.6 8.2 %collective-permute-start.5 = (bf16[2,5,128,128]{3,2,1,0:T(8,128)(2,1)}, bf16[2,5,128,128]{3,2,1,0:T(8,128)(2,1)S(1)}, u32[]{:S(2)}, u32[]{:S(2)}) collective-permute-start(bf16[2,5,128,128]{3,2,1,0:T(8,128)(2,1)} %bitcast.130), channel_id=1, source_target_pairs={{0,32},{32,64},{64,96},{96,128},{128,160},{160,192},{192,224},{224... | collective-permute-start | bytes 983048 | tf_op jit(solution)/shard_map/ppermute | solution.py:42
  4.6 0.7 copy-start.6
  4.6 0.7 copy-start.3
  8.9 0.7 copy-start.4
  11.2 0.7 copy-start.5
  11.9 1.0 copy-start.2
  12.9 1.1 copy-start.1
  14.4 10.0 %collective-permute-start.7 = (f32[1,645,128]{2,1,0:T(8,128)S(1)}, f32[1,645,128]{2,1,0:T(8,128)S(1)}, u32[]{:S(2)}, u32[]{:S(2)}) collective-permute-start(f32[1,645,128]{2,1,0:T(8,128)S(1)} %get-tuple-element.38), channel_id=1, source_target_pairs={{0,1},{1,2},{2,3},{3,4},{4,5},{5,6},{6,7},{7,8},{8,9},{9,10},{10,1... | collective-permute-start | bytes 990728 | tf_op jit(solution)/shard_map/ppermute | solution.py:25
  19.6 10.1 %collective-permute-start = (f32[1,645,128]{2,1,0:T(8,128)S(1)}, f32[1,645,128]{2,1,0:T(8,128)S(1)}, u32[]{:S(2)}, u32[]{:S(2)}) collective-permute-start(f32[1,645,128]{2,1,0:T(8,128)S(1)} %get-tuple-element.37), channel_id=1, source_target_pairs={{1,0},{2,1},{3,2},{4,3},{5,4},{6,5},{7,6},{8,7},{9,8},{10,9},{11,1... | collective-permute-start | bytes 990728 | tf_op jit(solution)/shard_map/ppermute | solution.py:25
  29.9 16.2 %collective-permute-start.8 = (f32[1,645,128]{2,1,0:T(8,128)S(1)}, f32[1,645,128]{2,1,0:T(8,128)S(1)}, u32[]{:S(2)}, u32[]{:S(2)}) collective-permute-start(f32[1,645,128]{2,1,0:T(8,128)S(1)} %pad_maximum_fusion.6), channel_id=1, source_target_pairs={{0,2},{1,3},{2,4},{3,5},{4,6},{5,7},{6,8},{7,9},{8,10},{9,11},{10,... | collective-permute-start | bytes 990728 | tf_op jit(solution)/shard_map/ppermute | solution.py:25
  32.8 20.3 %collective-permute-start.1 = (f32[1,645,128]{2,1,0:T(8,128)S(1)}, f32[1,645,128]{2,1,0:T(8,128)S(1)}, u32[]{:S(2)}, u32[]{:S(2)}) collective-permute-start(f32[1,645,128]{2,1,0:T(8,128)S(1)} %pad_maximum_fusion.2), channel_id=1, source_target_pairs={{2,0},{3,1},{4,2},{5,3},{6,4},{7,5},{8,6},{9,7},{10,8},{11,9},{12,... | collective-permute-start | bytes 990728 | tf_op jit(solution)/shard_map/ppermute | solution.py:25
  46.3 19.7 %collective-permute-start.9 = (f32[1,645,128]{2,1,0:T(8,128)S(1)}, f32[1,645,128]{2,1,0:T(8,128)S(1)}, u32[]{:S(2)}, u32[]{:S(2)}) collective-permute-start(f32[1,645,128]{2,1,0:T(8,128)S(1)} %pad_maximum_fusion.7), channel_id=1, source_target_pairs={{0,4},{1,5},{2,6},{3,7},{4,8},{5,9},{6,10},{7,11},{8,12},{9,13},{1... | collective-permute-start | bytes 990728 | tf_op jit(solution)/shard_map/ppermute | solution.py:25
  53.3 24.1 %collective-permute-start.2 = (f32[1,645,128]{2,1,0:T(8,128)S(1)}, f32[1,645,128]{2,1,0:T(8,128)S(1)}, u32[]{:S(2)}, u32[]{:S(2)}) collective-permute-start(f32[1,645,128]{2,1,0:T(8,128)S(1)} %pad_maximum_fusion.3), channel_id=1, source_target_pairs={{4,0},{5,1},{6,2},{7,3},{8,4},{9,5},{10,6},{11,7},{12,8},{13,9},{1... | collective-permute-start | bytes 990728 | tf_op jit(solution)/shard_map/ppermute | solution.py:25
  66.3 13.3 %collective-permute-start.10 = (f32[1,645,128]{2,1,0:T(8,128)S(1)}, f32[1,645,128]{2,1,0:T(8,128)S(1)}, u32[]{:S(2)}, u32[]{:S(2)}) collective-permute-start(f32[1,645,128]{2,1,0:T(8,128)S(1)} %pad_maximum_fusion.8), channel_id=1, source_target_pairs={{0,8},{1,9},{2,10},{3,11},{4,12},{5,13},{6,14},{7,15},{8,16},{9,17... | collective-permute-start | bytes 990728 | tf_op jit(solution)/shard_map/ppermute | solution.py:25
  77.6 10.5 %collective-permute-start.3 = (f32[1,645,128]{2,1,0:T(8,128)S(1)}, f32[1,645,128]{2,1,0:T(8,128)S(1)}, u32[]{:S(2)}, u32[]{:S(2)}) collective-permute-start(f32[1,645,128]{2,1,0:T(8,128)S(1)} %pad_maximum_fusion.4), channel_id=1, source_target_pairs={{8,0},{9,1},{10,2},{11,3},{12,4},{13,5},{14,6},{15,7},{16,8},{17,9... | collective-permute-start | bytes 990728 | tf_op jit(solution)/shard_map/ppermute | solution.py:25
  79.8 13.5 %collective-permute-start.11 = (f32[1,645,128]{2,1,0:T(8,128)S(1)}, f32[1,645,128]{2,1,0:T(8,128)S(1)}, u32[]{:S(2)}, u32[]{:S(2)}) collective-permute-start(f32[1,645,128]{2,1,0:T(8,128)S(1)} %pad_maximum_fusion.9), channel_id=1, source_target_pairs={{0,16},{1,17},{2,18},{3,19},{4,20},{5,21},{6,22},{7,23},{8,24},{9,... | collective-permute-start | bytes 990728 | tf_op jit(solution)/shard_map/ppermute | solution.py:25
  88.3 11.1 %collective-permute-start.4 = (f32[1,645,128]{2,1,0:T(8,128)S(1)}, f32[1,645,128]{2,1,0:T(8,128)S(1)}, u32[]{:S(2)}, u32[]{:S(2)}) collective-permute-start(f32[1,645,128]{2,1,0:T(8,128)S(1)} %pad_maximum_fusion.5), channel_id=1, source_target_pairs={{16,0},{17,1},{18,2},{19,3},{20,4},{21,5},{22,6},{23,7},{24,8},{25... | collective-permute-start | bytes 990728 | tf_op jit(solution)/shard_map/ppermute | solution.py:25
  107.4 34.0 %collective-permute-start.6 = (bf16[2,5,128,128]{3,1,2,0:T(8,128)(2,1)S(1)}, bf16[2,5,128,128]{3,1,2,0:T(8,128)(2,1)S(1)}, u32[]{:S(2)}, u32[]{:S(2)}) collective-permute-start(bf16[2,5,128,128]{3,1,2,0:T(8,128)(2,1)S(1)} %convolution_convert_fusion.2), channel_id=1, source_target_pairs={{32,0},{64,32},{96,64},{128,96},{160,128},{192,160},{224,192},{256... | collective-permute-start | bytes 983048 | tf_op jit(solution)/shard_map/ppermute | solution.py:42

commit v2 on v0

--- a/solution.py
+++ b/solution.py
@@ -2,24 +2,8 @@
 import jax.numpy as jnp
 from jax import lax
 from jax.sharding import PartitionSpec as P
-
-
-def carried_in(value, axis, combine, identity, reverse):
-    length, place = (lax.axis_size(axis), lax.axis_index(axis))
-    everything = jax.tree.map(lambda part: lax.all_gather(part, axis), value)
-    start = jax.tree.map(
-        lambda part, zero: jnp.broadcast_to(jnp.asarray(zero, part.dtype), part.shape),
-        value,
-        identity,
-    )
-
-    def lap(k, before):
-        at = length - 1 - k if reverse else k
-        reached = at > place if reverse else at < place
-        new = combine(before, jax.tree.map(lambda part: part[at], everything))
-        return jax.tree.map(lambda a, b: jnp.where(reached, a, b), new, before)
-
-    return lax.fori_loop(0, length, lap, start)
+from jax.experimental import pallas as pl
+from jax.experimental.pallas import tpu as pltpu
 
 
 def from_behind(value, axis, steps):
@@ -70,50 +54,64 @@
     return (grads, returned)
 
 
-def affine_join(earlier, latter):
-    return (earlier[0] * latter[0], latter[0][..., None] * earlier[1] + latter[1])
+def recurrence_kernel(fresh_t, weights_t, decays_t):
+    col_total, part, channel_count = fresh_t.shape
+
+    def body(fresh_ref, weight_ref, decay_ref, grad_ref, gate_ref, state_ref):
+        state = jnp.zeros((part, channel_count), jnp.float32)
+        for column in range(col_total):
+            state = decay_ref[column] * state + fresh_ref[column]
+            state_ref[column] = state
+        carried = jnp.zeros((part, channel_count), jnp.float32)
+        for column in reversed(range(col_total)):
+            grad = weight_ref[column] + carried
+            grad_ref[column] = grad
+            if column > 0:
+                gate_ref[column] = jnp.sum(grad * state_ref[column - 1], axis=-1, keepdims=True)
+            else:
+                gate_ref[column] = jnp.zeros((part, 1), jnp.float32)
+            carried = decay_ref[column] * grad
+
+    return pl.pallas_call(
+        body,
+        out_shape=(
+            jax.ShapeDtypeStruct((col_total, part, channel_count), jnp.float32),
+            jax.ShapeDtypeStruct((col_total, part, 1), jnp.float32),
+        ),
+        scratch_shapes=[pltpu.VMEM((col_total, part, channel_count), jnp.float32)],
+    )(fresh_t, weights_t, decays_t)
 
 
 def chain_scan(fresh, decay_rows, cotangent):
     row_count, col_count, flat_rows, channel_count = fresh.shape
-    identity = (
-        jnp.ones((row_count, flat_rows), jnp.float32),
-        jnp.zeros((row_count, flat_rows, channel_count), jnp.float32),
+    count = lax.axis_size("col")
+    rows = row_count * flat_rows
+    part = rows // count
+    assert part * count == rows and part <= channel_count
+    col_total = count * col_count
+
+    def by_column(value):
+        return jnp.swapaxes(value, 0, 1).reshape(col_count, count, part, -1)
+
+    decay_lane = jnp.pad(
+        by_column(decay_rows).reshape(col_count, count, 1, part),
+        ((0, 0), (0, 0), (0, 0), (0, channel_count - part)),
     )
-    states_now = identity[1]
-    passed = identity[0]
-    local_states = []
-    reach_decay = []
-    for column in range(col_count):
-        states_now = decay_rows[:, column, :, None] * states_now + fresh[:, column]
-        passed = passed * decay_rows[:, column]
-        local_states.append(states_now)
-        reach_decay.append(passed)
-    entering = carried_in((passed, states_now), "col", affine_join, identity, False)
-    full_states = [
-        local_states[column] + reach_decay[column][..., None] * entering[1]
-        for column in range(col_count)
-    ]
-    before_states = [entering[1]] + full_states[:-1]
-    carried = identity[1]
-    tail_decay = identity[0]
-    local_grads = [None] * col_count
-    tail_list = [None] * col_count
-    for column in reversed(range(col_count)):
-        local_grads[column] = cotangent[:, column] + carried
-        tail_list[column] = tail_decay
-        carried = decay_rows[:, column, :, None] * local_grads[column]
-        tail_decay = tail_decay * decay_rows[:, column]
-    arriving = carried_in((tail_decay, carried), "col", affine_join, identity, True)
-    full_grads = [
-        local_grads[column] + tail_list[column][..., None] * arriving[1]
-        for column in range(col_count)
-    ]
-    condition_derivative = jnp.stack(full_grads, 1)
-    gate_grad = jnp.stack(
-        [jnp.sum(full_grads[column] * before_states[column], -1) for column in range(col_count)], 1
+    payload = jnp.concatenate([by_column(fresh), by_column(cotangent), decay_lane], 2)
+    payload = jnp.swapaxes(payload, 0, 1)
+    got = lax.all_to_all(payload, "col", 0, 0, tiled=True)
+    got = got.reshape(col_total, 2 * part + 1, channel_count)
+    grad_t, gate_t = recurrence_kernel(
+        got[:, :part], got[:, part : 2 * part], got[:, 2 * part, :part][..., None]
     )
-    return (condition_derivative, gate_grad)
+    gate_lane = jnp.pad(
+        gate_t.reshape(col_total, 1, part), ((0, 0), (0, 0), (0, channel_count - part))
+    )
+    back = jnp.concatenate([grad_t, gate_lane], 1).reshape(count, col_count, part + 1, channel_count)
+    ret = lax.all_to_all(back, "col", 0, 0, tiled=True)
+    grads = jnp.swapaxes(ret[:, :, :part], 0, 1).reshape(col_count, row_count, flat_rows, channel_count)
+    gates = jnp.swapaxes(ret[:, :, part, :part], 0, 1).reshape(col_count, row_count, flat_rows)
+    return (jnp.swapaxes(grads, 0, 1), jnp.swapaxes(gates, 0, 1))
 
 
 def local(blocks, sources, targets, counts, environment, top_boundary, decays, weights):

time: 329 us -> 120 us (0.36)
  the two profiles are of different devices: /device:TPU:1 before, /device:TPU:17 now
where the time goes in v2:
time: 120 us; the launch traced here: 119 us
  blocking collectives  69.4 us (58%)
  local copies, waits for them, and re-layouts  14.9 us (12%)
  starting transfers between devices  10.9 us (9%)
  Pallas kernels  8.23 us (7%)
  waiting for transfers between devices  7.72 us (6%)
  matrix products  5.99 us (5%)
  other arithmetic  1.4 us (1%)
    all_to_all x1, blocking collectives, chain_scan(): got = lax.all_to_all(payload, 'col', 0, 0, tiled=True)  44.5 us
    all_to_all x1, blocking collectives, chain_scan(): ret = lax.all_to_all(back, 'col', 0, 0, tiled=True)  24.9 us
    ppermute x2, starting transfers between devices, from_behind(): lax.ppermute(value, axis, [(source, source + steps) for source in range(i...  10.9 us
    pallas_call x1, Pallas kernels, recurrence_kernel(): pl.pallas_call(body, out_shape=(jax.ShapeDtypeStruct((col_total, part, ch...  8.23 us
    ppermute x2, waiting for transfers between devices, from_behind(): lax.ppermute(value, axis, [(source, source + steps) for source in range(i...  7.72 us
    unnamed x22, local copies, waits for them, and re-layouts  6.17 us
  transfers between devices with their start and end apart: 2, of which 2 were waited for; matrix products, arithmetic and copies ran while one was open for 5% of the time, Pallas kernels for 0%

profile of v2, /device:TPU:17, one launch (start us, length us, event | category | flops | bytes accessed | tf_op | source)
XLA Modules:
  0.0 119.4 jit_solution(2102516638519301460)
XLA Ops:
  0.6 0.0 copy-start
  0.6 0.0 copy-start.8
  0.7 0.0 copy-start.4
  0.7 0.0 copy-start.7
  0.7 3.9 %collective-permute-start = (bf16[2,5,128,128]{3,2,1,0:T(8,128)(2,1)}, bf16[2,5,128,128]{3,2,1,0:T(8,128)(2,1)S(1)}, u32[]{:S(2)}, u32[]{:S(2)}) collective-permute-start(bf16[2,5,128,128]{3,2,1,0:T(8,128)(2,1)} %bitcast.65), channel_id=1, source_target_pairs={{0,32},{32,64},{64,96},{96,128},{128,160},{160,192},{192,224},{224... | collective-permute-start | bytes 983048 | tf_op jit(solution)/shard_map/ppermute | solution.py:12
  4.6 0.7 copy.75
  5.3 0.1 reshape_reshape_transpose_reshape.3
  5.4 2.4 %copy.74 = f32[1,2,5,128,128]{4,1,3,2,0:T(2,128)} copy(f32[1,2,5,128,128]{4,3,2,1,0:T(8,128)} %param.15) | data formatting | bytes 1310720 | tf_op args[7]
  7.9 0.0 copy-done.8
  7.9 0.1 fusion.28
  7.9 1.0 collective-permute-done
  8.9 0.0 copy-done.4
  8.9 0.4 convolution_convert_fusion.1
  9.3 0.5 convolution_bitcast_fusion.1
  9.9 0.4 copy.71
  10.3 0.0 copy-start.5
  10.3 0.3 copy-done.6
  10.5 0.6 fusion.16
  11.1 0.1 copy-done.5
  11.2 0.1 bitcast_add_fusion
  11.4 0.5 copy.73
  11.9 0.4 copy-done.2
  12.3 0.6 fusion.1
  12.9 44.5 %all_to_all.10 = f32[32,2,41,128]{3,1,2,0:T(2,128)S(1)} all-to-all(f32[32,2,41,128]{3,1,2,0:T(2,128)S(1)} %fusion.1), channel_id=1, replica_groups=mesh['row'=16,'col'=32] {'col'}, dimensions={0} | all-to-all | bytes 2686976 | tf_op jit(solution)/shard_map/all_to_all | solution.py:102
  57.4 0.2 copy.77
  57.7 1.3 %fusion.29 = (f32[64,20,128]{2,1,0:T(8,128)}, f32[64,20,128]{2,1,0:T(8,128)}) fusion(f32[64,41,128]{2,1,0:T(8,128)S(1)} %bitcast.59), kind=kLoop, calls=%fused_computation.42 | loop fusion | bytes 2621440 | tf_op jit(solution)/shard_map/slice | solution.py:105
  58.9 1.4 %copy.79.decay_ref = f32[64,20,1]{2,1,0:T(8,128)} copy(f32[64,20,1]{1,0,2:T(8,128)S(1)} %bitcast.66) | data formatting | bytes 10240 | tf_op jit(solution)/shard_map/broadcast_in_dim;squeeze | solution.py:105
  60.3 8.2 %shard_map.103 = (f32[64,20,128]{2,1,0:T(8,128)}, f32[64,20,1]{2,1,0:T(8,128)}) custom-call(f32[64,20,128]{2,1,0:T(8,128)} %get-tuple-element.20.fresh_ref, f32[64,20,128]{2,1,0:T(8,128)} %get-tuple-element.19.weight_ref, f32[64,20,1]{2,1,0:T(8,128)} %copy.79.decay_ref), custom_call_target="tpu_custom_call" | custom-call | tf_op jit(solution)/shard_map/pallas_call | solution.py:75
  68.5 1.5 %copy.80 = f32[64,20,1]{0,2,1:T(1,128)S(1)} copy(f32[64,20,1]{2,1,0:T(8,128)} %get-tuple-element.6) | data formatting | bytes 10240 | tf_op jit(solution)/shard_map/pallas_call | solution.py:75
  70.0 0.1 copy.81
  70.1 0.0 copy-done.3
  70.1 0.1 select_maximum_fusion
  70.2 0.4 copy.82
  70.6 24.9 %all_to_all.11 = f32[32,2,21,128]{3,1,2,0:T(2,128)S(1)} all-to-all(f32[32,2,21,128]{3,1,2,0:T(2,128)S(1)} %copy.82), channel_id=1, replica_groups=mesh['row'=16,'col'=32] {'col'}, dimensions={0} | all-to-all | bytes 1376256 | tf_op jit(solution)/shard_map/all_to_all | solution.py:111
  95.5 0.8 copy-done.1
  96.3 0.5 convolution_convert_fusion
  96.9 0.4 copy.87
  97.3 1.3 %convolution_bitcast_fusion = f32[2,8,128,128]{2,3,1,0:T(8,128)} fusion(bf16[2,8,128,128]{2,3,1,0:T(8,128)(2,1)S(1)} %copy.87, bf16[1,2,8,128,128]{4,3,2,1,0:T(8,128)(2,1)S(1)} %copy-done), kind=kOutput, calls=%fused_computation.1 | convolution fusion | flops 67108864 | bytes 2097152 | tf_op jit(solution)/shard_map/rckab,rckaj->rckbj/dot_general | solution.py:50
  98.5 1.6 %copy.88 = f32[2,8,128,128]{3,1,2,0:T(8,128)S(1)} copy(f32[2,8,128,128]{2,3,1,0:T(8,128)} %convolution_bitcast_fusion) | data formatting | bytes 2097152 | tf_op jit(solution)/shard_map/rckab,rckaj->rckbj/dot_general | solution.py:50
  100.2 1.4 %convolution_convert_fusion.2 = bf16[2,5,128,128]{3,1,2,0:T(8,128)(2,1)} fusion(f32[2,8,128,128]{3,1,2,0:T(8,128)S(1)} %copy.88, s32[2,8]{1,0:T(2,128)S(1)} %bitcast.71, pred[2,8]{1,0:T(4,128)(4,1)S(1)} %get-tuple-element.22), kind=kOutput, calls=%fused_computation.9 | convolution fusion | flops 15892640 | bytes 1376336 | tf_op jit(solution)/shard_map/rckn,rckbj->rcnbj/dot_general | solution.py:51
  101.6 7.0 %collective-permute-start.1 = (bf16[2,5,128,128]{3,1,2,0:T(8,128)(2,1)}, bf16[2,5,128,128]{3,1,2,0:T(8,128)(2,1)S(1)}, u32[]{:S(2)}, u32[]{:S(2)}) collective-permute-start(bf16[2,5,128,128]{3,1,2,0:T(8,128)(2,1)} %convolution_convert_fusion.2), channel_id=1, source_target_pairs={{32,0},{64,32},{96,64},{128,96},{160,128},{192,160},{224,192},{256... | collective-permute-start | bytes 983048 | tf_op jit(solution)/shard_map/ppermute | solution.py:12
  108.6 0.8 slice_bitcast_fusion
  109.3 0.1 reshape_transpose_reshape.15
  109.5 0.6 copy.92
  110.1 1.3 %fusion.3 = bf16[1,2,8,128,128]{4,3,2,1,0:T(8,128)(2,1)} fusion(bf16[2,8,128,128]{2,3,1,0:T(8,128)(2,1)S(1)} %copy.87, f32[2,8]{1,0:T(2,128)S(1)} %get-tuple-element.21, bf16[2,8,128,128]{3,1,2,0:T(8,128)(2,1)S(1)} %convolution_convert_fusion.1), kind=kOutput, calls=%fused_computation.10 | convolution fusion | flops 67633152 | bytes 1572928 | tf_op jit(solution)/shard_map/rckaj,rckbj->rckab/dot_general | solution.py:47
  111.3 6.8 %collective-permute-done.1 = bf16[2,5,128,128]{3,1,2,0:T(8,128)(2,1)S(1)} collective-permute-done((bf16[2,5,128,128]{3,1,2,0:T(8,128)(2,1)}, bf16[2,5,128,128]{3,1,2,0:T(8,128)(2,1)S(1)}, u32[]{:S(2)}, u32[]{:S(2)}) %collective-permute-start.1) | collective-permute-done | bytes 327712 | tf_op jit(solution)/shard_map/ppermute | solution.py:12
  118.1 0.5 fusion.5
  118.6 0.8 copy.91
  (11 shorter events, 0.1 us)
Async XLA Ops:
  0.6 8.7 %copy-start = (bf16[1,2,8,128,128]{4,3,2,1,0:T(8,128)(2,1)S(1)}, bf16[1,2,8,128,128]{4,3,2,1,0:T(8,128)(2,1)}, u32[]{:S(2)}) copy-start(bf16[1,2,8,128,128]{4,3,2,1,0:T(8,128)(2,1)} %param.8) | copy-start | bytes 1572868
  0.6 7.2 %copy-start.8 = (s32[1,2]{1,0:T(1,128)S(1)}, s32[1,2]{1,0:T(1,128)}, u32[]{:S(2)}) copy-start(s32[1,2]{1,0:T(1,128)} %param.11) | copy-start | bytes 28
  0.7 8.2 %copy-start.4 = (bf16[2,5,128,128]{3,2,1,0:T(8,128)(2,1)S(1)}, bf16[2,5,128,128]{3,2,1,0:T(8,128)(2,1)}, u32[]{:S(2)}) copy-start(bf16[2,5,128,128]{3,2,1,0:T(8,128)(2,1)} %param.13) | copy-start | bytes 983044
  0.7 8.3 %copy-start.7 = (s32[1,2,8]{2,1,0:T(2,128)S(1)}, s32[1,2,8]{2,1,0:T(2,128)}, u32[]{:S(2)}) copy-start(s32[1,2,8]{2,1,0:T(2,128)} %param.9) | copy-start | bytes 196
  0.7 8.2 %collective-permute-start = (bf16[2,5,128,128]{3,2,1,0:T(8,128)(2,1)}, bf16[2,5,128,128]{3,2,1,0:T(8,128)(2,1)S(1)}, u32[]{:S(2)}, u32[]{:S(2)}) collective-permute-start(bf16[2,5,128,128]{3,2,1,0:T(8,128)(2,1)} %bitcast.65), channel_id=1, source_target_pairs={{0,32},{32,64},{64,96},{96,128},{128,160},{160,192},{192,224},{224... | collective-permute-start | bytes 983048 | tf_op jit(solution)/shard_map/ppermute | solution.py:12
  9.9 0.7 copy-start.6
  10.3 1.0 copy-start.5
  11.2 1.1 copy-start.2
  68.5 1.6 %copy-start.3 = (f32[64,20,128]{2,1,0:T(8,128)S(1)}, f32[64,20,128]{2,1,0:T(8,128)}, u32[]{:S(2)}) copy-start(f32[64,20,128]{2,1,0:T(8,128)} %get-tuple-element.5) | copy-start | bytes 1966084
  95.4 0.9 copy-start.1
  101.6 16.6 %collective-permute-start.1 = (bf16[2,5,128,128]{3,1,2,0:T(8,128)(2,1)}, bf16[2,5,128,128]{3,1,2,0:T(8,128)(2,1)S(1)}, u32[]{:S(2)}, u32[]{:S(2)}) collective-permute-start(bf16[2,5,128,128]{3,1,2,0:T(8,128)(2,1)} %convolution_convert_fusion.2), channel_id=1, source_target_pairs={{32,0},{64,32},{96,64},{128,96},{160,128},{192,160},{224,192},{256... | collective-permute-start | bytes 983048 | tf_op jit(solution)/shard_map/ppermute | solution.py:12

commit v3 on v0

--- a/solution.py
+++ b/solution.py
@@ -2,24 +2,8 @@
 import jax.numpy as jnp
 from jax import lax
 from jax.sharding import PartitionSpec as P
-
-
-def carried_in(value, axis, combine, identity, reverse):
-    length, place = (lax.axis_size(axis), lax.axis_index(axis))
-    everything = jax.tree.map(lambda part: lax.all_gather(part, axis), value)
-    start = jax.tree.map(
-        lambda part, zero: jnp.broadcast_to(jnp.asarray(zero, part.dtype), part.shape),
-        value,
-        identity,
-    )
-
-    def lap(k, before):
-        at = length - 1 - k if reverse else k
-        reached = at > place if reverse else at < place
-        new = combine(before, jax.tree.map(lambda part: part[at], everything))
-        return jax.tree.map(lambda a, b: jnp.where(reached, a, b), new, before)
-
-    return lax.fori_loop(0, length, lap, start)
+from jax.experimental import pallas as pl
+from jax.experimental.pallas import tpu as pltpu
 
 
 def from_behind(value, axis, steps):
@@ -70,8 +54,49 @@
     return (grads, returned)
 
 
-def affine_join(earlier, latter):
-    return (earlier[0] * latter[0], latter[0][..., None] * earlier[1] + latter[1])
+def carry_kernel(fwd_b, bwd_b, fwd_a, bwd_a):
+    count, part, channel_count = fwd_b.shape
+
+    def body(fwd_b_ref, bwd_b_ref, fwd_a_ref, bwd_a_ref, out_ref):
+        state = jnp.zeros((part, channel_count), jnp.float32)
+        for source in range(count):
+            out_ref[source, 0] = state
+            state = fwd_a_ref[source] * state + fwd_b_ref[source]
+        state = jnp.zeros((part, channel_count), jnp.float32)
+        for source in reversed(range(count)):
+            out_ref[source, 1] = state
+            state = bwd_a_ref[source] * state + bwd_b_ref[source]
+
+    return pl.pallas_call(
+        body,
+        out_shape=jax.ShapeDtypeStruct((count, 2, part, channel_count), jnp.float32),
+    )(fwd_b, bwd_b, fwd_a, bwd_a)
+
+
+def carry_exchange(fwd_a, fwd_b, bwd_a, bwd_b):
+    row_count, flat_rows, channel_count = fwd_b.shape
+    count = lax.axis_size("col")
+    rows = row_count * flat_rows
+    part = rows // count
+    assert part * count == rows and 2 * part <= channel_count
+    factors = jnp.concatenate(
+        [fwd_a.reshape(count, 1, part), bwd_a.reshape(count, 1, part)], 2
+    )
+    factors = jnp.pad(factors, ((0, 0), (0, 0), (0, channel_count - 2 * part)))
+    payload = jnp.concatenate(
+        [fwd_b.reshape(count, part, channel_count), bwd_b.reshape(count, part, channel_count), factors], 1
+    )
+    got = lax.all_to_all(payload, "col", 0, 0, tiled=True)
+    carries = carry_kernel(
+        got[:, :part],
+        got[:, part : 2 * part],
+        got[:, 2 * part, :part][..., None],
+        got[:, 2 * part, part : 2 * part][..., None],
+    )
+    ret = lax.all_to_all(carries, "col", 0, 0, tiled=True)
+    entering = ret[:, 0].reshape(row_count, flat_rows, channel_count)
+    arriving = ret[:, 1].reshape(row_count, flat_rows, channel_count)
+    return (entering, arriving)
 
 
 def chain_scan(fresh, decay_rows, cotangent):
@@ -89,12 +114,6 @@
         passed = passed * decay_rows[:, column]
         local_states.append(states_now)
         reach_decay.append(passed)
-    entering = carried_in((passed, states_now), "col", affine_join, identity, False)
-    full_states = [
-        local_states[column] + reach_decay[column][..., None] * entering[1]
-        for column in range(col_count)
-    ]
-    before_states = [entering[1]] + full_states[:-1]
     carried = identity[1]
     tail_decay = identity[0]
     local_grads = [None] * col_count
@@ -104,9 +123,14 @@
         tail_list[column] = tail_decay
         carried = decay_rows[:, column, :, None] * local_grads[column]
         tail_decay = tail_decay * decay_rows[:, column]
-    arriving = carried_in((tail_decay, carried), "col", affine_join, identity, True)
+    entering, arriving = carry_exchange(passed, states_now, tail_decay, carried)
+    full_states = [
+        local_states[column] + reach_decay[column][..., None] * entering
+        for column in range(col_count)
+    ]
+    before_states = [entering] + full_states[:-1]
     full_grads = [
-        local_grads[column] + tail_list[column][..., None] * arriving[1]
+        local_grads[column] + tail_list[column][..., None] * arriving
         for column in range(col_count)
     ]
     condition_derivative = jnp.stack(full_grads, 1)

time: 329 us -> 120 us (0.36)
  the two profiles are of different devices: /device:TPU:1 before, /device:TPU:17 now
where the time goes in v3:
time: 120 us; the launch traced here: 119 us
  blocking collectives  32.4 us (27%)
  waiting for transfers between devices  23.8 us (20%)
  local copies, waits for them, and re-layouts  20.2 us (17%)
  starting transfers between devices  18.4 us (15%)
  other arithmetic  12.9 us (11%)
  matrix products  7.96 us (7%)
  Pallas kernels  2.52 us (2%)
    all_to_all x1, blocking collectives, carry_exchange(): got = lax.all_to_all(payload, 'col', 0, 0, tiled=True)  32.4 us
    all_to_all x1, waiting for transfers between devices, carry_exchange(): ret = lax.all_to_all(carries, 'col', 0, 0, tiled=True)  16.9 us
    ppermute x2, starting transfers between devices, from_behind(): lax.ppermute(value, axis, [(source, source + steps) for source in range(i...  10.5 us
    reduce_sum x2, other arithmetic, chain_scan(): jnp.sum(full_grads[column] * before_states[column], -1)  10.2 us
    all_to_all x1, starting transfers between devices, carry_exchange(): ret = lax.all_to_all(carries, 'col', 0, 0, tiled=True)  7.94 us
    unnamed x39, local copies, waits for them, and re-layouts  7.07 us
    ppermute x2, waiting for transfers between devices, from_behind(): lax.ppermute(value, axis, [(source, source + steps) for source in range(i...  6.85 us
    dot_general x1, matrix products, backward_blocks(): jnp.einsum('rckn,rckbj->rcnbj', taken, contrib, precision=lax.Precision.H...  2.75 us
  transfers between devices with their start and end apart: 3, of which 2 were waited for; matrix products, arithmetic and copies ran while one was open for 5% of the time, Pallas kernels for 0%

profile of v3, /device:TPU:17, one launch (start us, length us, event | category | flops | bytes accessed | tf_op | source)
XLA Modules:
  0.0 119.2 jit_solution(3675401545748416175)
XLA Ops:
  0.6 3.9 %collective-permute-start = (bf16[2,5,128,128]{3,2,1,0:T(8,128)(2,1)}, bf16[2,5,128,128]{3,2,1,0:T(8,128)(2,1)S(1)}, u32[]{:S(2)}, u32[]{:S(2)}) collective-permute-start(bf16[2,5,128,128]{3,2,1,0:T(8,128)(2,1)} %bitcast.97), channel_id=1, source_target_pairs={{0,32},{32,64},{64,96},{96,128},{128,160},{160,192},{192,224},{224... | collective-permute-start | bytes 983048 | tf_op jit(solution)/shard_map/ppermute | solution.py:12
  4.6 0.7 copy-done.17
  5.2 0.6 fusion.30
  5.9 0.1 mul.156
  6.0 1.1 fusion.34
  7.1 0.8 squeeze.31
  8.0 0.8 squeeze.32
  8.8 0.1 mul.164
  8.9 0.1 fusion.12
  9.1 0.7 copy-done.14
  9.8 0.4 convolution_convert_fusion.1
  10.2 0.5 convolution_bitcast_fusion.1
  10.7 0.4 copy.108
  11.1 0.7 copy-done.15
  11.8 0.6 fusion.18
  12.4 0.4 copy-done.12
  12.8 0.1 bitcast_add_fusion
  13.0 0.8 copy-done.2
  13.8 0.9 copy-done.9
  14.8 0.1 copy-done.8
  14.9 0.4 multiply_add_fusion
  15.4 32.4 %all_to_all.10 = f32[32,41,128]{2,1,0:T(8,128)S(1)} all-to-all(f32[32,41,128]{2,1,0:T(8,128)S(1)} %pad_maximum_fusion), channel_id=1, replica_groups=mesh['row'=16,'col'=32] {'col'}, dimensions={0} | all-to-all | bytes 1343488 | tf_op jit(solution)/shard_map/all_to_all | solution.py:89
  47.9 1.1 copy.114.fwd_a_ref
  49.0 1.1 copy.115.bwd_a_ref
  50.0 0.9 fusion.32
  50.9 2.5 %shard_map.103 = f32[32,2,20,128]{3,2,1,0:T(8,128)} custom-call(f32[32,20,128]{2,1,0:T(8,128)} %get-tuple-element.26.fwd_b_ref, f32[32,20,128]{2,1,0:T(8,128)} %get-tuple-element.25.bwd_b_ref, f32[32,20,1]{2,1,0:T(8,128)} %copy.114.fwd_a_ref, f32[32,20,1]{2,1,0:T(8,128)} %copy.115.bwd_a_ref), custom_call_target="tpu_custom_call" | custom-call | tf_op jit(solution)/shard_map/pallas_call | solution.py:70
  53.5 2.3 %copy.116 = f32[32,2,20,128]{3,1,2,0:T(2,128)} copy(f32[32,2,20,128]{3,2,1,0:T(8,128)} %shard_map.103) | data formatting | bytes 1310720 | tf_op jit(solution)/shard_map/pallas_call | solution.py:70
  55.8 7.9 %all-to-all-start.1 = ((f32[32,2,20,128]{3,1,2,0:T(2,128)}), f32[32,2,20,128]{3,1,2,0:T(2,128)S(1)}, u32[]{:S(2)}, u32[]{:S(2)}) async-start(f32[32,2,20,128]{3,1,2,0:T(2,128)} %copy.116), calls=%async_computation.1 | async-start | bytes 1310720 | tf_op jit(solution)/shard_map/all_to_all | solution.py:96
  63.7 16.9 %all-to-all-done.1 = f32[32,2,20,128]{3,1,2,0:T(2,128)S(1)} async-done(((f32[32,2,20,128]{3,1,2,0:T(2,128)}), f32[32,2,20,128]{3,1,2,0:T(2,128)S(1)}, u32[]{:S(2)}, u32[]{:S(2)}) %all-to-all-start.1) | async-done | bytes 655392 | tf_op jit(solution)/shard_map/all_to_all | solution.py:96
  80.7 9.8 %multiply_reduce_fusion = (f32[32,20]{1,0:T(8,128)S(1)}, f32[32,1,20,128]{3,1,2,0:T(1,128)}, f32[32,1,20,128]{3,1,2,0:T(1,128)S(1)}) fusion(f32[32,1,20,128]{3,1,2,0:T(1,128)S(1)} %bitcast.91, f32[32,1,20,128]{3,1,2,0:T(1,128)S(1)} %bitcast.90, f32[32,20]{1,0:T(8,128)S(1)} %mul.154, f32[32,2,20,128]{3,1,2,0:T(2,128)S(1)} %all-to-all-done.1), kind=kLoop, calls=%fused_computation.27 | loop fusion | flops 490880 | bytes 1971200 | tf_op jit(solution)/shard_map/reduce_sum | solution.py:138
  90.5 0.2 slice_add_fusion
  90.6 0.6 copy-done.6
  91.2 0.2 copy_dynamic-update-slice_fusion.1
  91.4 0.2 copy_dynamic-update-slice_fusion
  91.6 1.1 convolution_convert_fusion
  92.8 1.4 %copy.124 = bf16[2,8,128,128]{2,3,1,0:T(8,128)(2,1)S(1)} copy(bf16[2,8,128,128]{3,1,2,0:T(8,128)(2,1)} %convolution_convert_fusion) | data formatting | bytes 1048576 | tf_op jit(solution)/shard_map/convert_element_type | solution.py:45
  94.2 1.3 %convolution_bitcast_fusion = f32[2,8,128,128]{2,3,1,0:T(8,128)} fusion(bf16[2,8,128,128]{2,3,1,0:T(8,128)(2,1)S(1)} %copy.124, bf16[1,2,8,128,128]{4,3,2,1,0:T(8,128)(2,1)S(1)} %copy-done), kind=kOutput, calls=%fused_computation | convolution fusion | flops 67108864 | bytes 2097152 | tf_op jit(solution)/shard_map/rckab,rckaj->rckbj/dot_general | solution.py:50
  95.5 2.5 %copy.125 = f32[2,8,128,128]{3,1,2,0:T(8,128)} copy(f32[2,8,128,128]{2,3,1,0:T(8,128)} %convolution_bitcast_fusion) | data formatting | bytes 2097152 | tf_op jit(solution)/shard_map/rckab,rckaj->rckbj/dot_general | solution.py:50
  98.0 2.8 %convolution_convert_fusion.2 = bf16[2,5,128,128]{3,1,2,0:T(8,128)(2,1)} fusion(f32[2,8,128,128]{3,1,2,0:T(8,128)} %copy.125, s32[2,8]{1,0:T(2,128)S(1)} %bitcast.104, pred[2,8]{1,0:T(4,128)(4,1)S(1)} %get-tuple-element.37), kind=kOutput, calls=%fused_computation.6 | convolution fusion | flops 15892640 | bytes 1376336 | tf_op jit(solution)/shard_map/rckn,rckbj->rcnbj/dot_general | solution.py:51
  100.8 6.6 %collective-permute-start.1 = (bf16[2,5,128,128]{3,1,2,0:T(8,128)(2,1)}, bf16[2,5,128,128]{3,1,2,0:T(8,128)(2,1)}, u32[]{:S(2)}, u32[]{:S(2)}) collective-permute-start(bf16[2,5,128,128]{3,1,2,0:T(8,128)(2,1)} %convolution_convert_fusion.2), channel_id=1, source_target_pairs={{32,0},{64,32},{96,64},{128,96},{160,128},{192,160},{224,192},{256... | collective-permute-start | bytes 983048 | tf_op jit(solution)/shard_map/ppermute | solution.py:12
  107.3 0.4 fusion.11
  107.7 0.1 stack.21
  107.8 0.6 copy.129
  108.4 0.6 copy-done.16
  109.1 1.3 %fusion.1 = bf16[1,2,8,128,128]{4,3,2,1,0:T(8,128)(2,1)} fusion(bf16[2,8,128,128]{2,3,1,0:T(8,128)(2,1)S(1)} %copy.124, f32[2,8]{1,0:T(2,128)S(1)} %copy-done.16, bf16[2,8,128,128]{3,1,2,0:T(8,128)(2,1)S(1)} %convolution_convert_fusion.1), kind=kOutput, calls=%fused_computation.7 | convolution fusion | flops 67633152 | bytes 1572928 | tf_op jit(solution)/shard_map/rckaj,rckbj->rckab/dot_general | solution.py:47
  110.3 6.8 %collective-permute-done.1 = bf16[2,5,128,128]{3,1,2,0:T(8,128)(2,1)} collective-permute-done((bf16[2,5,128,128]{3,1,2,0:T(8,128)(2,1)}, bf16[2,5,128,128]{3,1,2,0:T(8,128)(2,1)}, u32[]{:S(2)}, u32[]{:S(2)}) %collective-permute-start.1) | collective-permute-done | bytes 327712 | tf_op jit(solution)/shard_map/ppermute | solution.py:12
  117.2 1.2 fusion.2
  118.4 0.8 copy.128
  (39 shorter events, 0.5 us)
Async XLA Ops:
  0.6 9.6 %copy-start = (bf16[1,2,8,128,128]{4,3,2,1,0:T(8,128)(2,1)S(1)}, bf16[1,2,8,128,128]{4,3,2,1,0:T(8,128)(2,1)}, u32[]{:S(2)}) copy-start(bf16[1,2,8,128,128]{4,3,2,1,0:T(8,128)(2,1)} %param.8) | copy-start | bytes 1572868
  0.6 8.4 %collective-permute-start = (bf16[2,5,128,128]{3,2,1,0:T(8,128)(2,1)}, bf16[2,5,128,128]{3,2,1,0:T(8,128)(2,1)S(1)}, u32[]{:S(2)}, u32[]{:S(2)}) collective-permute-start(bf16[2,5,128,128]{3,2,1,0:T(8,128)(2,1)} %bitcast.97), channel_id=1, source_target_pairs={{0,32},{32,64},{64,96},{96,128},{128,160},{160,192},{192,224},{224... | collective-permute-start | bytes 983048 | tf_op jit(solution)/shard_map/ppermute | solution.py:12
  4.6 1.3 %copy-start.13 = (f32[1,2,5,128]{3,1,2,0:T(2,128)S(1)}, f32[1,2,5,128]{3,1,2,0:T(2,128)}, u32[]{:S(2)}) copy-start(f32[1,2,5,128]{3,1,2,0:T(2,128)} %param.14) | copy-start | bytes 15364
  4.6 0.7 copy-start.17
  7.1 0.9 copy-start.4
  8.0 1.1 copy-start.11
  9.1 0.7 copy-start.14
  11.1 0.7 copy-start.15
  11.8 1.0 copy-start.12
  12.9 0.8 copy-start.2
  13.8 1.0 copy-start.9
  13.8 1.1 copy-start.8
  55.8 24.9 %copy-start.5 = (f32[1,1,640,128]{3,2,1,0:T(8,128)S(1)}, f32[1,1,640,128]{3,2,1,0:T(8,128)}, u32[]{:S(2)}) copy-start(f32[1,1,640,128]{3,2,1,0:T(8,128)} %copy-done.4) | copy-start | bytes 983044
  55.8 24.9 %all-to-all-start.1 = ((f32[32,2,20,128]{3,1,2,0:T(2,128)}), f32[32,2,20,128]{3,1,2,0:T(2,128)S(1)}, u32[]{:S(2)}, u32[]{:S(2)}) async-start(f32[32,2,20,128]{3,1,2,0:T(2,128)} %copy.116), calls=%async_computation.1 | async-start | bytes 1310720 | tf_op jit(solution)/shard_map/all_to_all | solution.py:96
  80.7 9.8 %copy-start.1 = (f32[1,2,5,128,128]{4,3,2,1,0:T(8,128)S(1)}, f32[1,2,5,128,128]{4,3,2,1,0:T(8,128)}, u32[]{:S(2)}) copy-start(f32[1,2,5,128,128]{4,3,2,1,0:T(8,128)} %param.15) | copy-start | bytes 1966084
  90.5 0.8 copy-start.6
  98.0 9.3 %copy-start.3 = (f32[1,2,5,128,128]{4,3,2,1,0:T(8,128)S(1)}, f32[1,2,5,128,128]{4,3,2,1,0:T(8,128)}, u32[]{:S(2)}) copy-start(f32[1,2,5,128,128]{4,3,2,1,0:T(8,128)} %copy-done.2) | copy-start | bytes 1966084
  98.0 9.3 %copy-start.7 = (f32[32,1,20,128]{3,1,2,0:T(1,128)S(1)}, f32[32,1,20,128]{3,1,2,0:T(1,128)}, u32[]{:S(2)}) copy-start(f32[32,1,20,128]{3,1,2,0:T(1,128)} %copy-done.6) | copy-start | bytes 983044
  98.0 9.3 %copy-start.10 = (f32[32,1,20,128]{3,1,2,0:T(1,128)S(1)}, f32[32,1,20,128]{3,1,2,0:T(1,128)}, u32[]{:S(2)}) copy-start(f32[32,1,20,128]{3,1,2,0:T(1,128)} %get-tuple-element.28) | copy-start | bytes 983044
  100.8 16.4 %collective-permute-start.1 = (bf16[2,5,128,128]{3,1,2,0:T(8,128)(2,1)}, bf16[2,5,128,128]{3,1,2,0:T(8,128)(2,1)}, u32[]{:S(2)}, u32[]{:S(2)}) collective-permute-start(bf16[2,5,128,128]{3,1,2,0:T(8,128)(2,1)} %convolution_convert_fusion.2), channel_id=1, source_target_pairs={{32,0},{64,32},{96,64},{128,96},{160,128},{192,160},{224,192},{256... | collective-permute-start | bytes 983048 | tf_op jit(solution)/shard_map/ppermute | solution.py:12
  108.4 0.6 copy-start.16

commit v4 on v2

--- a/solution.py
+++ b/solution.py
@@ -54,32 +54,75 @@
     return (grads, returned)
 
 
-def recurrence_kernel(fresh_t, weights_t, decays_t):
-    col_total, part, channel_count = fresh_t.shape
+def carry_kernel(fwd_b, bwd_b, factor):
+    count, part, channel_count = fwd_b.shape
 
-    def body(fresh_ref, weight_ref, decay_ref, grad_ref, gate_ref, state_ref):
+    def body(fwd_b_ref, bwd_b_ref, factor_ref, out_ref):
         state = jnp.zeros((part, channel_count), jnp.float32)
-        for column in range(col_total):
-            state = decay_ref[column] * state + fresh_ref[column]
-            state_ref[column] = state
-        carried = jnp.zeros((part, channel_count), jnp.float32)
-        for column in reversed(range(col_total)):
-            grad = weight_ref[column] + carried
-            grad_ref[column] = grad
-            if column > 0:
-                gate_ref[column] = jnp.sum(grad * state_ref[column - 1], axis=-1, keepdims=True)
-            else:
-                gate_ref[column] = jnp.zeros((part, 1), jnp.float32)
-            carried = decay_ref[column] * grad
+        for source in range(count):
+            out_ref[source, 0] = state
+            state = factor_ref[source] * state + fwd_b_ref[source]
+        state = jnp.zeros((part, channel_count), jnp.float32)
+        for source in reversed(range(count)):
+            out_ref[source, 1] = state
+            state = factor_ref[source] * state + bwd_b_ref[source]
+
+    return pl.pallas_call(
+        body,
+        out_shape=jax.ShapeDtypeStruct((count, 2, part, channel_count), jnp.float32),
+    )(fwd_b, bwd_b, factor)
+
+
+def summary_kernel(fresh, cotangent, decay_col, factor_row, count):
+    col_count, rows, channel_count = fresh.shape
+    part = rows // count
+
+    def body(fresh_ref, weight_ref, decay_ref, factor_ref, out_ref):
+        for chunk in range(count):
+            span = pl.ds(chunk * part, part)
+            state = fresh_ref[0, span, :]
+            for column in range(1, col_count):
+                state = decay_ref[column, span, :] * state + fresh_ref[column, span, :]
+            grad = weight_ref[col_count - 1, span, :]
+            for column in reversed(range(col_count - 1)):
+                grad = weight_ref[column, span, :] + decay_ref[column + 1, span, :] * grad
+            grad = decay_ref[0, span, :] * grad
+            out_ref[chunk, pl.ds(0, part), :] = state
+            out_ref[chunk, pl.ds(part, part), :] = grad
+            out_ref[chunk, pl.ds(2 * part, 1), :] = factor_ref[pl.ds(chunk, 1), :]
+
+    return pl.pallas_call(
+        body,
+        out_shape=jax.ShapeDtypeStruct((count, 2 * part + 1, channel_count), jnp.float32),
+    )(fresh, cotangent, decay_col, factor_row)
+
+
+def fixup_kernel(fresh, cotangent, decay_col, carries):
+    col_count, rows, channel_count = fresh.shape
+    count, _, part, _ = carries.shape
+
+    def body(fresh_ref, weight_ref, decay_ref, carry_ref, grad_ref, gate_ref):
+        for chunk in range(count):
+            span = pl.ds(chunk * part, part)
+            grad = carry_ref[chunk, 1]
+            grads = [None] * col_count
+            for column in reversed(range(col_count)):
+                grad = weight_ref[column, span, :] + grad
+                grads[column] = grad
+                grad_ref[column, span, :] = grad
+                grad = decay_ref[column, span, :] * grad
+            state = carry_ref[chunk, 0]
+            for column in range(col_count):
+                gate_ref[column, span, :] = jnp.sum(grads[column] * state, axis=-1, keepdims=True)
+                state = decay_ref[column, span, :] * state + fresh_ref[column, span, :]
 
     return pl.pallas_call(
         body,
         out_shape=(
-            jax.ShapeDtypeStruct((col_total, part, channel_count), jnp.float32),
-            jax.ShapeDtypeStruct((col_total, part, 1), jnp.float32),
+            jax.ShapeDtypeStruct((col_count, rows, channel_count), jnp.float32),
+            jax.ShapeDtypeStruct((col_count, rows, 1), jnp.float32),
         ),
-        scratch_shapes=[pltpu.VMEM((col_total, part, channel_count), jnp.float32)],
-    )(fresh_t, weights_t, decays_t)
+    )(fresh, cotangent, decay_col, carries)
 
 
 def chain_scan(fresh, decay_rows, cotangent):
@@ -88,30 +131,23 @@
     rows = row_count * flat_rows
     part = rows // count
     assert part * count == rows and part <= channel_count
-    col_total = count * col_count
 
     def by_column(value):
-        return jnp.swapaxes(value, 0, 1).reshape(col_count, count, part, -1)
+        return jnp.swapaxes(value, 0, 1).reshape(col_count, rows, -1)
 
-    decay_lane = jnp.pad(
-        by_column(decay_rows).reshape(col_count, count, 1, part),
-        ((0, 0), (0, 0), (0, 0), (0, channel_count - part)),
-    )
-    payload = jnp.concatenate([by_column(fresh), by_column(cotangent), decay_lane], 2)
-    payload = jnp.swapaxes(payload, 0, 1)
+    fresh_c = by_column(fresh)
+    weight_c = by_column(cotangent)
+    decay_c = by_column(decay_rows[..., None])
+    factor = jnp.prod(jnp.swapaxes(decay_rows, 0, 1).reshape(col_count, count, part), 0)
+    factor_row = jnp.pad(factor, ((0, 0), (0, channel_count - part)))
+    payload = summary_kernel(fresh_c, weight_c, decay_c, factor_row, count)
     got = lax.all_to_all(payload, "col", 0, 0, tiled=True)
-    got = got.reshape(col_total, 2 * part + 1, channel_count)
-    grad_t, gate_t = recurrence_kernel(
-        got[:, :part], got[:, part : 2 * part], got[:, 2 * part, :part][..., None]
-    )
-    gate_lane = jnp.pad(
-        gate_t.reshape(col_total, 1, part), ((0, 0), (0, 0), (0, channel_count - part))
-    )
-    back = jnp.concatenate([grad_t, gate_lane], 1).reshape(count, col_count, part + 1, channel_count)
-    ret = lax.all_to_all(back, "col", 0, 0, tiled=True)
-    grads = jnp.swapaxes(ret[:, :, :part], 0, 1).reshape(col_count, row_count, flat_rows, channel_count)
-    gates = jnp.swapaxes(ret[:, :, part, :part], 0, 1).reshape(col_count, row_count, flat_rows)
-    return (jnp.swapaxes(grads, 0, 1), jnp.swapaxes(gates, 0, 1))
+    carries = carry_kernel(got[:, :part], got[:, part : 2 * part], got[:, 2 * part, :part][..., None])
+    ret = lax.all_to_all(carries, "col", 0, 0, tiled=True)
+    grads, gates = fixup_kernel(fresh_c, weight_c, decay_c, ret)
+    grads = jnp.swapaxes(grads.reshape(col_count, row_count, flat_rows, channel_count), 0, 1)
+    gates = jnp.swapaxes(gates.reshape(col_count, row_count, flat_rows), 0, 1)
+    return (grads, gates)
 
 
 def local(blocks, sources, targets, counts, environment, top_boundary, decays, weights):

time: 120 us -> 112 us (0.933)
  blocking collectives: 69.4 us -> 56.1 us
  Pallas kernels: 8.23 us -> 12.9 us
  local copies, waits for them, and re-layouts: 14.9 us -> 11.8 us
  waiting for transfers between devices: 7.72 us -> 9.63 us
    all_to_all x1, blocking collectives: 44.5 us -> 32.7 us  [chain_scan(): got = lax.all_to_all(payload, 'col', 0, 0, tiled=True)]
    pallas_call x1 -> x3, Pallas kernels: 8.23 us -> 12.9 us  [the longest x1 7.93 us: fixup_kernel(): pl.pallas_call(body, out_shape=(jax.ShapeDtypeStruct((col_count, rows, ch...]
    unnamed x22 -> x19, local copies, waits for them, and re-layouts: 6.17 us -> 3.18 us
    ppermute x2, waiting for transfers between devices: 7.72 us -> 9.63 us  [from_behind(): lax.ppermute(value, axis, [(source, source + steps) for source in range(i...]
    all_to_all x1, blocking collectives: 24.9 us -> 23.4 us  [chain_scan(): ret = lax.all_to_all(carries, 'col', 0, 0, tiled=True)]
  transfers between devices with their start and end apart: 2 -> 2, of which waited for: 2 -> 2; matrix products, arithmetic and copies ran while one was open for 5% -> 4% of each run, Pallas kernels for 0% -> 0%
where the time goes in v4:
time: 112 us
  blocking collectives  56.1 us (50%)
  Pallas kernels  12.9 us (12%)
  local copies, waits for them, and re-layouts  11.8 us (11%)
  starting transfers between devices  11.1 us (10%)
  waiting for transfers between devices  9.63 us (9%)
  matrix products  7.08 us (6%)
  other arithmetic  2.45 us (2%)
    all_to_all x1, blocking collectives, chain_scan(): got = lax.all_to_all(payload, 'col', 0, 0, tiled=True)  32.7 us
    all_to_all x1, blocking collectives, chain_scan(): ret = lax.all_to_all(carries, 'col', 0, 0, tiled=True)  23.4 us
    ppermute x2, starting transfers between devices, from_behind(): lax.ppermute(value, axis, [(source, source + steps) for source in range(i...  11.1 us
    ppermute x2, waiting for transfers between devices, from_behind(): lax.ppermute(value, axis, [(source, source + steps) for source in range(i...  9.63 us
    pallas_call x1, Pallas kernels, fixup_kernel(): pl.pallas_call(body, out_shape=(jax.ShapeDtypeStruct((col_count, rows, ch...  7.93 us
    unnamed x19, local copies, waits for them, and re-layouts  3.18 us
    pallas_call x1, Pallas kernels, summary_kernel(): pl.pallas_call(body, out_shape=jax.ShapeDtypeStruct((count, 2 * part + 1,...  2.64 us
    pallas_call x1, Pallas kernels, carry_kernel(): pl.pallas_call(body, out_shape=jax.ShapeDtypeStruct((count, 2, part, chan...  2.38 us
  transfers between devices with their start and end apart: 2, of which 2 were waited for; matrix products, arithmetic and copies ran while one was open for 4% of the time, Pallas kernels for 0%

profile of v4, /device:TPU:17, one launch (start us, length us, event | category | flops | bytes accessed | tf_op | source)
XLA Modules:
  0.0 111.8 jit_solution(15794252958981105631)
XLA Ops:
  0.6 0.0 copy-start
  0.6 0.0 copy-start.5
  0.7 3.9 %collective-permute-start = (bf16[2,5,128,128]{3,2,1,0:T(8,128)(2,1)}, bf16[2,5,128,128]{3,2,1,0:T(8,128)(2,1)S(1)}, u32[]{:S(2)}, u32[]{:S(2)}) collective-permute-start(bf16[2,5,128,128]{3,2,1,0:T(8,128)(2,1)} %bitcast.55), channel_id=1, source_target_pairs={{0,32},{32,64},{64,96},{96,128},{128,160},{160,192},{192,224},{224... | collective-permute-start | bytes 983048 | tf_op jit(solution)/shard_map/ppermute | solution.py:12
  4.6 0.0 copy-done.5
  4.6 0.1 reduce_prod.12
  4.7 0.0 copy-start.3
  4.7 1.1 copy.74.decay_ref
  5.8 0.6 pad.4.factor_ref
  6.4 0.0 copy-start.8
  6.4 0.7 copy-done.8
  7.1 0.1 fusion.26
  7.2 1.7 %collective-permute-done = bf16[2,5,128,128]{3,2,1,0:T(8,128)(2,1)S(1)} collective-permute-done((bf16[2,5,128,128]{3,2,1,0:T(8,128)(2,1)}, bf16[2,5,128,128]{3,2,1,0:T(8,128)(2,1)S(1)}, u32[]{:S(2)}, u32[]{:S(2)}) %collective-permute-start) | collective-permute-done | bytes 327712 | tf_op jit(solution)/shard_map/ppermute | solution.py:12
  8.9 0.0 copy-done.3
  8.9 0.0 copy-start.7
  8.9 0.7 copy-done.7
  9.6 0.4 convolution_convert_fusion.1
  10.0 0.0 copy-done
  10.0 0.5 convolution_bitcast_fusion.1
  10.5 0.4 copy.67
  10.9 0.0 copy-start.6
  10.9 0.7 copy-done.6
  11.6 0.0 copy-start.4
  11.6 0.6 fusion.14
  12.2 0.4 copy-done.4
  12.6 1.0 bitcast_add_fusion
  13.6 2.6 %shard_map.103 = f32[32,41,128]{2,1,0:T(8,128)} custom-call(f32[2,640,128]{2,1,0:T(8,128)} %bitcast.49, f32[2,640,128]{2,1,0:T(8,128)} %bitcast.51, f32[2,640,1]{2,1,0:T(8,128)} %copy.74.decay_ref, f32[32,128]{1,0:T(8,128)} %pad.4.factor_ref), custom_call_target="tpu_custom_call" | custom-call | tf_op jit(solution)/shard_map/pallas_call | solution.py:94
  16.2 32.7 %all_to_all.10 = f32[32,41,128]{2,1,0:T(8,128)S(1)} all-to-all(f32[32,41,128]{2,1,0:T(8,128)} %shard_map.103), channel_id=1, replica_groups=mesh['row'=16,'col'=32] {'col'}, dimensions={0} | all-to-all | bytes 1343488 | tf_op jit(solution)/shard_map/all_to_all | solution.py:144
  48.9 1.1 copy.72.factor_ref
  49.9 0.9 fusion.27
  50.9 2.4 %shard_map.104 = f32[32,2,20,128]{3,2,1,0:T(8,128)} custom-call(f32[32,20,128]{2,1,0:T(8,128)} %get-tuple-element.20.fwd_b_ref, f32[32,20,128]{2,1,0:T(8,128)} %get-tuple-element.19.bwd_b_ref, f32[32,20,1]{2,1,0:T(8,128)} %copy.72.factor_ref), custom_call_target="tpu_custom_call" | custom-call | tf_op jit(solution)/shard_map/pallas_call | solution.py:70
  53.2 1.5 %copy.73 = f32[32,2,20,128]{3,1,2,0:T(2,128)S(1)} copy(f32[32,2,20,128]{3,2,1,0:T(8,128)} %shard_map.104) | data formatting | bytes 1310720 | tf_op jit(solution)/shard_map/pallas_call | solution.py:70
  54.7 23.4 %all_to_all.11 = f32[32,2,20,128]{3,1,2,0:T(2,128)S(1)} all-to-all(f32[32,2,20,128]{3,1,2,0:T(2,128)S(1)} %copy.73), channel_id=1, replica_groups=mesh['row'=16,'col'=32] {'col'}, dimensions={0} | all-to-all | bytes 1310720 | tf_op jit(solution)/shard_map/all_to_all | solution.py:146
  78.1 1.0 copy.75.carry_ref
  79.1 7.9 %shard_map.105 = (f32[2,640,128]{2,1,0:T(8,128)}, f32[2,640,1]{2,1,0:T(8,128)}) custom-call(f32[2,640,128]{2,1,0:T(8,128)} %bitcast.50, f32[2,640,128]{2,1,0:T(8,128)} %bitcast.52, f32[2,640,1]{2,1,0:T(8,128)} %copy.74.decay_ref, f32[32,2,20,128]{3,2,1,0:T(8,128)} %copy.75.carry_ref), custom_call_target="tpu_custom_call" | custom-call | tf_op jit(solution)/shard_map/pallas_call | solution.py:119
  87.0 1.6 %convolution_convert_fusion = bf16[2,8,128,128]{3,1,2,0:T(8,128)(2,1)S(1)} fusion(f32[2,5,128,128]{3,2,1,0:T(8,128)} %bitcast.53, s32[2,8]{1,0:T(2,128)S(1)} %bitcast.60), kind=kOutput, calls=%fused_computation.3 | convolution fusion | flops 2883664 | bytes 1179712 | tf_op jit(solution)/shard_map/rckn,rcnaj->rckaj/dot_general | solution.py:43
  88.6 0.4 copy.80
  89.0 1.3 %convolution_bitcast_fusion = f32[2,8,128,128]{2,3,1,0:T(8,128)} fusion(bf16[2,8,128,128]{2,3,1,0:T(8,128)(2,1)S(1)} %copy.80, bf16[1,2,8,128,128]{4,3,2,1,0:T(8,128)(2,1)S(1)} %copy-done), kind=kOutput, calls=%fused_computation | convolution fusion | flops 67108864 | bytes 2097152 | tf_op jit(solution)/shard_map/rckab,rckaj->rckbj/dot_general | solution.py:50
  90.3 1.6 %copy.81 = f32[2,8,128,128]{3,1,2,0:T(8,128)S(1)} copy(f32[2,8,128,128]{2,3,1,0:T(8,128)} %convolution_bitcast_fusion) | data formatting | bytes 2097152 | tf_op jit(solution)/shard_map/rckab,rckaj->rckbj/dot_general | solution.py:50
  91.9 0.0 copy-start.2
  91.9 1.4 %convolution_convert_fusion.2 = bf16[2,5,128,128]{3,1,2,0:T(8,128)(2,1)} fusion(f32[2,8,128,128]{3,1,2,0:T(8,128)S(1)} %copy.81, s32[2,8]{1,0:T(2,128)S(1)} %bitcast.62, pred[2,8]{1,0:T(4,128)(4,1)S(1)} %get-tuple-element.22), kind=kOutput, calls=%fused_computation.6 | convolution fusion | flops 15892640 | bytes 1376336 | tf_op jit(solution)/shard_map/rckn,rckbj->rcnbj/dot_general | solution.py:51
  93.3 7.2 %collective-permute-start.1 = (bf16[2,5,128,128]{3,1,2,0:T(8,128)(2,1)}, bf16[2,5,128,128]{3,1,2,0:T(8,128)(2,1)S(1)}, u32[]{:S(2)}, u32[]{:S(2)}) collective-permute-start(bf16[2,5,128,128]{3,1,2,0:T(8,128)(2,1)} %convolution_convert_fusion.2), channel_id=1, source_target_pairs={{32,0},{64,32},{96,64},{128,96},{160,128},{192,160},{224,192},{256... | collective-permute-start | bytes 983048 | tf_op jit(solution)/shard_map/ppermute | solution.py:12
  100.5 0.0 copy-done.2
  100.5 0.8 reduce.1
  101.4 1.3 %fusion.1 = bf16[1,2,8,128,128]{4,3,2,1,0:T(8,128)(2,1)} fusion(bf16[2,8,128,128]{2,3,1,0:T(8,128)(2,1)S(1)} %copy.80, f32[2,8]{1,0:T(2,128)S(1)} %get-tuple-element.21, bf16[2,8,128,128]{3,1,2,0:T(8,128)(2,1)S(1)} %convolution_convert_fusion.1), kind=kOutput, calls=%fused_computation.7 | convolution fusion | flops 67633152 | bytes 1572928 | tf_op jit(solution)/shard_map/rckaj,rckbj->rckab/dot_general | solution.py:47
  102.6 7.9 %collective-permute-done.1 = bf16[2,5,128,128]{3,1,2,0:T(8,128)(2,1)S(1)} collective-permute-done((bf16[2,5,128,128]{3,1,2,0:T(8,128)(2,1)}, bf16[2,5,128,128]{3,1,2,0:T(8,128)(2,1)S(1)}, u32[]{:S(2)}, u32[]{:S(2)}) %collective-permute-start.1) | collective-permute-done | bytes 327712 | tf_op jit(solution)/shard_map/ppermute | solution.py:12
  110.6 0.0 copy-done.1
  110.6 0.5 fusion.3
  111.0 0.8 copy.83
  (4 shorter events, 0.1 us)
Async XLA Ops:
  0.6 9.4 %copy-start = (bf16[1,2,8,128,128]{4,3,2,1,0:T(8,128)(2,1)S(1)}, bf16[1,2,8,128,128]{4,3,2,1,0:T(8,128)(2,1)}, u32[]{:S(2)}) copy-start(bf16[1,2,8,128,128]{4,3,2,1,0:T(8,128)(2,1)} %param.8) | copy-start | bytes 1572868
  0.6 3.9 %copy-start.5 = (f32[1,2,5,128]{3,1,2,0:T(2,128)S(1)}, f32[1,2,5,128]{3,1,2,0:T(2,128)}, u32[]{:S(2)}) copy-start(f32[1,2,5,128]{3,1,2,0:T(2,128)} %param.14) | copy-start | bytes 15364
  0.7 8.2 %collective-permute-start = (bf16[2,5,128,128]{3,2,1,0:T(8,128)(2,1)}, bf16[2,5,128,128]{3,2,1,0:T(8,128)(2,1)S(1)}, u32[]{:S(2)}, u32[]{:S(2)}) collective-permute-start(bf16[2,5,128,128]{3,2,1,0:T(8,128)(2,1)} %bitcast.55), channel_id=1, source_target_pairs={{0,32},{32,64},{64,96},{96,128},{128,160},{160,192},{192,224},{224... | collective-permute-start | bytes 983048 | tf_op jit(solution)/shard_map/ppermute | solution.py:12
  4.7 4.2 %copy-start.3 = (bf16[2,5,128,128]{3,2,1,0:T(8,128)(2,1)S(1)}, bf16[2,5,128,128]{3,2,1,0:T(8,128)(2,1)}, u32[]{:S(2)}) copy-start(bf16[2,5,128,128]{3,2,1,0:T(8,128)(2,1)} %param.13) | copy-start | bytes 983044
  6.4 0.7 copy-start.8
  8.9 0.7 copy-start.7
  10.9 0.7 copy-start.6
  11.6 1.0 copy-start.4
  91.9 8.6 %copy-start.2 = (f32[2,640,1]{2,1,0:T(8,128)S(1)}, f32[2,640,1]{2,1,0:T(8,128)}, u32[]{:S(2)}) copy-start(f32[2,640,1]{2,1,0:T(8,128)} %get-tuple-element.6) | copy-start | bytes 15364
  93.3 17.2 %collective-permute-start.1 = (bf16[2,5,128,128]{3,1,2,0:T(8,128)(2,1)}, bf16[2,5,128,128]{3,1,2,0:T(8,128)(2,1)S(1)}, u32[]{:S(2)}, u32[]{:S(2)}) collective-permute-start(bf16[2,5,128,128]{3,1,2,0:T(8,128)(2,1)} %convolution_convert_fusion.2), channel_id=1, source_target_pairs={{32,0},{64,32},{96,64},{128,96},{160,128},{192,160},{224,192},{256... | collective-permute-start | bytes 983048 | tf_op jit(solution)/shard_map/ppermute | solution.py:12
  101.4 9.2 %copy-start.1 = (f32[2,640,128]{2,1,0:T(8,128)S(1)}, f32[2,640,128]{2,1,0:T(8,128)}, u32[]{:S(2)}) copy-start(f32[2,640,128]{2,1,0:T(8,128)} %get-tuple-element.5) | copy-start | bytes 1966084

commit v5 on v4

--- a/solution.py
+++ b/solution.py
@@ -89,11 +89,11 @@
             grad = decay_ref[0, span, :] * grad
             out_ref[chunk, pl.ds(0, part), :] = state
             out_ref[chunk, pl.ds(part, part), :] = grad
-            out_ref[chunk, pl.ds(2 * part, 1), :] = factor_ref[pl.ds(chunk, 1), :]
+            out_ref[chunk, pl.ds(2 * part, 2), :] = factor_ref[chunk]
 
     return pl.pallas_call(
         body,
-        out_shape=jax.ShapeDtypeStruct((count, 2 * part + 1, channel_count), jnp.float32),
+        out_shape=jax.ShapeDtypeStruct((count, 2 * part + 2, channel_count), jnp.float32),
     )(fresh, cotangent, decay_col, factor_row)
 
 
@@ -104,14 +104,14 @@
     def body(fresh_ref, weight_ref, decay_ref, carry_ref, grad_ref, gate_ref):
         for chunk in range(count):
             span = pl.ds(chunk * part, part)
-            grad = carry_ref[chunk, 1]
+            grad = carry_ref[chunk, 1].astype(jnp.float32)
             grads = [None] * col_count
             for column in reversed(range(col_count)):
                 grad = weight_ref[column, span, :] + grad
                 grads[column] = grad
                 grad_ref[column, span, :] = grad
                 grad = decay_ref[column, span, :] * grad
-            state = carry_ref[chunk, 0]
+            state = carry_ref[chunk, 0].astype(jnp.float32)
             for column in range(col_count):
                 gate_ref[column, span, :] = jnp.sum(grads[column] * state, axis=-1, keepdims=True)
                 state = decay_ref[column, span, :] * state + fresh_ref[column, span, :]
@@ -139,11 +139,16 @@
     weight_c = by_column(cotangent)
     decay_c = by_column(decay_rows[..., None])
     factor = jnp.prod(jnp.swapaxes(decay_rows, 0, 1).reshape(col_count, count, part), 0)
-    factor_row = jnp.pad(factor, ((0, 0), (0, channel_count - part)))
+    factor_high = factor.astype(jnp.bfloat16).astype(jnp.float32)
+    factor_low = (factor - factor_high).astype(jnp.bfloat16).astype(jnp.float32)
+    factor_row = jnp.pad(
+        jnp.stack([factor_high, factor_low], 1), ((0, 0), (0, 0), (0, channel_count - part))
+    )
     payload = summary_kernel(fresh_c, weight_c, decay_c, factor_row, count)
-    got = lax.all_to_all(payload, "col", 0, 0, tiled=True)
-    carries = carry_kernel(got[:, :part], got[:, part : 2 * part], got[:, 2 * part, :part][..., None])
-    ret = lax.all_to_all(carries, "col", 0, 0, tiled=True)
+    got = lax.all_to_all(payload.astype(jnp.bfloat16), "col", 0, 0, tiled=True).astype(jnp.float32)
+    factor_got = got[:, 2 * part, :part] + got[:, 2 * part + 1, :part]
+    carries = carry_kernel(got[:, :part], got[:, part : 2 * part], factor_got[..., None])
+    ret = lax.all_to_all(carries.astype(jnp.bfloat16), "col", 0, 0, tiled=True)
     grads, gates = fixup_kernel(fresh_c, weight_c, decay_c, ret)
     grads = jnp.swapaxes(grads.reshape(col_count, row_count, flat_rows, channel_count), 0, 1)
     gates = jnp.swapaxes(gates.reshape(col_count, row_count, flat_rows), 0, 1)

time: 112 us -> 97.8 us (0.87)
  blocking collectives: 56.1 us -> 40.7 us
  other arithmetic: 2.45 us -> 5.56 us
  local copies, waits for them, and re-layouts: 11.8 us -> 10 us
    all_to_all x2, blocking collectives: 56.1 us -> 40.7 us  [the longest x1 23.4 us: chain_scan(): lax.all_to_all(payload.astype(jnp.bfloat16), 'col', 0, 0, tiled=True)]
    convert_element_type x0 -> x5, other arithmetic: none -> 2.47 us  [the longest x1 1.19 us: chain_scan(): payload.astype(jnp.bfloat16)]
    pallas_call x1 -> x0, local copies, waits for them, and re-layouts: 1.47 us -> none  [carry_kernel(): pl.pallas_call(body, out_shape=jax.ShapeDtypeStruct((count, 2, part, chan...]
where the time goes in v5:
time: 97.8 us; the launch traced here: 97.3 us
  blocking collectives  40.7 us (42%)
  Pallas kernels  12.8 us (13%)
  starting transfers between devices  10.1 us (10%)
  waiting for transfers between devices  10.1 us (10%)
  local copies, waits for them, and re-layouts  10 us (10%)
  matrix products  7.09 us (7%)
  other arithmetic  5.56 us (6%)
    all_to_all x1, blocking collectives, chain_scan(): lax.all_to_all(payload.astype(jnp.bfloat16), 'col', 0, 0, tiled=True)  23.4 us
    all_to_all x1, blocking collectives, chain_scan(): ret = lax.all_to_all(carries.astype(jnp.bfloat16), 'col', 0, 0, tiled=True)  17.2 us
    ppermute x2, starting transfers between devices, from_behind(): lax.ppermute(value, axis, [(source, source + steps) for source in range(i...  10.1 us
    ppermute x2, waiting for transfers between devices, from_behind(): lax.ppermute(value, axis, [(source, source + steps) for source in range(i...  10.1 us
    pallas_call x1, Pallas kernels, fixup_kernel(): pl.pallas_call(body, out_shape=(jax.ShapeDtypeStruct((col_count, rows, ch...  7.78 us
    unnamed x19, local copies, waits for them, and re-layouts  3.18 us
    pallas_call x1, Pallas kernels, summary_kernel(): pl.pallas_call(body, out_shape=jax.ShapeDtypeStruct((count, 2 * part + 2,...  2.65 us
    pallas_call x1, Pallas kernels, carry_kernel(): pl.pallas_call(body, out_shape=jax.ShapeDtypeStruct((count, 2, part, chan...  2.4 us
  transfers between devices with their start and end apart: 2, of which 2 were waited for; matrix products, arithmetic and copies ran while one was open for 4% of the time, Pallas kernels for 0%

profile of v5, /device:TPU:17, one launch (start us, length us, event | category | flops | bytes accessed | tf_op | source)
XLA Modules:
  0.0 97.3 jit_solution(11277792992607662458)
XLA Ops:
  0.6 0.0 copy-start
  0.6 0.0 copy-start.5
  0.7 3.9 %collective-permute-start = (bf16[2,5,128,128]{3,2,1,0:T(8,128)(2,1)}, bf16[2,5,128,128]{3,2,1,0:T(8,128)(2,1)S(1)}, u32[]{:S(2)}, u32[]{:S(2)}) collective-permute-start(bf16[2,5,128,128]{3,2,1,0:T(8,128)(2,1)} %bitcast.56), channel_id=1, source_target_pairs={{0,32},{32,64},{64,96},{96,128},{128,160},{160,192},{192,224},{224... | collective-permute-start | bytes 983048 | tf_op jit(solution)/shard_map/ppermute | solution.py:12
  4.6 0.0 copy-done.5
  4.6 0.1 reduce_prod.12
  4.7 0.1 copy.74
  4.8 0.1 copy.75
  5.0 0.0 copy-start.3
  5.0 1.1 %copy.81.decay_ref = f32[2,640,1]{2,1,0:T(8,128)} copy(f32[2,640,1]{1,0,2:T(2,128)S(1)} %bitcast.59) | data formatting | bytes 10240 | tf_op jit(solution)/shard_map/reshape;transpose;broadcast_in_dim;reshape | solution.py:136
  6.1 0.7 select_maximum_fusion.factor_ref
  6.7 0.7 copy-done.8
  7.4 0.1 fusion.26
  7.5 1.4 %collective-permute-done = bf16[2,5,128,128]{3,2,1,0:T(8,128)(2,1)S(1)} collective-permute-done((bf16[2,5,128,128]{3,2,1,0:T(8,128)(2,1)}, bf16[2,5,128,128]{3,2,1,0:T(8,128)(2,1)S(1)}, u32[]{:S(2)}, u32[]{:S(2)}) %collective-permute-start) | collective-permute-done | bytes 327712 | tf_op jit(solution)/shard_map/ppermute | solution.py:12
  8.9 0.0 copy-done.3
  8.9 0.0 copy-start.7
  8.9 0.7 copy-done.7
  9.6 0.4 convolution_convert_fusion.1
  10.0 0.0 copy-done
  10.0 0.5 convolution_bitcast_fusion.1
  10.5 0.4 copy.71
  10.9 0.0 copy-start.6
  10.9 0.7 copy-done.6
  11.6 0.6 fusion.14
  12.2 0.4 copy-done.4
  12.6 1.0 %bitcast_add_fusion = f32[1,2,5,128,128]{4,3,2,1,0:T(8,128)} fusion(f32[2,5,128,128]{3,1,2,0:T(8,128)S(1)} %fusion.14, bf16[1,2,5,128,128]{4,3,2,1,0:T(8,128)(2,1)S(1)} %copy-done.4), kind=kLoop, calls=%fused_computation.11 | loop fusion | flops 327680 | bytes 1638400 | tf_op jit(solution)/shard_map/add | solution.py:167
  13.5 2.7 %shard_map.103 = f32[32,42,128]{2,1,0:T(8,128)} custom-call(f32[2,640,128]{2,1,0:T(8,128)} %bitcast.50, f32[2,640,128]{2,1,0:T(8,128)} %bitcast.52, f32[2,640,1]{2,1,0:T(8,128)} %copy.81.decay_ref, f32[32,2,128]{2,1,0:T(2,128)} %select_maximum_fusion.factor_ref), custom_call_target="tpu_custom_call" | custom-call | tf_op jit(solution)/shard_map/pallas_call | solution.py:94
  16.2 1.2 %convert_element_type.117 = bf16[32,42,128]{2,1,0:T(8,128)(2,1)S(1)} convert(f32[32,42,128]{2,1,0:T(8,128)} %shard_map.103) | non-fusion elementwise | flops 172032 | bytes 1032192 | tf_op jit(solution)/shard_map/convert_element_type | solution.py:148
  17.4 23.4 %all_to_all.10 = bf16[32,42,128]{2,1,0:T(8,128)(2,1)S(1)} all-to-all(bf16[32,42,128]{2,1,0:T(8,128)(2,1)S(1)} %convert_element_type.117), channel_id=1, replica_groups=mesh['row'=16,'col'=32] {'col'}, dimensions={0} | all-to-all | bytes 688128 | tf_op jit(solution)/shard_map/all_to_all | solution.py:148
  40.8 0.1 convert_element_type.118
  40.9 1.1 %copy.79.factor_ref = f32[32,20,1]{2,1,0:T(8,128)} copy(f32[32,20,1]{1,0,2:T(8,128)S(1)} %bitcast.58) | data formatting | bytes 5120 | tf_op jit(solution)/shard_map/add | solution.py:149
  41.9 0.9 fusion.27
  42.9 2.4 %shard_map.104 = f32[32,2,20,128]{3,2,1,0:T(8,128)} custom-call(f32[32,20,128]{2,1,0:T(8,128)} %get-tuple-element.20.fwd_b_ref, f32[32,20,128]{2,1,0:T(8,128)} %get-tuple-element.19.bwd_b_ref, f32[32,20,1]{2,1,0:T(8,128)} %copy.79.factor_ref), custom_call_target="tpu_custom_call" | custom-call | tf_op jit(solution)/shard_map/pallas_call | solution.py:70
  45.3 1.2 %convert_element_type.119 = bf16[32,2,20,128]{3,2,1,0:T(8,128)(2,1)S(1)} convert(f32[32,2,20,128]{3,2,1,0:T(8,128)} %shard_map.104) | non-fusion elementwise | flops 163840 | bytes 983040 | tf_op jit(solution)/shard_map/convert_element_type | solution.py:151
  46.5 0.3 copy.80
  46.7 17.2 %all_to_all.11 = bf16[32,2,20,128]{3,1,2,0:T(2,128)(2,1)S(1)} all-to-all(bf16[32,2,20,128]{3,1,2,0:T(2,128)(2,1)S(1)} %copy.80), channel_id=1, replica_groups=mesh['row'=16,'col'=32] {'col'}, dimensions={0} | all-to-all | bytes 655360 | tf_op jit(solution)/shard_map/all_to_all | solution.py:151
  64.0 0.8 copy.82.carry_ref
  64.8 7.8 %shard_map.105 = (f32[2,640,128]{2,1,0:T(8,128)}, f32[2,640,1]{2,1,0:T(8,128)}) custom-call(f32[2,640,128]{2,1,0:T(8,128)} %bitcast.51, f32[2,640,128]{2,1,0:T(8,128)} %bitcast.53, f32[2,640,1]{2,1,0:T(8,128)} %copy.81.decay_ref, bf16[32,2,20,128]{3,2,1,0:T(8,128)(2,1)} %copy.82.carry_ref), custom_call_target="tpu_custom_call" | custom-call | tf_op jit(solution)/shard_map/pallas_call | solution.py:119
  72.5 1.6 %convolution_convert_fusion = bf16[2,8,128,128]{3,1,2,0:T(8,128)(2,1)S(1)} fusion(f32[2,5,128,128]{3,2,1,0:T(8,128)} %bitcast.54, s32[2,8]{1,0:T(2,128)S(1)} %bitcast.62), kind=kOutput, calls=%fused_computation.3 | convolution fusion | flops 2883664 | bytes 1179712 | tf_op jit(solution)/shard_map/rckn,rcnaj->rckaj/dot_general | solution.py:43
  74.2 0.4 copy.87
  74.6 1.3 %convolution_bitcast_fusion = f32[2,8,128,128]{2,3,1,0:T(8,128)} fusion(bf16[2,8,128,128]{2,3,1,0:T(8,128)(2,1)S(1)} %copy.87, bf16[1,2,8,128,128]{4,3,2,1,0:T(8,128)(2,1)S(1)} %copy-done), kind=kOutput, calls=%fused_computation | convolution fusion | flops 67108864 | bytes 2097152 | tf_op jit(solution)/shard_map/rckab,rckaj->rckbj/dot_general | solution.py:50
  75.8 1.6 %copy.88 = f32[2,8,128,128]{3,1,2,0:T(8,128)S(1)} copy(f32[2,8,128,128]{2,3,1,0:T(8,128)} %convolution_bitcast_fusion) | data formatting | bytes 2097152 | tf_op jit(solution)/shard_map/rckab,rckaj->rckbj/dot_general | solution.py:50
  77.5 1.4 %convolution_convert_fusion.2 = bf16[2,5,128,128]{3,1,2,0:T(8,128)(2,1)} fusion(f32[2,8,128,128]{3,1,2,0:T(8,128)S(1)} %copy.88, s32[2,8]{1,0:T(2,128)S(1)} %bitcast.64, pred[2,8]{1,0:T(4,128)(4,1)S(1)} %get-tuple-element.22), kind=kOutput, calls=%fused_computation.6 | convolution fusion | flops 15892640 | bytes 1376336 | tf_op jit(solution)/shard_map/rckn,rckbj->rcnbj/dot_general | solution.py:51
  78.9 6.2 %collective-permute-start.1 = (bf16[2,5,128,128]{3,1,2,0:T(8,128)(2,1)}, bf16[2,5,128,128]{3,1,2,0:T(8,128)(2,1)S(1)}, u32[]{:S(2)}, u32[]{:S(2)}) collective-permute-start(bf16[2,5,128,128]{3,1,2,0:T(8,128)(2,1)} %convolution_convert_fusion.2), channel_id=1, source_target_pairs={{32,0},{64,32},{96,64},{128,96},{160,128},{192,160},{224,192},{256... | collective-permute-start | bytes 983048 | tf_op jit(solution)/shard_map/ppermute | solution.py:12
  85.1 0.8 reduce.1
  86.0 1.3 %fusion.1 = bf16[1,2,8,128,128]{4,3,2,1,0:T(8,128)(2,1)} fusion(bf16[2,8,128,128]{2,3,1,0:T(8,128)(2,1)S(1)} %copy.87, f32[2,8]{1,0:T(2,128)S(1)} %get-tuple-element.21, bf16[2,8,128,128]{3,1,2,0:T(8,128)(2,1)S(1)} %convolution_convert_fusion.1), kind=kOutput, calls=%fused_computation.7 | convolution fusion | flops 67633152 | bytes 1572928 | tf_op jit(solution)/shard_map/rckaj,rckbj->rckab/dot_general | solution.py:47
  87.3 8.7 %collective-permute-done.1 = bf16[2,5,128,128]{3,1,2,0:T(8,128)(2,1)S(1)} collective-permute-done((bf16[2,5,128,128]{3,1,2,0:T(8,128)(2,1)}, bf16[2,5,128,128]{3,1,2,0:T(8,128)(2,1)S(1)}, u32[]{:S(2)}, u32[]{:S(2)}) %collective-permute-start.1) | collective-permute-done | bytes 327712 | tf_op jit(solution)/shard_map/ppermute | solution.py:12
  96.0 0.5 fusion.3
  96.5 0.8 copy.90
  (11 shorter events, 0.1 us)
Async XLA Ops:
  0.6 9.4 %copy-start = (bf16[1,2,8,128,128]{4,3,2,1,0:T(8,128)(2,1)S(1)}, bf16[1,2,8,128,128]{4,3,2,1,0:T(8,128)(2,1)}, u32[]{:S(2)}) copy-start(bf16[1,2,8,128,128]{4,3,2,1,0:T(8,128)(2,1)} %param.8) | copy-start | bytes 1572868
  0.6 3.9 %copy-start.5 = (f32[1,2,5,128]{3,1,2,0:T(2,128)S(1)}, f32[1,2,5,128]{3,1,2,0:T(2,128)}, u32[]{:S(2)}) copy-start(f32[1,2,5,128]{3,1,2,0:T(2,128)} %param.14) | copy-start | bytes 15364
  0.7 8.2 %collective-permute-start = (bf16[2,5,128,128]{3,2,1,0:T(8,128)(2,1)}, bf16[2,5,128,128]{3,2,1,0:T(8,128)(2,1)S(1)}, u32[]{:S(2)}, u32[]{:S(2)}) collective-permute-start(bf16[2,5,128,128]{3,2,1,0:T(8,128)(2,1)} %bitcast.56), channel_id=1, source_target_pairs={{0,32},{32,64},{64,96},{96,128},{128,160},{160,192},{192,224},{224... | collective-permute-start | bytes 983048 | tf_op jit(solution)/shard_map/ppermute | solution.py:12
  5.0 3.9 %copy-start.3 = (bf16[2,5,128,128]{3,2,1,0:T(8,128)(2,1)S(1)}, bf16[2,5,128,128]{3,2,1,0:T(8,128)(2,1)}, u32[]{:S(2)}) copy-start(bf16[2,5,128,128]{3,2,1,0:T(8,128)(2,1)} %param.13) | copy-start | bytes 983044
  6.7 0.7 copy-start.8
  8.9 0.7 copy-start.7
  10.9 0.7 copy-start.6
  11.6 1.0 %copy-start.4 = (bf16[1,2,5,128,128]{4,3,2,1,0:T(8,128)(2,1)S(1)}, bf16[1,2,5,128,128]{4,3,2,1,0:T(8,128)(2,1)}, u32[]{:S(2)}) copy-start(bf16[1,2,5,128,128]{4,3,2,1,0:T(8,128)(2,1)} %param.12) | copy-start | bytes 983044
  77.5 7.7 %copy-start.2 = (f32[2,640,1]{2,1,0:T(8,128)S(1)}, f32[2,640,1]{2,1,0:T(8,128)}, u32[]{:S(2)}) copy-start(f32[2,640,1]{2,1,0:T(8,128)} %get-tuple-element.6) | copy-start | bytes 15364
  78.9 17.1 %collective-permute-start.1 = (bf16[2,5,128,128]{3,1,2,0:T(8,128)(2,1)}, bf16[2,5,128,128]{3,1,2,0:T(8,128)(2,1)S(1)}, u32[]{:S(2)}, u32[]{:S(2)}) collective-permute-start(bf16[2,5,128,128]{3,1,2,0:T(8,128)(2,1)} %convolution_convert_fusion.2), channel_id=1, source_target_pairs={{32,0},{64,32},{96,64},{128,96},{160,128},{192,160},{224,192},{256... | collective-permute-start | bytes 983048 | tf_op jit(solution)/shard_map/ppermute | solution.py:12
  86.0 10.0 %copy-start.1 = (f32[2,640,128]{2,1,0:T(8,128)S(1)}, f32[2,640,128]{2,1,0:T(8,128)}, u32[]{:S(2)}) copy-start(f32[2,640,128]{2,1,0:T(8,128)} %get-tuple-element.5) | copy-start | bytes 1966084

commit v6 on v4

--- a/solution.py
+++ b/solution.py
@@ -32,26 +32,47 @@
     return jnp.einsum("rckn,rckaj->rcnaj", placed, products, precision=lax.Precision.HIGHEST)
 
 
-def backward_blocks(blocks, above_env, rounded, src_pick, dst_pick, active_slot_list):
-    taken = (src_pick & active_slot_list[..., None]).astype(jnp.float32)
-    src_bf = src_pick.astype(jnp.bfloat16)
-    dst_bf = dst_pick.astype(jnp.bfloat16)
-    slot_live = active_slot_list.astype(jnp.float32)
-    gathered = jnp.einsum(
-        "rckn,rcnbj->rckbj", src_bf, above_env, preferred_element_type=jnp.float32
-    ).astype(jnp.bfloat16)
-    picked = jnp.einsum(
-        "rckn,rcnaj->rckaj", dst_bf, rounded, preferred_element_type=jnp.float32
-    ).astype(jnp.bfloat16)
-    grads = (
-        jnp.einsum("rckaj,rckbj->rckab", picked, gathered, preferred_element_type=jnp.float32)
-        * slot_live[..., None, None]
-    ).astype(jnp.bfloat16)
-    contrib = jnp.einsum("rckab,rckaj->rckbj", blocks, picked, preferred_element_type=jnp.float32)
-    returned = jnp.einsum(
-        "rckn,rckbj->rcnbj", taken, contrib, precision=lax.Precision.HIGHEST
-    ).astype(jnp.bfloat16)
-    return (grads, returned)
+def backward_kernel(blocks, above_env, rounded, sources, targets, counts):
+    site_count, slot_count = blocks.shape[:2]
+    sector_count = above_env.shape[1]
+
+    def body(src_ref, dst_ref, cnt_ref, blocks_ref, above_ref, rounded_ref, grads_ref, ret_ref, acc_ref):
+        for site in range(site_count):
+            acc_ref[...] = jnp.zeros(acc_ref.shape, jnp.float32)
+            for slot in range(slot_count):
+                place = site * slot_count + slot
+                source = jnp.clip(src_ref[place], 0, sector_count - 1)
+                target = jnp.clip(dst_ref[place], 0, sector_count - 1)
+                live = slot < cnt_ref[site]
+                picked = rounded_ref[site, target]
+                gathered = above_ref[site, source]
+                grad = lax.dot_general(
+                    picked, gathered, (((1,), (1,)), ((), ())), preferred_element_type=jnp.float32
+                )
+                grads_ref[site, slot] = jnp.where(live, grad, 0.0).astype(grads_ref.dtype)
+                contrib = lax.dot_general(
+                    blocks_ref[site, slot], picked, (((0,), (0,)), ((), ())),
+                    preferred_element_type=jnp.float32,
+                )
+
+                @pl.when(live)
+                def _():
+                    acc_ref[source] += contrib
+
+            ret_ref[site] = acc_ref[...].astype(ret_ref.dtype)
+
+    smem = pl.BlockSpec(memory_space=pltpu.SMEM)
+    vmem = pl.BlockSpec(memory_space=pltpu.VMEM)
+    return pl.pallas_call(
+        body,
+        in_specs=[smem, smem, smem, vmem, vmem, vmem],
+        out_specs=(vmem, vmem),
+        out_shape=(
+            jax.ShapeDtypeStruct(blocks.shape, jnp.bfloat16),
+            jax.ShapeDtypeStruct(above_env.shape, jnp.bfloat16),
+        ),
+        scratch_shapes=[pltpu.VMEM(above_env.shape[1:], jnp.float32)],
+    )(sources, targets, counts, blocks, above_env, rounded)
 
 
 def carry_kernel(fwd_b, bwd_b, factor):
@@ -167,9 +188,17 @@
     condition_derivative, gate_grad = chain_scan(fresh, decay_rows, cotangent)
     condition_derivative = condition_derivative.reshape(environment.shape)
     rounded = condition_derivative.astype(jnp.bfloat16)
-    grad_blocks, returned = backward_blocks(
-        blocks, above_env, rounded, src_pick, dst_pick, active_slot_list
-    )
+    site_count = row_count * col_count
+    grad_blocks, returned = backward_kernel(
+        blocks.reshape((site_count,) + blocks.shape[2:]),
+        above_env.reshape((site_count,) + above_env.shape[2:]),
+        rounded.reshape((site_count,) + rounded.shape[2:]),
+        sources.reshape(-1),
+        targets.reshape(-1),
+        counts.reshape(-1),
+    )
+    grad_blocks = grad_blocks.reshape(blocks.shape)
+    returned = returned.reshape(environment.shape)
     below_rows = from_behind(returned[0], "row", -1)
     following_horizontals = jnp.concatenate([returned[1:], below_rows[None]], 0)
     grad_env = (condition_derivative + following_horizontals.astype(jnp.float32)).astype(

time: 112 us -> 112 us (level)
  blocking collectives: 56.1 us -> 32.7 us
  waiting for transfers between devices: 9.63 us -> 23.7 us
  starting transfers between devices: 11.1 us -> 18.4 us
  matrix products: 7.08 us -> 1.47 us
  Pallas kernels: 12.9 us -> 18.2 us
  other arithmetic: 2.45 us -> 4.62 us
    all_to_all x1 -> x0, blocking collectives: 23.4 us -> none  [chain_scan(): ret = lax.all_to_all(carries, 'col', 0, 0, tiled=True)]
    all_to_all x0 -> x1, waiting for transfers between devices: none -> 14.9 us  [chain_scan(): ret = lax.all_to_all(carries, 'col', 0, 0, tiled=True)]
    all_to_all x0 -> x1, starting transfers between devices: none -> 7.52 us  [chain_scan(): ret = lax.all_to_all(carries, 'col', 0, 0, tiled=True)]
    dot_general x4 -> x0, matrix products: 5.6 us -> none  [the longest x1 1.64 us: backward_blocks(): jnp.einsum('rckn,rcnaj->rckaj', dst_bf, rounded, preferred_element_type=j...]
    pallas_call x0 -> x1, Pallas kernels: none -> 5.25 us  [backward_kernel(): pl.pallas_call(body, in_specs=[smem, smem, smem, vmem, vmem, vmem], out_s...]
    convert_element_type x1, other arithmetic: 0.07 us -> 1.86 us  [local(): rounded = condition_derivative.astype(jnp.bfloat16)]
    dot_general x1 -> x0, local copies, waits for them, and re-layouts: 1.61 us -> none  [backward_blocks(): jnp.einsum('rckab,rckaj->rckbj', blocks, picked, preferred_element_type=j...]
    reshape x0 -> x2, local copies, waits for them, and re-layouts: none -> 1.19 us  [the longest x1 0.6 us: local(): targets.reshape(-1)]
  transfers between devices with their start and end apart: 2 -> 3, of which waited for: 2 -> 3; matrix products, arithmetic and copies ran while one was open for 4% -> 4% of each run, Pallas kernels for 0% -> 0%
where the time goes in v6:
time: 112 us
  blocking collectives  32.7 us (29%)
  waiting for transfers between devices  23.7 us (21%)
  starting transfers between devices  18.4 us (16%)
  Pallas kernels  18.2 us (16%)
  local copies, waits for them, and re-layouts  11.8 us (11%)
  other arithmetic  4.62 us (4%)
  matrix products  1.47 us (1%)
    all_to_all x1, blocking collectives, chain_scan(): got = lax.all_to_all(payload, 'col', 0, 0, tiled=True)  32.7 us
    all_to_all x1, waiting for transfers between devices, chain_scan(): ret = lax.all_to_all(carries, 'col', 0, 0, tiled=True)  14.9 us
    ppermute x2, starting transfers between devices, from_behind(): lax.ppermute(value, axis, [(source, source + steps) for source in range(i...  10.9 us
    ppermute x2, waiting for transfers between devices, from_behind(): lax.ppermute(value, axis, [(source, source + steps) for source in range(i...  8.81 us
    pallas_call x1, Pallas kernels, fixup_kernel(): pl.pallas_call(body, out_shape=(jax.ShapeDtypeStruct((col_count, rows, ch...  7.93 us
    all_to_all x1, starting transfers between devices, chain_scan(): ret = lax.all_to_all(carries, 'col', 0, 0, tiled=True)  7.52 us
    pallas_call x1, Pallas kernels, backward_kernel(): pl.pallas_call(body, in_specs=[smem, smem, smem, vmem, vmem, vmem], out_s...  5.25 us
    unnamed x20, local copies, waits for them, and re-layouts  3.08 us
  transfers between devices with their start and end apart: 3, of which 3 were waited for; matrix products, arithmetic and copies ran while one was open for 4% of the time, Pallas kernels for 0%

profile of v6, /device:TPU:17, one launch (start us, length us, event | category | flops | bytes accessed | tf_op | source)
XLA Modules:
  0.0 111.6 jit_solution(15443500373221267092)
XLA Ops:
  0.6 0.0 copy-start.6
  0.6 3.8 %collective-permute-start = (bf16[2,5,128,128]{3,2,1,0:T(8,128)(2,1)}, bf16[2,5,128,128]{3,2,1,0:T(8,128)(2,1)S(1)}, u32[]{:S(2)}, u32[]{:S(2)}) collective-permute-start(bf16[2,5,128,128]{3,2,1,0:T(8,128)(2,1)} %bitcast.38), channel_id=1, source_target_pairs={{0,32},{32,64},{64,96},{96,128},{128,160},{160,192},{192,224},{224... | collective-permute-start | bytes 983048 | tf_op jit(solution)/shard_map/ppermute | solution.py:12
  4.4 0.0 copy-done.6
  4.4 0.0 copy-start.4
  4.4 1.1 copy.48.decay_ref
  5.6 0.1 reduce_prod.12
  5.7 0.6 pad.4.factor_ref
  6.3 0.7 copy-done.9
  6.9 0.1 iota_compare_fusion.2
  7.0 1.7 %collective-permute-done = bf16[2,5,128,128]{3,2,1,0:T(8,128)(2,1)S(1)} collective-permute-done((bf16[2,5,128,128]{3,2,1,0:T(8,128)(2,1)}, bf16[2,5,128,128]{3,2,1,0:T(8,128)(2,1)S(1)}, u32[]{:S(2)}, u32[]{:S(2)}) %collective-permute-start) | collective-permute-done | bytes 327712 | tf_op jit(solution)/shard_map/ppermute | solution.py:12
  8.7 0.0 copy-done.4
  8.8 0.0 copy-start
  8.8 0.0 copy-start.7
  8.8 0.7 copy-done.7
  9.5 0.0 copy-start.2
  9.5 0.4 convolution_convert_fusion
  9.9 0.0 copy-done
  9.9 0.7 copy-done.2
  10.5 0.5 convolution_bitcast_fusion
  11.0 0.4 copy.41
  11.4 0.0 copy-start.8
  11.5 0.7 copy-done.8
  12.1 0.0 copy-start.5
  12.1 0.6 fusion.5
  12.7 0.4 copy-done.5
  13.1 1.0 bitcast_add_fusion
  14.1 2.6 %shard_map.103 = f32[32,41,128]{2,1,0:T(8,128)} custom-call(f32[2,640,128]{2,1,0:T(8,128)} %bitcast.31, f32[2,640,128]{2,1,0:T(8,128)} %bitcast.35, f32[2,640,1]{2,1,0:T(8,128)} %copy.48.decay_ref, f32[32,128]{1,0:T(8,128)} %pad.4.factor_ref), custom_call_target="tpu_custom_call" | custom-call | tf_op jit(solution)/shard_map/pallas_call | solution.py:115
  16.7 32.7 %all_to_all.10 = f32[32,41,128]{2,1,0:T(8,128)S(1)} all-to-all(f32[32,41,128]{2,1,0:T(8,128)} %shard_map.103), channel_id=1, replica_groups=mesh['row'=16,'col'=32] {'col'}, dimensions={0} | all-to-all | bytes 1343488 | tf_op jit(solution)/shard_map/all_to_all | solution.py:165
  49.4 1.1 copy.46.factor_ref
  50.5 0.9 fusion.13
  51.4 2.4 %shard_map.104 = f32[32,2,20,128]{3,2,1,0:T(8,128)} custom-call(f32[32,20,128]{2,1,0:T(8,128)} %get-tuple-element.24.fwd_b_ref, f32[32,20,128]{2,1,0:T(8,128)} %get-tuple-element.23.bwd_b_ref, f32[32,20,1]{2,1,0:T(8,128)} %copy.46.factor_ref), custom_call_target="tpu_custom_call" | custom-call | tf_op jit(solution)/shard_map/pallas_call | solution.py:91
  53.8 2.3 %copy.47 = f32[32,2,20,128]{3,1,2,0:T(2,128)} copy(f32[32,2,20,128]{3,2,1,0:T(8,128)} %shard_map.104) | data formatting | bytes 1310720 | tf_op jit(solution)/shard_map/pallas_call | solution.py:91
  56.1 7.5 %all-to-all-start.1 = ((f32[32,2,20,128]{3,1,2,0:T(2,128)}), f32[32,2,20,128]{3,1,2,0:T(2,128)S(1)}, u32[]{:S(2)}, u32[]{:S(2)}) async-start(f32[32,2,20,128]{3,1,2,0:T(2,128)} %copy.47), calls=%async_computation.1 | async-start | bytes 1310720 | tf_op jit(solution)/shard_map/all_to_all | solution.py:167
  63.6 0.6 reshape.83.src_ref
  64.2 0.6 reshape.84.dst_ref
  64.8 14.9 %all-to-all-done.1 = f32[32,2,20,128]{3,1,2,0:T(2,128)S(1)} async-done(((f32[32,2,20,128]{3,1,2,0:T(2,128)}), f32[32,2,20,128]{3,1,2,0:T(2,128)S(1)}, u32[]{:S(2)}, u32[]{:S(2)}) %all-to-all-start.1) | async-done | bytes 655392 | tf_op jit(solution)/shard_map/all_to_all | solution.py:167
  79.7 1.0 copy.49.carry_ref
  80.7 7.9 %shard_map.105 = (f32[2,640,128]{2,1,0:T(8,128)}, f32[2,640,1]{2,1,0:T(8,128)}) custom-call(f32[2,640,128]{2,1,0:T(8,128)} %bitcast.32, f32[2,640,128]{2,1,0:T(8,128)} %bitcast.36, f32[2,640,1]{2,1,0:T(8,128)} %copy.48.decay_ref, f32[32,2,20,128]{3,2,1,0:T(8,128)} %copy.49.carry_ref), custom_call_target="tpu_custom_call" | custom-call | tf_op jit(solution)/shard_map/pallas_call | solution.py:140
  88.6 1.9 %convert_element_type.29.rounded_ref = bf16[2,5,128,128]{3,2,1,0:T(8,128)(2,1)} convert(f32[2,5,128,128]{3,2,1,0:T(8,128)} %bitcast.33) | non-fusion elementwise | flops 163840 | bytes 983040 | tf_op jit(solution)/shard_map/convert_element_type | solution.py:190
  90.5 0.0 copy-start.3
  90.5 0.0 copy-start.1
  90.5 5.3 %shard_map.106 = (bf16[2,8,128,128]{3,2,1,0:T(8,128)(2,1)}, bf16[2,5,128,128]{3,2,1,0:T(8,128)(2,1)}) custom-call(s32[16]{0:T(128)} %reshape.83.src_ref, s32[16]{0:T(128)} %reshape.84.dst_ref, s32[2]{0:T(128)} %bitcast.44, bf16[2,8,128,128]{3,2,1,0:T(8,128)(2,1)} %bitcast.37, bf16[2,5,128,128]{3,2,1,0:T(8,128)(2,1)} %copy-done, ...), custom_call_target="tpu_custom_call" | custom-call | tf_op jit(solution)/shard_map/pallas_call | solution.py:66
  95.7 7.2 %collective-permute-start.1 = (bf16[2,5,128,128]{3,2,1,0:T(8,128)(2,1)}, bf16[2,5,128,128]{3,2,1,0:T(8,128)(2,1)S(1)}, u32[]{:S(2)}, u32[]{:S(2)}) collective-permute-start(bf16[2,5,128,128]{3,2,1,0:T(8,128)(2,1)} %get-tuple-element.9), channel_id=1, source_target_pairs={{32,0},{64,32},{96,64},{128,96},{160,128},{192,160},{224,192},{256... | collective-permute-start | bytes 983048 | tf_op jit(solution)/shard_map/ppermute | solution.py:12
  102.9 0.0 copy-done.3
  102.9 0.8 reduce.1
  103.8 7.1 %collective-permute-done.1 = bf16[2,5,128,128]{3,2,1,0:T(8,128)(2,1)S(1)} collective-permute-done((bf16[2,5,128,128]{3,2,1,0:T(8,128)(2,1)}, bf16[2,5,128,128]{3,2,1,0:T(8,128)(2,1)S(1)}, u32[]{:S(2)}, u32[]{:S(2)}) %collective-permute-start.1) | collective-permute-done | bytes 327712 | tf_op jit(solution)/shard_map/ppermute | solution.py:12
  110.8 0.0 copy-done.1
  110.8 0.8 fusion.2
  (4 shorter events, 0.1 us)
Async XLA Ops:
  0.6 3.8 %copy-start.6 = (f32[1,2,5,128]{3,1,2,0:T(2,128)S(1)}, f32[1,2,5,128]{3,1,2,0:T(2,128)}, u32[]{:S(2)}) copy-start(f32[1,2,5,128]{3,1,2,0:T(2,128)} %param.14) | copy-start | bytes 15364
  0.6 8.1 %collective-permute-start = (bf16[2,5,128,128]{3,2,1,0:T(8,128)(2,1)}, bf16[2,5,128,128]{3,2,1,0:T(8,128)(2,1)S(1)}, u32[]{:S(2)}, u32[]{:S(2)}) collective-permute-start(bf16[2,5,128,128]{3,2,1,0:T(8,128)(2,1)} %bitcast.38), channel_id=1, source_target_pairs={{0,32},{32,64},{64,96},{96,128},{128,160},{160,192},{192,224},{224... | collective-permute-start | bytes 983048 | tf_op jit(solution)/shard_map/ppermute | solution.py:12
  4.4 4.3 %copy-start.4 = (bf16[2,5,128,128]{3,2,1,0:T(8,128)(2,1)S(1)}, bf16[2,5,128,128]{3,2,1,0:T(8,128)(2,1)}, u32[]{:S(2)}) copy-start(bf16[2,5,128,128]{3,2,1,0:T(8,128)(2,1)} %param.13) | copy-start | bytes 983044
  6.3 0.7 copy-start.9
  8.8 1.1 copy-start
  8.8 0.7 copy-start.7
  9.5 1.0 copy-start.2
  11.4 0.7 copy-start.8
  12.1 1.0 copy-start.5
  56.1 23.6 %all-to-all-start.1 = ((f32[32,2,20,128]{3,1,2,0:T(2,128)}), f32[32,2,20,128]{3,1,2,0:T(2,128)S(1)}, u32[]{:S(2)}, u32[]{:S(2)}) async-start(f32[32,2,20,128]{3,1,2,0:T(2,128)} %copy.47), calls=%async_computation.1 | async-start | bytes 1310720 | tf_op jit(solution)/shard_map/all_to_all | solution.py:167
  90.5 12.4 %copy-start.3 = (f32[2,640,1]{2,1,0:T(8,128)S(1)}, f32[2,640,1]{2,1,0:T(8,128)}, u32[]{:S(2)}) copy-start(f32[2,640,1]{2,1,0:T(8,128)} %get-tuple-element.10) | copy-start | bytes 15364
  90.5 20.4 %copy-start.1 = (f32[2,640,128]{2,1,0:T(8,128)S(1)}, f32[2,640,128]{2,1,0:T(8,128)}, u32[]{:S(2)}) copy-start(f32[2,640,128]{2,1,0:T(8,128)} %get-tuple-element.7) | copy-start | bytes 1966084
  95.7 15.1 %collective-permute-start.1 = (bf16[2,5,128,128]{3,2,1,0:T(8,128)(2,1)}, bf16[2,5,128,128]{3,2,1,0:T(8,128)(2,1)S(1)}, u32[]{:S(2)}, u32[]{:S(2)}) collective-permute-start(bf16[2,5,128,128]{3,2,1,0:T(8,128)(2,1)} %get-tuple-element.9), channel_id=1, source_target_pairs={{32,0},{64,32},{96,64},{128,96},{160,128},{192,160},{224,192},{256... | collective-permute-start | bytes 983048 | tf_op jit(solution)/shard_map/ppermute | solution.py:12

commit v7 on v6

--- a/solution.py
+++ b/solution.py
@@ -44,7 +44,7 @@
                 source = jnp.clip(src_ref[place], 0, sector_count - 1)
                 target = jnp.clip(dst_ref[place], 0, sector_count - 1)
                 live = slot < cnt_ref[site]
-                picked = rounded_ref[site, target]
+                picked = rounded_ref[site, target].astype(jnp.bfloat16)
                 gathered = above_ref[site, source]
                 grad = lax.dot_general(
                     picked, gathered, (((1,), (1,)), ((), ())), preferred_element_type=jnp.float32
@@ -118,11 +118,11 @@
     )(fresh, cotangent, decay_col, factor_row)
 
 
-def fixup_kernel(fresh, cotangent, decay_col, carries):
+def fixup_kernel(fresh, cotangent, decay_full, carries):
     col_count, rows, channel_count = fresh.shape
     count, _, part, _ = carries.shape
 
-    def body(fresh_ref, weight_ref, decay_ref, carry_ref, grad_ref, gate_ref):
+    def body(fresh_ref, weight_ref, decay_ref, carry_ref, grad_ref, prod_ref):
         for chunk in range(count):
             span = pl.ds(chunk * part, part)
             grad = carry_ref[chunk, 1]
@@ -134,16 +134,14 @@
                 grad = decay_ref[column, span, :] * grad
             state = carry_ref[chunk, 0]
             for column in range(col_count):
-                gate_ref[column, span, :] = jnp.sum(grads[column] * state, axis=-1, keepdims=True)
+                prod_ref[column, span, :] = grads[column] * state
                 state = decay_ref[column, span, :] * state + fresh_ref[column, span, :]
 
-    return pl.pallas_call(
-        body,
-        out_shape=(
-            jax.ShapeDtypeStruct((col_count, rows, channel_count), jnp.float32),
-            jax.ShapeDtypeStruct((col_count, rows, 1), jnp.float32),
-        ),
-    )(fresh, cotangent, decay_col, carries)
+    grads, prods = pl.pallas_call(
+        body,
+        out_shape=(jax.ShapeDtypeStruct((col_count, rows, channel_count), jnp.float32),) * 2,
+    )(fresh, cotangent, decay_full, carries)
+    return (grads, jnp.sum(prods, -1))
 
 
 def chain_scan(fresh, decay_rows, cotangent):
@@ -158,7 +156,7 @@
 
     fresh_c = by_column(fresh)
     weight_c = by_column(cotangent)
-    decay_c = by_column(decay_rows[..., None])
+    decay_c = jnp.broadcast_to(by_column(decay_rows[..., None]), fresh_c.shape)
     factor = jnp.prod(jnp.swapaxes(decay_rows, 0, 1).reshape(col_count, count, part), 0)
     factor_row = jnp.pad(factor, ((0, 0), (0, channel_count - part)))
     payload = summary_kernel(fresh_c, weight_c, decay_c, factor_row, count)
@@ -192,7 +190,7 @@
     grad_blocks, returned = backward_kernel(
         blocks.reshape((site_count,) + blocks.shape[2:]),
         above_env.reshape((site_count,) + above_env.shape[2:]),
-        rounded.reshape((site_count,) + rounded.shape[2:]),
+        condition_derivative.reshape((site_count,) + rounded.shape[2:]),
         sources.reshape(-1),
         targets.reshape(-1),
         counts.reshape(-1),

time: 112 us -> 107 us (0.955)
  Pallas kernels: 18.2 us -> 13.1 us
  other arithmetic: 4.62 us -> 2.77 us
    pallas_call x1, Pallas kernels: 7.93 us -> 2.93 us  [fixup_kernel(): pl.pallas_call(body, out_shape=(jax.ShapeDtypeStruct((col_count, rows, ch...]
    convert_element_type x1 -> x0, other arithmetic: 1.86 us -> none  [local(): rounded = condition_derivative.astype(jnp.bfloat16)]
    ppermute x2, waiting for transfers between devices: 8.81 us -> 9.93 us  [from_behind(): lax.ppermute(value, axis, [(source, source + steps) for source in range(i...]
    unnamed x20 -> x18, local copies, waits for them, and re-layouts: 3.08 us -> 3.07 us
  transfers between devices with their start and end apart: 3 -> 3, of which waited for: 3 -> 3; matrix products, arithmetic and copies ran while one was open for 4% -> 3% of each run, Pallas kernels for 0% -> 0%
where the time goes in v7:
time: 107 us; the launch traced here: 106 us
  blocking collectives  32.7 us (31%)
  waiting for transfers between devices  24.8 us (23%)
  starting transfers between devices  18.6 us (17%)
  Pallas kernels  13.1 us (12%)
  local copies, waits for them, and re-layouts  11.7 us (11%)
  other arithmetic  2.77 us (3%)
  matrix products  1.47 us (1%)
    all_to_all x1, blocking collectives, chain_scan(): got = lax.all_to_all(payload, 'col', 0, 0, tiled=True)  32.7 us
    all_to_all x1, waiting for transfers between devices, chain_scan(): ret = lax.all_to_all(carries, 'col', 0, 0, tiled=True)  14.9 us
    ppermute x2, starting transfers between devices, from_behind(): lax.ppermute(value, axis, [(source, source + steps) for source in range(i...  11.1 us
    ppermute x2, waiting for transfers between devices, from_behind(): lax.ppermute(value, axis, [(source, source + steps) for source in range(i...  9.93 us
    all_to_all x1, starting transfers between devices, chain_scan(): ret = lax.all_to_all(carries, 'col', 0, 0, tiled=True)  7.52 us
    pallas_call x1, Pallas kernels, backward_kernel(): pl.pallas_call(body, in_specs=[smem, smem, smem, vmem, vmem, vmem], out_s...  5.34 us
    unnamed x18, local copies, waits for them, and re-layouts  3.07 us
    pallas_call x1, Pallas kernels, fixup_kernel(): pl.pallas_call(body, out_shape=(jax.ShapeDtypeStruct((col_count, rows, ch...  2.93 us
  transfers between devices with their start and end apart: 3, of which 3 were waited for; matrix products, arithmetic and copies ran while one was open for 3% of the time, Pallas kernels for 0%

profile of v7, /device:TPU:17, one launch (start us, length us, event | category | flops | bytes accessed | tf_op | source)
XLA Modules:
  0.0 105.9 jit_solution(10777144385579495580)
XLA Ops:
  0.6 0.0 copy-start.5
  0.6 3.8 %collective-permute-start = (bf16[2,5,128,128]{3,2,1,0:T(8,128)(2,1)}, bf16[2,5,128,128]{3,2,1,0:T(8,128)(2,1)S(1)}, u32[]{:S(2)}, u32[]{:S(2)}) collective-permute-start(bf16[2,5,128,128]{3,2,1,0:T(8,128)(2,1)} %bitcast.38), channel_id=1, source_target_pairs={{0,32},{32,64},{64,96},{96,128},{128,160},{160,192},{192,224},{224... | collective-permute-start | bytes 983048 | tf_op jit(solution)/shard_map/ppermute | solution.py:12
  4.4 0.0 copy-done.5
  4.5 0.1 reduce_prod.12
  4.6 0.6 pad.4.factor_ref
  5.2 0.0 copy-start.8
  5.2 0.7 copy-done.8
  5.8 0.1 iota_compare_fusion.2
  5.9 2.8 %collective-permute-done = bf16[2,5,128,128]{3,2,1,0:T(8,128)(2,1)S(1)} collective-permute-done((bf16[2,5,128,128]{3,2,1,0:T(8,128)(2,1)}, bf16[2,5,128,128]{3,2,1,0:T(8,128)(2,1)S(1)}, u32[]{:S(2)}, u32[]{:S(2)}) %collective-permute-start) | collective-permute-done | bytes 327712 | tf_op jit(solution)/shard_map/ppermute | solution.py:12
  8.8 0.0 copy-start
  8.8 0.0 copy-start.6
  8.8 0.7 copy-done.6
  9.5 0.0 copy-start.2
  9.5 0.4 convolution_convert_fusion
  9.9 0.0 copy-done
  9.9 0.7 copy-done.2
  10.5 0.5 convolution_bitcast_fusion
  11.0 0.4 copy.31
  11.4 0.0 copy-start.7
  11.5 0.7 copy-done.7
  12.1 0.0 copy-start.4
  12.1 0.6 fusion.5
  12.7 0.4 copy-done.4
  13.1 1.0 bitcast_add_fusion
  14.1 1.1 %broadcast_in_dim.5.decay_ref = f32[2,640,128]{2,1,0:T(8,128)} broadcast(f32[2,640]{1,0:T(2,128)S(1)} %bitcast.40), dimensions={0,1} | broadcast | bytes 660480 | tf_op jit(solution)/shard_map/broadcast_in_dim | solution.py:159
  15.2 2.5 %shard_map.103 = f32[32,41,128]{2,1,0:T(8,128)} custom-call(f32[2,640,128]{2,1,0:T(8,128)} %bitcast.31, f32[2,640,128]{2,1,0:T(8,128)} %bitcast.35, f32[2,640,128]{2,1,0:T(8,128)} %broadcast_in_dim.5.decay_ref, f32[32,128]{1,0:T(8,128)} %pad.4.factor_ref), custom_call_target="tpu_custom_call" | custom-call | tf_op jit(solution)/shard_map/pallas_call | solution.py:115
  17.7 32.7 %all_to_all.10 = f32[32,41,128]{2,1,0:T(8,128)S(1)} all-to-all(f32[32,41,128]{2,1,0:T(8,128)} %shard_map.103), channel_id=1, replica_groups=mesh['row'=16,'col'=32] {'col'}, dimensions={0} | all-to-all | bytes 1343488 | tf_op jit(solution)/shard_map/all_to_all | solution.py:163
  50.3 1.1 copy.34.factor_ref
  51.4 0.9 fusion.13
  52.3 2.4 %shard_map.104 = f32[32,2,20,128]{3,2,1,0:T(8,128)} custom-call(f32[32,20,128]{2,1,0:T(8,128)} %get-tuple-element.12.fwd_b_ref, f32[32,20,128]{2,1,0:T(8,128)} %get-tuple-element.11.bwd_b_ref, f32[32,20,1]{2,1,0:T(8,128)} %copy.34.factor_ref), custom_call_target="tpu_custom_call" | custom-call | tf_op jit(solution)/shard_map/pallas_call | solution.py:91
  54.7 2.3 %copy.35 = f32[32,2,20,128]{3,1,2,0:T(2,128)} copy(f32[32,2,20,128]{3,2,1,0:T(8,128)} %shard_map.104) | data formatting | bytes 1310720 | tf_op jit(solution)/shard_map/pallas_call | solution.py:91
  57.0 7.5 %all-to-all-start.1 = ((f32[32,2,20,128]{3,1,2,0:T(2,128)}), f32[32,2,20,128]{3,1,2,0:T(2,128)S(1)}, u32[]{:S(2)}, u32[]{:S(2)}) async-start(f32[32,2,20,128]{3,1,2,0:T(2,128)} %copy.35), calls=%async_computation.1 | async-start | bytes 1310720 | tf_op jit(solution)/shard_map/all_to_all | solution.py:165
  64.5 0.6 reshape.79.src_ref
  65.1 0.6 reshape.80.dst_ref
  65.7 14.9 %all-to-all-done.1 = f32[32,2,20,128]{3,1,2,0:T(2,128)S(1)} async-done(((f32[32,2,20,128]{3,1,2,0:T(2,128)}), f32[32,2,20,128]{3,1,2,0:T(2,128)S(1)}, u32[]{:S(2)}, u32[]{:S(2)}) %all-to-all-start.1) | async-done | bytes 655392 | tf_op jit(solution)/shard_map/all_to_all | solution.py:165
  80.6 0.9 copy.36.carry_ref
  81.6 2.9 %shard_map.105 = (f32[2,640,128]{2,1,0:T(8,128)}, f32[2,640,128]{2,1,0:T(8,128)}) custom-call(f32[2,640,128]{2,1,0:T(8,128)} %bitcast.32, f32[2,640,128]{2,1,0:T(8,128)} %bitcast.36, f32[2,640,128]{2,1,0:T(8,128)} %broadcast_in_dim.5.decay_ref, f32[32,2,20,128]{3,2,1,0:T(8,128)} %copy.36.carry_ref), custom_call_target="tpu_custom_call" | custom-call | tf_op jit(solution)/shard_map/pallas_call | solution.py:140
  84.5 0.0 copy-start.3
  84.5 5.3 %shard_map.106 = (bf16[2,8,128,128]{3,2,1,0:T(8,128)(2,1)}, bf16[2,5,128,128]{3,2,1,0:T(8,128)(2,1)}) custom-call(s32[16]{0:T(128)} %reshape.79.src_ref, s32[16]{0:T(128)} %reshape.80.dst_ref, s32[2]{0:T(128)} %bitcast.44, bf16[2,8,128,128]{3,2,1,0:T(8,128)(2,1)} %bitcast.37, bf16[2,5,128,128]{3,2,1,0:T(8,128)(2,1)} %copy-done, f32[2,5,128,128]{3,2,1,0:T(8,128)} %bitcast.33), custom_call_target="tpu_custom_call" | custom-call | tf_op jit(solution)/shard_map/pallas_call | solution.py:66
  89.8 0.0 copy-start.1
  89.8 7.3 %collective-permute-start.1 = (bf16[2,5,128,128]{3,2,1,0:T(8,128)(2,1)}, bf16[2,5,128,128]{3,2,1,0:T(8,128)(2,1)S(1)}, u32[]{:S(2)}, u32[]{:S(2)}) collective-permute-start(bf16[2,5,128,128]{3,2,1,0:T(8,128)(2,1)} %get-tuple-element.9), channel_id=1, source_target_pairs={{32,0},{64,32},{96,64},{128,96},{160,128},{192,160},{224,192},{256... | collective-permute-start | bytes 983048 | tf_op jit(solution)/shard_map/ppermute | solution.py:12
  97.1 0.0 copy-done.3
  97.1 0.8 reduce_sum.9
  98.0 7.1 %collective-permute-done.1 = bf16[2,5,128,128]{3,2,1,0:T(8,128)(2,1)S(1)} collective-permute-done((bf16[2,5,128,128]{3,2,1,0:T(8,128)(2,1)}, bf16[2,5,128,128]{3,2,1,0:T(8,128)(2,1)S(1)}, u32[]{:S(2)}, u32[]{:S(2)}) %collective-permute-start.1) | collective-permute-done | bytes 327712 | tf_op jit(solution)/shard_map/ppermute | solution.py:12
  105.1 0.0 copy-done.1
  105.1 0.8 fusion.2
  (3 shorter events, 0.1 us)
Async XLA Ops:
  0.6 3.8 %copy-start.5 = (f32[1,2,5,128]{3,1,2,0:T(2,128)S(1)}, f32[1,2,5,128]{3,1,2,0:T(2,128)}, u32[]{:S(2)}) copy-start(f32[1,2,5,128]{3,1,2,0:T(2,128)} %param.14) | copy-start | bytes 15364
  0.6 8.1 %collective-permute-start = (bf16[2,5,128,128]{3,2,1,0:T(8,128)(2,1)}, bf16[2,5,128,128]{3,2,1,0:T(8,128)(2,1)S(1)}, u32[]{:S(2)}, u32[]{:S(2)}) collective-permute-start(bf16[2,5,128,128]{3,2,1,0:T(8,128)(2,1)} %bitcast.38), channel_id=1, source_target_pairs={{0,32},{32,64},{64,96},{96,128},{128,160},{160,192},{192,224},{224... | collective-permute-start | bytes 983048 | tf_op jit(solution)/shard_map/ppermute | solution.py:12
  5.2 0.7 copy-start.8
  8.8 1.1 %copy-start = (bf16[2,5,128,128]{3,2,1,0:T(8,128)(2,1)}, bf16[2,5,128,128]{3,2,1,0:T(8,128)(2,1)S(1)}, u32[]{:S(2)}) copy-start(bf16[2,5,128,128]{3,2,1,0:T(8,128)(2,1)S(1)} %broadcast_select_fusion.above_ref) | copy-start | bytes 983044
  8.8 0.7 copy-start.6
  9.5 1.0 copy-start.2
  11.4 0.7 copy-start.7
  12.1 1.0 copy-start.4
  57.0 23.6 %all-to-all-start.1 = ((f32[32,2,20,128]{3,1,2,0:T(2,128)}), f32[32,2,20,128]{3,1,2,0:T(2,128)S(1)}, u32[]{:S(2)}, u32[]{:S(2)}) async-start(f32[32,2,20,128]{3,1,2,0:T(2,128)} %copy.35), calls=%async_computation.1 | async-start | bytes 1310720 | tf_op jit(solution)/shard_map/all_to_all | solution.py:165
  84.5 12.6 %copy-start.3 = (f32[2,640,128]{2,1,0:T(8,128)S(1)}, f32[2,640,128]{2,1,0:T(8,128)}, u32[]{:S(2)}) copy-start(f32[2,640,128]{2,1,0:T(8,128)} %get-tuple-element.10) | copy-start | bytes 1966084
  89.8 15.3 %copy-start.1 = (f32[2,640,128]{2,1,0:T(8,128)S(1)}, f32[2,640,128]{2,1,0:T(8,128)}, u32[]{:S(2)}) copy-start(f32[2,640,128]{2,1,0:T(8,128)} %get-tuple-element.7) | copy-start | bytes 1966084
  89.8 15.3 %collective-permute-start.1 = (bf16[2,5,128,128]{3,2,1,0:T(8,128)(2,1)}, bf16[2,5,128,128]{3,2,1,0:T(8,128)(2,1)S(1)}, u32[]{:S(2)}, u32[]{:S(2)}) collective-permute-start(bf16[2,5,128,128]{3,2,1,0:T(8,128)(2,1)} %get-tuple-element.9), channel_id=1, source_target_pairs={{32,0},{64,32},{96,64},{128,96},{160,128},{192,160},{224,192},{256... | collective-permute-start | bytes 983048 | tf_op jit(solution)/shard_map/ppermute | solution.py:12

commit v8 on v7

--- a/solution.py
+++ b/solution.py
@@ -75,23 +75,30 @@
     )(sources, targets, counts, blocks, above_env, rounded)
 
 
-def carry_kernel(fwd_b, bwd_b, factor):
-    count, part, channel_count = fwd_b.shape
-
-    def body(fwd_b_ref, bwd_b_ref, factor_ref, out_ref):
+def carry_kernel(got, part):
+    count, _, channel_count = got.shape
+
+    def body(got_ref, out_ref):
+        diagonal = lax.broadcasted_iota(jnp.int32, (part, channel_count), 0) == lax.broadcasted_iota(
+            jnp.int32, (part, channel_count), 1
+        )
+        factors = []
+        for source in range(count):
+            row = got_ref[source, pl.ds(2 * part, 1), :]
+            factors.append(jnp.sum(jnp.where(diagonal, row, 0.0), axis=-1, keepdims=True))
         state = jnp.zeros((part, channel_count), jnp.float32)
         for source in range(count):
-            out_ref[source, 0] = state
-            state = factor_ref[source] * state + fwd_b_ref[source]
+            out_ref[source, pl.ds(0, part), :] = state
+            state = factors[source] * state + got_ref[source, pl.ds(0, part), :]
         state = jnp.zeros((part, channel_count), jnp.float32)
         for source in reversed(range(count)):
-            out_ref[source, 1] = state
-            state = factor_ref[source] * state + bwd_b_ref[source]
+            out_ref[source, pl.ds(part, part), :] = state
+            state = factors[source] * state + got_ref[source, pl.ds(part, part), :]
 
     return pl.pallas_call(
         body,
-        out_shape=jax.ShapeDtypeStruct((count, 2, part, channel_count), jnp.float32),
-    )(fwd_b, bwd_b, factor)
+        out_shape=jax.ShapeDtypeStruct((count, 2 * part, channel_count), jnp.float32),
+    )(got)
 
 
 def summary_kernel(fresh, cotangent, decay_col, factor_row, count):
@@ -120,19 +127,20 @@
 
 def fixup_kernel(fresh, cotangent, decay_full, carries):
     col_count, rows, channel_count = fresh.shape
-    count, _, part, _ = carries.shape
+    count = carries.shape[0]
+    part = rows // count
 
     def body(fresh_ref, weight_ref, decay_ref, carry_ref, grad_ref, prod_ref):
         for chunk in range(count):
             span = pl.ds(chunk * part, part)
-            grad = carry_ref[chunk, 1]
+            grad = carry_ref[chunk, pl.ds(part, part), :]
             grads = [None] * col_count
             for column in reversed(range(col_count)):
                 grad = weight_ref[column, span, :] + grad
                 grads[column] = grad
                 grad_ref[column, span, :] = grad
                 grad = decay_ref[column, span, :] * grad
-            state = carry_ref[chunk, 0]
+            state = carry_ref[chunk, pl.ds(0, part), :]
             for column in range(col_count):
                 prod_ref[column, span, :] = grads[column] * state
                 state = decay_ref[column, span, :] * state + fresh_ref[column, span, :]
@@ -161,7 +169,7 @@
     factor_row = jnp.pad(factor, ((0, 0), (0, channel_count - part)))
     payload = summary_kernel(fresh_c, weight_c, decay_c, factor_row, count)
     got = lax.all_to_all(payload, "col", 0, 0, tiled=True)
-    carries = carry_kernel(got[:, :part], got[:, part : 2 * part], got[:, 2 * part, :part][..., None])
+    carries = carry_kernel(got, part)
     ret = lax.all_to_all(carries, "col", 0, 0, tiled=True)
     grads, gates = fixup_kernel(fresh_c, weight_c, decay_c, ret)
     grads = jnp.swapaxes(grads.reshape(col_count, row_count, flat_rows, channel_count), 0, 1)

time: 107 us -> 102 us (0.953)
  local copies, waits for them, and re-layouts: 11.7 us -> 7.35 us
    pallas_call x1 -> x0, local copies, waits for them, and re-layouts: 2.32 us -> none  [carry_kernel(): pl.pallas_call(body, out_shape=jax.ShapeDtypeStruct((count, 2, part, chan...]
    unnamed x18 -> x20, local copies, waits for them, and re-layouts: 3.07 us -> 3.91 us
where the time goes in v8:
time: 102 us; the launch traced here: 101 us
  blocking collectives  32.8 us (32%)
  waiting for transfers between devices  24.8 us (24%)
  starting transfers between devices  18.6 us (18%)
  Pallas kernels  12.9 us (13%)
  local copies, waits for them, and re-layouts  7.35 us (7%)
  other arithmetic  2.76 us (3%)
  matrix products  1.47 us (1%)
    all_to_all x1, blocking collectives, chain_scan(): got = lax.all_to_all(payload, 'col', 0, 0, tiled=True)  32.8 us
    all_to_all x1, waiting for transfers between devices, chain_scan(): ret = lax.all_to_all(carries, 'col', 0, 0, tiled=True)  14.8 us
    ppermute x2, starting transfers between devices, from_behind(): lax.ppermute(value, axis, [(source, source + steps) for source in range(i...  11.1 us
    ppermute x2, waiting for transfers between devices, from_behind(): lax.ppermute(value, axis, [(source, source + steps) for source in range(i...  9.92 us
    all_to_all x1, starting transfers between devices, chain_scan(): ret = lax.all_to_all(carries, 'col', 0, 0, tiled=True)  7.52 us
    pallas_call x1, Pallas kernels, backward_kernel(): pl.pallas_call(body, in_specs=[smem, smem, smem, vmem, vmem, vmem], out_s...  5.34 us
    unnamed x20, local copies, waits for them, and re-layouts  3.91 us
    pallas_call x1, Pallas kernels, fixup_kernel(): pl.pallas_call(body, out_shape=(jax.ShapeDtypeStruct((col_count, rows, ch...  2.88 us
  transfers between devices with their start and end apart: 3, of which 3 were waited for; matrix products, arithmetic and copies ran while one was open for 3% of the time, Pallas kernels for 0%

profile of v8, /device:TPU:17, one launch (start us, length us, event | category | flops | bytes accessed | tf_op | source)
XLA Modules:
  0.0 101.4 jit_solution(5974329071595988789)
XLA Ops:
  0.6 0.0 copy-start.6
  0.6 3.8 %collective-permute-start = (bf16[2,5,128,128]{3,2,1,0:T(8,128)(2,1)}, bf16[2,5,128,128]{3,2,1,0:T(8,128)(2,1)S(1)}, u32[]{:S(2)}, u32[]{:S(2)}) collective-permute-start(bf16[2,5,128,128]{3,2,1,0:T(8,128)(2,1)} %bitcast.37), channel_id=1, source_target_pairs={{0,32},{32,64},{64,96},{96,128},{128,160},{160,192},{192,224},{224... | collective-permute-start | bytes 983048 | tf_op jit(solution)/shard_map/ppermute | solution.py:12
  4.4 0.0 copy-done.6
  4.5 0.1 reduce_prod.12
  4.6 0.6 pad.4.factor_ref
  5.2 0.0 copy-start.9
  5.2 0.7 copy-done.9
  5.8 0.1 iota_compare_fusion.2
  5.9 2.8 %collective-permute-done = bf16[2,5,128,128]{3,2,1,0:T(8,128)(2,1)S(1)} collective-permute-done((bf16[2,5,128,128]{3,2,1,0:T(8,128)(2,1)}, bf16[2,5,128,128]{3,2,1,0:T(8,128)(2,1)S(1)}, u32[]{:S(2)}, u32[]{:S(2)}) %collective-permute-start) | collective-permute-done | bytes 327712 | tf_op jit(solution)/shard_map/ppermute | solution.py:12
  8.8 0.0 copy-start
  8.8 0.0 copy-start.7
  8.8 0.7 copy-done.7
  9.5 0.0 copy-start.3
  9.5 0.4 convolution_convert_fusion
  9.9 0.0 copy-done
  9.9 0.7 copy-done.3
  10.5 0.5 convolution_bitcast_fusion
  11.0 0.4 copy.17
  11.4 0.0 copy-start.8
  11.5 0.7 copy-done.8
  12.1 0.0 copy-start.5
  12.1 0.6 fusion.5
  12.7 0.4 copy-done.5
  13.1 1.0 bitcast_add_fusion
  14.1 1.1 %broadcast_in_dim.5.decay_ref = f32[2,640,128]{2,1,0:T(8,128)} broadcast(f32[2,640]{1,0:T(2,128)S(1)} %bitcast.38), dimensions={0,1} | broadcast | bytes 660480 | tf_op jit(solution)/shard_map/broadcast_in_dim | solution.py:167
  15.2 2.5 %shard_map.103 = f32[32,41,128]{2,1,0:T(8,128)} custom-call(f32[2,640,128]{2,1,0:T(8,128)} %bitcast.30, f32[2,640,128]{2,1,0:T(8,128)} %bitcast.32, f32[2,640,128]{2,1,0:T(8,128)} %broadcast_in_dim.5.decay_ref, f32[32,128]{1,0:T(8,128)} %pad.4.factor_ref), custom_call_target="tpu_custom_call" | custom-call | tf_op jit(solution)/shard_map/pallas_call | solution.py:122
  17.7 32.8 %all_to_all.10.got_ref = f32[32,41,128]{2,1,0:T(8,128)} all-to-all(f32[32,41,128]{2,1,0:T(8,128)} %shard_map.103), channel_id=1, replica_groups=mesh['row'=16,'col'=32] {'col'}, dimensions={0} | all-to-all | bytes 1343488 | tf_op jit(solution)/shard_map/all_to_all | solution.py:171
  50.4 2.2 %shard_map.104 = f32[32,40,128]{2,1,0:T(8,128)} custom-call(f32[32,41,128]{2,1,0:T(8,128)} %all_to_all.10.got_ref), custom_call_target="tpu_custom_call" | custom-call | tf_op jit(solution)/shard_map/pallas_call | solution.py:98
  52.6 7.5 %all-to-all-start.1 = ((f32[32,40,128]{2,1,0:T(8,128)}), f32[32,40,128]{2,1,0:T(8,128)S(1)}, u32[]{:S(2)}, u32[]{:S(2)}) async-start(f32[32,40,128]{2,1,0:T(8,128)} %shard_map.104), calls=%async_computation.1 | async-start | bytes 1310720 | tf_op jit(solution)/shard_map/all_to_all | solution.py:173
  60.2 0.6 reshape.79.src_ref
  60.8 0.7 reshape.80.dst_ref
  61.4 14.8 %all-to-all-done.1.carry_ref = f32[32,40,128]{2,1,0:T(8,128)S(1)} async-done(((f32[32,40,128]{2,1,0:T(8,128)}), f32[32,40,128]{2,1,0:T(8,128)S(1)}, u32[]{:S(2)}, u32[]{:S(2)}) %all-to-all-start.1) | async-done | bytes 655392 | tf_op jit(solution)/shard_map/all_to_all | solution.py:173
  76.2 0.0 copy-start.1
  76.2 0.8 copy-done.1
  77.1 2.9 %shard_map.105 = (f32[2,640,128]{2,1,0:T(8,128)}, f32[2,640,128]{2,1,0:T(8,128)}) custom-call(f32[2,640,128]{2,1,0:T(8,128)} %bitcast.31, f32[2,640,128]{2,1,0:T(8,128)} %bitcast.33, f32[2,640,128]{2,1,0:T(8,128)} %broadcast_in_dim.5.decay_ref, f32[32,40,128]{2,1,0:T(8,128)} %copy-done.1), custom_call_target="tpu_custom_call" | custom-call | tf_op jit(solution)/shard_map/pallas_call | solution.py:148
  80.0 0.0 copy-start.4
  80.0 5.3 %shard_map.106 = (bf16[2,8,128,128]{3,2,1,0:T(8,128)(2,1)}, bf16[2,5,128,128]{3,2,1,0:T(8,128)(2,1)}) custom-call(s32[16]{0:T(128)} %reshape.79.src_ref, s32[16]{0:T(128)} %reshape.80.dst_ref, s32[2]{0:T(128)} %bitcast.42, bf16[2,8,128,128]{3,2,1,0:T(8,128)(2,1)} %bitcast.36, bf16[2,5,128,128]{3,2,1,0:T(8,128)(2,1)} %copy-done, f32[2,5,128,128]{3,2,1,0:T(8,128)} %bitcast.34), custom_call_target="tpu_custom_call" | custom-call | tf_op jit(solution)/shard_map/pallas_call | solution.py:66
  85.3 0.0 copy-start.2
  85.3 7.3 %collective-permute-start.1 = (bf16[2,5,128,128]{3,2,1,0:T(8,128)(2,1)}, bf16[2,5,128,128]{3,2,1,0:T(8,128)(2,1)S(1)}, u32[]{:S(2)}, u32[]{:S(2)}) collective-permute-start(bf16[2,5,128,128]{3,2,1,0:T(8,128)(2,1)} %get-tuple-element.9), channel_id=1, source_target_pairs={{32,0},{64,32},{96,64},{128,96},{160,128},{192,160},{224,192},{256... | collective-permute-start | bytes 983048 | tf_op jit(solution)/shard_map/ppermute | solution.py:12
  92.6 0.0 copy-done.4
  92.6 0.8 reduce_sum.9
  93.5 7.1 %collective-permute-done.1 = bf16[2,5,128,128]{3,2,1,0:T(8,128)(2,1)S(1)} collective-permute-done((bf16[2,5,128,128]{3,2,1,0:T(8,128)(2,1)}, bf16[2,5,128,128]{3,2,1,0:T(8,128)(2,1)S(1)}, u32[]{:S(2)}, u32[]{:S(2)}) %collective-permute-start.1) | collective-permute-done | bytes 327712 | tf_op jit(solution)/shard_map/ppermute | solution.py:12
  100.6 0.0 copy-done.2
  100.6 0.8 fusion.2
  (2 shorter events, 0.1 us)
Async XLA Ops:
  0.6 3.8 %copy-start.6 = (f32[1,2,5,128]{3,1,2,0:T(2,128)S(1)}, f32[1,2,5,128]{3,1,2,0:T(2,128)}, u32[]{:S(2)}) copy-start(f32[1,2,5,128]{3,1,2,0:T(2,128)} %param.14) | copy-start | bytes 15364
  0.6 8.1 %collective-permute-start = (bf16[2,5,128,128]{3,2,1,0:T(8,128)(2,1)}, bf16[2,5,128,128]{3,2,1,0:T(8,128)(2,1)S(1)}, u32[]{:S(2)}, u32[]{:S(2)}) collective-permute-start(bf16[2,5,128,128]{3,2,1,0:T(8,128)(2,1)} %bitcast.37), channel_id=1, source_target_pairs={{0,32},{32,64},{64,96},{96,128},{128,160},{160,192},{192,224},{224... | collective-permute-start | bytes 983048 | tf_op jit(solution)/shard_map/ppermute | solution.py:12
  5.2 0.7 copy-start.9
  8.8 1.1 %copy-start = (bf16[2,5,128,128]{3,2,1,0:T(8,128)(2,1)}, bf16[2,5,128,128]{3,2,1,0:T(8,128)(2,1)S(1)}, u32[]{:S(2)}) copy-start(bf16[2,5,128,128]{3,2,1,0:T(8,128)(2,1)S(1)} %broadcast_select_fusion.above_ref) | copy-start | bytes 983044
  8.8 0.7 copy-start.7
  9.5 1.0 %copy-start.3 = (bf16[1,2,8,128,128]{4,3,2,1,0:T(8,128)(2,1)S(1)}, bf16[1,2,8,128,128]{4,3,2,1,0:T(8,128)(2,1)}, u32[]{:S(2)}) copy-start(bf16[1,2,8,128,128]{4,3,2,1,0:T(8,128)(2,1)} %param.8) | copy-start | bytes 1572868
  11.4 0.7 copy-start.8
  12.1 1.0 copy-start.5
  52.6 23.6 %all-to-all-start.1 = ((f32[32,40,128]{2,1,0:T(8,128)}), f32[32,40,128]{2,1,0:T(8,128)S(1)}, u32[]{:S(2)}, u32[]{:S(2)}) async-start(f32[32,40,128]{2,1,0:T(8,128)} %shard_map.104), calls=%async_computation.1 | async-start | bytes 1310720 | tf_op jit(solution)/shard_map/all_to_all | solution.py:173
  76.2 0.8 copy-start.1
  80.0 12.6 %copy-start.4 = (f32[2,640,128]{2,1,0:T(8,128)S(1)}, f32[2,640,128]{2,1,0:T(8,128)}, u32[]{:S(2)}) copy-start(f32[2,640,128]{2,1,0:T(8,128)} %get-tuple-element.10) | copy-start | bytes 1966084
  85.3 15.3 %copy-start.2 = (f32[2,640,128]{2,1,0:T(8,128)S(1)}, f32[2,640,128]{2,1,0:T(8,128)}, u32[]{:S(2)}) copy-start(f32[2,640,128]{2,1,0:T(8,128)} %get-tuple-element.7) | copy-start | bytes 1966084
  85.3 15.2 %collective-permute-start.1 = (bf16[2,5,128,128]{3,2,1,0:T(8,128)(2,1)}, bf16[2,5,128,128]{3,2,1,0:T(8,128)(2,1)S(1)}, u32[]{:S(2)}, u32[]{:S(2)}) collective-permute-start(bf16[2,5,128,128]{3,2,1,0:T(8,128)(2,1)} %get-tuple-element.9), channel_id=1, source_target_pairs={{32,0},{64,32},{96,64},{128,96},{160,128},{192,160},{224,192},{256... | collective-permute-start | bytes 983048 | tf_op jit(solution)/shard_map/ppermute | solution.py:12

commit v9 on v8

--- a/solution.py
+++ b/solution.py
@@ -12,24 +12,33 @@
     return lax.ppermute(value, axis, [(source, source + steps) for source in range(initial, last)])
 
 
-def slot_tables(sources, targets, counts, sector_count):
-    active_slot_list = lax.broadcasted_iota(jnp.int32, sources.shape, 2) < counts[:, :, None]
-    sector_ids = lax.broadcasted_iota(jnp.int32, sources.shape + (sector_count,), 3)
-    src_pick = sources[..., None] == sector_ids
-    dst_pick = targets[..., None] == sector_ids
-    return (src_pick, dst_pick, active_slot_list)
-
-
-def forward_blocks(blocks, above_env, src_pick, dst_pick, active_slot_list):
-    placed = (dst_pick & active_slot_list[..., None]).astype(jnp.float32)
-    src_bf = src_pick.astype(jnp.bfloat16)
-    gathered = jnp.einsum(
-        "rckn,rcnbj->rckbj", src_bf, above_env, preferred_element_type=jnp.float32
-    ).astype(jnp.bfloat16)
-    products = jnp.einsum(
-        "rckab,rckbj->rckaj", blocks, gathered, preferred_element_type=jnp.float32
-    )
-    return jnp.einsum("rckn,rckaj->rcnaj", placed, products, precision=lax.Precision.HIGHEST)
+def forward_kernel(blocks, above_env, environment, sources, targets, counts):
+    site_count, slot_count = blocks.shape[:2]
+    sector_count = above_env.shape[1]
+
+    def body(src_ref, dst_ref, cnt_ref, blocks_ref, above_ref, env_ref, fresh_ref):
+        for site in range(site_count):
+            fresh_ref[site] = env_ref[site].astype(jnp.float32)
+            for slot in range(slot_count):
+                place = site * slot_count + slot
+                source = jnp.clip(src_ref[place], 0, sector_count - 1)
+                target = jnp.clip(dst_ref[place], 0, sector_count - 1)
+                product = jnp.dot(
+                    blocks_ref[site, slot], above_ref[site, source], preferred_element_type=jnp.float32
+                )
+
+                @pl.when(slot < cnt_ref[site])
+                def _():
+                    fresh_ref[site, target] += product
+
+    smem = pl.BlockSpec(memory_space=pltpu.SMEM)
+    vmem = pl.BlockSpec(memory_space=pltpu.VMEM)
+    return pl.pallas_call(
+        body,
+        in_specs=[smem, smem, smem, vmem, vmem, vmem],
+        out_specs=vmem,
+        out_shape=jax.ShapeDtypeStruct(environment.shape, jnp.float32),
+    )(sources, targets, counts, blocks, above_env, environment)
 
 
 def backward_kernel(blocks, above_env, rounded, sources, targets, counts):
@@ -184,21 +193,27 @@
     upper_env = from_behind(bottom, "row", 1)
     upper_env = jnp.where(lax.axis_index("row") == 0, top_boundary, upper_env)
     above_env = jnp.concatenate([upper_env[None], environment[: row_count - 1]], 0)
-    src_pick, dst_pick, active_slot_list = slot_tables(sources, targets, counts, sector_count)
-    transferred = forward_blocks(blocks, above_env, src_pick, dst_pick, active_slot_list)
-    fresh = (environment.astype(jnp.float32) + transferred).reshape(
-        row_count, col_count, flat_rows, channel_count
-    )
+    site_count = row_count * col_count
+
+    def by_site(value):
+        return value.reshape((site_count,) + value.shape[2:])
+
+    fresh = forward_kernel(
+        by_site(blocks),
+        by_site(above_env),
+        by_site(environment),
+        sources.reshape(-1),
+        targets.reshape(-1),
+        counts.reshape(-1),
+    ).reshape(row_count, col_count, flat_rows, channel_count)
     decay_rows = decays.reshape(row_count, col_count, flat_rows)
     cotangent = weights.reshape(row_count, col_count, flat_rows, channel_count)
     condition_derivative, gate_grad = chain_scan(fresh, decay_rows, cotangent)
     condition_derivative = condition_derivative.reshape(environment.shape)
-    rounded = condition_derivative.astype(jnp.bfloat16)
-    site_count = row_count * col_count
     grad_blocks, returned = backward_kernel(
         blocks.reshape((site_count,) + blocks.shape[2:]),
         above_env.reshape((site_count,) + above_env.shape[2:]),
-        condition_derivative.reshape((site_count,) + rounded.shape[2:]),
+        condition_derivative.reshape((site_count,) + condition_derivative.shape[2:]),
         sources.reshape(-1),
         targets.reshape(-1),
         counts.reshape(-1),

time: 102 us -> 101 us (level)
  blocking collectives: 32.8 us -> 56.5 us
  waiting for transfers between devices: 24.8 us -> 8.72 us
  starting transfers between devices: 18.6 us -> 11.1 us
  Pallas kernels: 12.9 us -> 17.3 us
  local copies, waits for them, and re-layouts: 7.35 us -> 3.74 us
  matrix products: 1.47 us -> 0 us
    all_to_all x0 -> x1, blocking collectives: none -> 23.7 us  [chain_scan(): ret = lax.all_to_all(carries, 'col', 0, 0, tiled=True)]
    all_to_all x1 -> x0, waiting for transfers between devices: 14.8 us -> none  [chain_scan(): ret = lax.all_to_all(carries, 'col', 0, 0, tiled=True)]
    all_to_all x1 -> x0, starting transfers between devices: 7.52 us -> none  [chain_scan(): ret = lax.all_to_all(carries, 'col', 0, 0, tiled=True)]
    pallas_call x0 -> x1, Pallas kernels: none -> 4.45 us  [forward_kernel(): pl.pallas_call(body, in_specs=[smem, smem, smem, vmem, vmem, vmem], out_s...]
    unnamed x20 -> x10, local copies, waits for them, and re-layouts: 3.91 us -> 0.76 us
    dot_general x3 -> x0, matrix products: 1.47 us -> none  [the longest x1 0.59 us: forward_blocks(): jnp.einsum('rckn,rckaj->rcnaj', placed, products, precision=lax.Precision...]
    ppermute x2, waiting for transfers between devices: 9.92 us -> 8.72 us  [from_behind(): lax.ppermute(value, axis, [(source, source + steps) for source in range(i...]
  transfers between devices with their start and end apart: 3 -> 2, of which waited for: 3 -> 2; matrix products, arithmetic and copies ran while one was open for 3% -> 3% of each run, Pallas kernels for 0% -> 0%
where the time goes in v9:
time: 101 us; the launch traced here: 100 us
  blocking collectives  56.5 us (56%)
  Pallas kernels  17.3 us (17%)
  starting transfers between devices  11.1 us (11%)
  waiting for transfers between devices  8.72 us (9%)
  local copies, waits for them, and re-layouts  3.74 us (4%)
  other arithmetic  2.43 us (2%)
    all_to_all x1, blocking collectives, chain_scan(): got = lax.all_to_all(payload, 'col', 0, 0, tiled=True)  32.8 us
    all_to_all x1, blocking collectives, chain_scan(): ret = lax.all_to_all(carries, 'col', 0, 0, tiled=True)  23.7 us
    ppermute x2, starting transfers between devices, from_behind(): lax.ppermute(value, axis, [(source, source + steps) for source in range(i...  11.1 us
    ppermute x2, waiting for transfers between devices, from_behind(): lax.ppermute(value, axis, [(source, source + steps) for source in range(i...  8.72 us
    pallas_call x1, Pallas kernels, backward_kernel(): pl.pallas_call(body, in_specs=[smem, smem, smem, vmem, vmem, vmem], out_s...  5.34 us
    pallas_call x1, Pallas kernels, forward_kernel(): pl.pallas_call(body, in_specs=[smem, smem, smem, vmem, vmem, vmem], out_s...  4.45 us
    pallas_call x1, Pallas kernels, fixup_kernel(): pl.pallas_call(body, out_shape=(jax.ShapeDtypeStruct((col_count, rows, ch...  2.88 us
    pallas_call x1, Pallas kernels, summary_kernel(): pl.pallas_call(body, out_shape=jax.ShapeDtypeStruct((count, 2 * part + 1,...  2.49 us
  transfers between devices with their start and end apart: 2, of which 2 were waited for; matrix products, arithmetic and copies ran while one was open for 3% of the time, Pallas kernels for 0%

profile of v9, /device:TPU:17, one launch (start us, length us, event | category | flops | bytes accessed | tf_op | source)
XLA Modules:
  0.0 100.4 jit_solution(6394690946650880580)
XLA Ops:
  0.6 3.8 %collective-permute-start = (bf16[2,5,128,128]{3,2,1,0:T(8,128)(2,1)}, bf16[2,5,128,128]{3,2,1,0:T(8,128)(2,1)S(1)}, u32[]{:S(2)}, u32[]{:S(2)}) collective-permute-start(bf16[2,5,128,128]{3,2,1,0:T(8,128)(2,1)} %bitcast.19), channel_id=1, source_target_pairs={{0,32},{32,64},{64,96},{96,128},{128,160},{160,192},{192,224},{224... | collective-permute-start | bytes 983048 | tf_op jit(solution)/shard_map/ppermute | solution.py:12
  4.4 0.0 copy-start.3
  4.4 0.0 copy-start.2
  4.4 0.7 copy-done.3
  5.1 0.0 copy-start.4
  5.1 0.6 reshape.32.src_ref
  5.7 0.1 copy-done.4
  5.8 0.6 reshape.33.dst_ref
  6.4 0.0 copy-done.2
  6.4 0.1 reduce_prod.12
  6.5 0.6 pad.4.factor_ref
  7.1 1.6 %collective-permute-done = bf16[2,5,128,128]{3,2,1,0:T(8,128)(2,1)S(1)} collective-permute-done((bf16[2,5,128,128]{3,2,1,0:T(8,128)(2,1)}, bf16[2,5,128,128]{3,2,1,0:T(8,128)(2,1)S(1)}, u32[]{:S(2)}, u32[]{:S(2)}) %collective-permute-start) | collective-permute-done | bytes 327712 | tf_op jit(solution)/shard_map/ppermute | solution.py:12
  8.7 0.8 broadcast_select_fusion.above_ref
  9.5 4.4 %shard_map.103 = f32[2,5,128,128]{3,2,1,0:T(8,128)} custom-call(s32[16]{0:T(128)} %reshape.32.src_ref, s32[16]{0:T(128)} %reshape.33.dst_ref, s32[2]{0:T(128)} %bitcast.23, bf16[2,8,128,128]{3,2,1,0:T(8,128)(2,1)} %bitcast.17, bf16[2,5,128,128]{3,2,1,0:T(8,128)(2,1)} %broadcast_select_fusion.above_ref, bf16[2,5,128,128]{3,2,1,0:T(8,128)(2,1)} %bitcast.20), custom_call_target="tpu_custom_call" | custom-call | tf_op jit(solution)/shard_map/pallas_call | solution.py:36
  13.9 1.1 %broadcast_in_dim.9.decay_ref = f32[2,640,128]{2,1,0:T(8,128)} broadcast(f32[2,640]{1,0:T(2,128)S(1)} %bitcast.21), dimensions={0,1} | broadcast | bytes 660480 | tf_op jit(solution)/shard_map/broadcast_in_dim | solution.py:176
  15.0 2.5 %shard_map.104 = f32[32,41,128]{2,1,0:T(8,128)} custom-call(f32[2,640,128]{2,1,0:T(8,128)} %bitcast.11, f32[2,640,128]{2,1,0:T(8,128)} %bitcast.13, f32[2,640,128]{2,1,0:T(8,128)} %broadcast_in_dim.9.decay_ref, f32[32,128]{1,0:T(8,128)} %pad.4.factor_ref), custom_call_target="tpu_custom_call" | custom-call | tf_op jit(solution)/shard_map/pallas_call | solution.py:131
  17.5 32.8 %all_to_all.10.got_ref = f32[32,41,128]{2,1,0:T(8,128)} all-to-all(f32[32,41,128]{2,1,0:T(8,128)} %shard_map.104), channel_id=1, replica_groups=mesh['row'=16,'col'=32] {'col'}, dimensions={0} | all-to-all | bytes 1343488 | tf_op jit(solution)/shard_map/all_to_all | solution.py:180
  50.3 2.2 %shard_map.105 = f32[32,40,128]{2,1,0:T(8,128)} custom-call(f32[32,41,128]{2,1,0:T(8,128)} %all_to_all.10.got_ref), custom_call_target="tpu_custom_call" | custom-call | tf_op jit(solution)/shard_map/pallas_call | solution.py:107
  52.4 23.7 %all_to_all.11.carry_ref = f32[32,40,128]{2,1,0:T(8,128)} all-to-all(f32[32,40,128]{2,1,0:T(8,128)} %shard_map.105), channel_id=1, replica_groups=mesh['row'=16,'col'=32] {'col'}, dimensions={0} | all-to-all | bytes 1310720 | tf_op jit(solution)/shard_map/all_to_all | solution.py:182
  76.2 2.9 %shard_map.106 = (f32[2,640,128]{2,1,0:T(8,128)}, f32[2,640,128]{2,1,0:T(8,128)}) custom-call(f32[2,640,128]{2,1,0:T(8,128)} %bitcast.12, f32[2,640,128]{2,1,0:T(8,128)} %bitcast.14, f32[2,640,128]{2,1,0:T(8,128)} %broadcast_in_dim.9.decay_ref, f32[32,40,128]{2,1,0:T(8,128)} %all_to_all.11.carry_ref), custom_call_target="tpu_custom_call" | custom-call | tf_op jit(solution)/shard_map/pallas_call | solution.py:157
  79.0 0.0 copy-start.1
  79.0 5.3 %shard_map.107 = (bf16[2,8,128,128]{3,2,1,0:T(8,128)(2,1)}, bf16[2,5,128,128]{3,2,1,0:T(8,128)(2,1)}) custom-call(s32[16]{0:T(128)} %reshape.32.src_ref, s32[16]{0:T(128)} %reshape.33.dst_ref, s32[2]{0:T(128)} %bitcast.24, bf16[2,8,128,128]{3,2,1,0:T(8,128)(2,1)} %bitcast.18, bf16[2,5,128,128]{3,2,1,0:T(8,128)(2,1)} %broadcast_select_fusion.above_ref, ...), custom_call_target="tpu_custom_call" | custom-call | tf_op jit(solution)/shard_map/pallas_call | solution.py:75
  84.4 0.0 copy-start
  84.4 7.3 %collective-permute-start.1 = (bf16[2,5,128,128]{3,2,1,0:T(8,128)(2,1)}, bf16[2,5,128,128]{3,2,1,0:T(8,128)(2,1)S(1)}, u32[]{:S(2)}, u32[]{:S(2)}) collective-permute-start(bf16[2,5,128,128]{3,2,1,0:T(8,128)(2,1)} %get-tuple-element.9), channel_id=1, source_target_pairs={{32,0},{64,32},{96,64},{128,96},{160,128},{192,160},{224,192},{256... | collective-permute-start | bytes 983048 | tf_op jit(solution)/shard_map/ppermute | solution.py:12
  91.7 0.0 copy-done.1
  91.7 0.8 reduce_sum.9
  92.5 7.1 %collective-permute-done.1 = bf16[2,5,128,128]{3,2,1,0:T(8,128)(2,1)S(1)} collective-permute-done((bf16[2,5,128,128]{3,2,1,0:T(8,128)(2,1)}, bf16[2,5,128,128]{3,2,1,0:T(8,128)(2,1)S(1)}, u32[]{:S(2)}, u32[]{:S(2)}) %collective-permute-start.1) | collective-permute-done | bytes 327712 | tf_op jit(solution)/shard_map/ppermute | solution.py:12
  99.6 0.0 copy-done
  99.6 0.8 fusion
  (1 shorter events, 0.0 us)
Async XLA Ops:
  0.6 8.1 %collective-permute-start = (bf16[2,5,128,128]{3,2,1,0:T(8,128)(2,1)}, bf16[2,5,128,128]{3,2,1,0:T(8,128)(2,1)S(1)}, u32[]{:S(2)}, u32[]{:S(2)}) collective-permute-start(bf16[2,5,128,128]{3,2,1,0:T(8,128)(2,1)} %bitcast.19), channel_id=1, source_target_pairs={{0,32},{32,64},{64,96},{96,128},{128,160},{160,192},{192,224},{224... | collective-permute-start | bytes 983048 | tf_op jit(solution)/shard_map/ppermute | solution.py:12
  4.4 0.7 copy-start.3
  4.4 2.0 %copy-start.2 = (f32[1,2,5,128]{3,1,2,0:T(2,128)S(1)}, f32[1,2,5,128]{3,1,2,0:T(2,128)}, u32[]{:S(2)}) copy-start(f32[1,2,5,128]{3,1,2,0:T(2,128)} %param.14) | copy-start | bytes 15364
  5.1 0.7 copy-start.4
  79.0 12.6 %copy-start.1 = (f32[2,640,128]{2,1,0:T(8,128)S(1)}, f32[2,640,128]{2,1,0:T(8,128)}, u32[]{:S(2)}) copy-start(f32[2,640,128]{2,1,0:T(8,128)} %get-tuple-element.10) | copy-start | bytes 1966084
  84.4 15.3 %copy-start = (f32[2,640,128]{2,1,0:T(8,128)S(1)}, f32[2,640,128]{2,1,0:T(8,128)}, u32[]{:S(2)}) copy-start(f32[2,640,128]{2,1,0:T(8,128)} %get-tuple-element.7) | copy-start | bytes 1966084
  84.4 15.3 %collective-permute-start.1 = (bf16[2,5,128,128]{3,2,1,0:T(8,128)(2,1)}, bf16[2,5,128,128]{3,2,1,0:T(8,128)(2,1)S(1)}, u32[]{:S(2)}, u32[]{:S(2)}) collective-permute-start(bf16[2,5,128,128]{3,2,1,0:T(8,128)(2,1)} %get-tuple-element.9), channel_id=1, source_target_pairs={{32,0},{64,32},{96,64},{128,96},{160,128},{192,160},{224,192},{256... | collective-permute-start | bytes 983048 | tf_op jit(solution)/shard_map/ppermute | solution.py:12

commit v10 on v9

--- a/solution.py
+++ b/solution.py
@@ -26,10 +26,7 @@
                 product = jnp.dot(
                     blocks_ref[site, slot], above_ref[site, source], preferred_element_type=jnp.float32
                 )
-
-                @pl.when(slot < cnt_ref[site])
-                def _():
-                    fresh_ref[site, target] += product
+                fresh_ref[site, target] += jnp.where(slot < cnt_ref[site], product, 0.0)
 
     smem = pl.BlockSpec(memory_space=pltpu.SMEM)
     vmem = pl.BlockSpec(memory_space=pltpu.VMEM)
@@ -63,10 +60,7 @@
                     blocks_ref[site, slot], picked, (((0,), (0,)), ((), ())),
                     preferred_element_type=jnp.float32,
                 )
-
-                @pl.when(live)
-                def _():
-                    acc_ref[source] += contrib
+                acc_ref[source] += jnp.where(live, contrib, 0.0)
 
             ret_ref[site] = acc_ref[...].astype(ret_ref.dtype)
 

time: 101 us -> 96.7 us (0.957)
  Pallas kernels: 17.3 us -> 13 us
    pallas_call x1, Pallas kernels: 5.34 us -> 3.04 us  [backward_kernel(): pl.pallas_call(body, in_specs=[smem, smem, smem, vmem, vmem, vmem], out_s...]
    pallas_call x1, Pallas kernels: 4.45 us -> 2.4 us  [forward_kernel(): pl.pallas_call(body, in_specs=[smem, smem, smem, vmem, vmem, vmem], out_s...]
where the time goes in v10:
time: 96.7 us; the launch traced here: 96.1 us
  blocking collectives  56.5 us (58%)
  Pallas kernels  13 us (13%)
  starting transfers between devices  11.1 us (11%)
  waiting for transfers between devices  8.73 us (9%)
  local copies, waits for them, and re-layouts  3.74 us (4%)
  other arithmetic  2.43 us (3%)
    all_to_all x1, blocking collectives, chain_scan(): got = lax.all_to_all(payload, 'col', 0, 0, tiled=True)  32.8 us
    all_to_all x1, blocking collectives, chain_scan(): ret = lax.all_to_all(carries, 'col', 0, 0, tiled=True)  23.7 us
    ppermute x2, starting transfers between devices, from_behind(): lax.ppermute(value, axis, [(source, source + steps) for source in range(i...  11.1 us
    ppermute x2, waiting for transfers between devices, from_behind(): lax.ppermute(value, axis, [(source, source + steps) for source in range(i...  8.73 us
    pallas_call x1, Pallas kernels, backward_kernel(): pl.pallas_call(body, in_specs=[smem, smem, smem, vmem, vmem, vmem], out_s...  3.04 us
    pallas_call x1, Pallas kernels, fixup_kernel(): pl.pallas_call(body, out_shape=(jax.ShapeDtypeStruct((col_count, rows, ch...  2.88 us
    pallas_call x1, Pallas kernels, summary_kernel(): pl.pallas_call(body, out_shape=jax.ShapeDtypeStruct((count, 2 * part + 1,...  2.49 us
    pallas_call x1, Pallas kernels, forward_kernel(): pl.pallas_call(body, in_specs=[smem, smem, smem, vmem, vmem, vmem], out_s...  2.4 us
  transfers between devices with their start and end apart: 2, of which 2 were waited for; matrix products, arithmetic and copies ran while one was open for 3% of the time, Pallas kernels for 0%

profile of v10, /device:TPU:17, one launch (start us, length us, event | category | flops | bytes accessed | tf_op | source)
XLA Modules:
  0.0 96.1 jit_solution(11789963454115701157)
XLA Ops:
  0.6 3.8 %collective-permute-start = (bf16[2,5,128,128]{3,2,1,0:T(8,128)(2,1)}, bf16[2,5,128,128]{3,2,1,0:T(8,128)(2,1)S(1)}, u32[]{:S(2)}, u32[]{:S(2)}) collective-permute-start(bf16[2,5,128,128]{3,2,1,0:T(8,128)(2,1)} %bitcast.19), channel_id=1, source_target_pairs={{0,32},{32,64},{64,96},{96,128},{128,160},{160,192},{192,224},{224... | collective-permute-start | bytes 983048 | tf_op jit(solution)/shard_map/ppermute | solution.py:12
  4.4 0.0 copy-start.3
  4.4 0.0 copy-start.2
  4.4 0.7 copy-done.3
  5.1 0.0 copy-start.4
  5.1 0.6 reshape.32.src_ref
  5.7 0.1 copy-done.4
  5.8 0.6 reshape.33.dst_ref
  6.4 0.0 copy-done.2
  6.4 0.1 reduce_prod.12
  6.5 0.6 pad.4.factor_ref
  7.1 1.6 %collective-permute-done = bf16[2,5,128,128]{3,2,1,0:T(8,128)(2,1)S(1)} collective-permute-done((bf16[2,5,128,128]{3,2,1,0:T(8,128)(2,1)}, bf16[2,5,128,128]{3,2,1,0:T(8,128)(2,1)S(1)}, u32[]{:S(2)}, u32[]{:S(2)}) %collective-permute-start) | collective-permute-done | bytes 327712 | tf_op jit(solution)/shard_map/ppermute | solution.py:12
  8.7 0.8 broadcast_select_fusion.above_ref
  9.5 2.4 %shard_map.103 = f32[2,5,128,128]{3,2,1,0:T(8,128)} custom-call(s32[16]{0:T(128)} %reshape.32.src_ref, s32[16]{0:T(128)} %reshape.33.dst_ref, s32[2]{0:T(128)} %bitcast.23, bf16[2,8,128,128]{3,2,1,0:T(8,128)(2,1)} %bitcast.17, bf16[2,5,128,128]{3,2,1,0:T(8,128)(2,1)} %broadcast_select_fusion.above_ref, bf16[2,5,128,128]{3,2,1,0:T(8,128)(2,1)} %bitcast.20), custom_call_target="tpu_custom_call" | custom-call | tf_op jit(solution)/shard_map/pallas_call | solution.py:33
  11.9 1.1 %broadcast_in_dim.9.decay_ref = f32[2,640,128]{2,1,0:T(8,128)} broadcast(f32[2,640]{1,0:T(2,128)S(1)} %bitcast.21), dimensions={0,1} | broadcast | bytes 660480 | tf_op jit(solution)/shard_map/broadcast_in_dim | solution.py:170
  13.0 2.5 %shard_map.104 = f32[32,41,128]{2,1,0:T(8,128)} custom-call(f32[2,640,128]{2,1,0:T(8,128)} %bitcast.11, f32[2,640,128]{2,1,0:T(8,128)} %bitcast.13, f32[2,640,128]{2,1,0:T(8,128)} %broadcast_in_dim.9.decay_ref, f32[32,128]{1,0:T(8,128)} %pad.4.factor_ref), custom_call_target="tpu_custom_call" | custom-call | tf_op jit(solution)/shard_map/pallas_call | solution.py:125
  15.5 32.8 %all_to_all.10.got_ref = f32[32,41,128]{2,1,0:T(8,128)} all-to-all(f32[32,41,128]{2,1,0:T(8,128)} %shard_map.104), channel_id=1, replica_groups=mesh['row'=16,'col'=32] {'col'}, dimensions={0} | all-to-all | bytes 1343488 | tf_op jit(solution)/shard_map/all_to_all | solution.py:174
  48.2 2.2 %shard_map.105 = f32[32,40,128]{2,1,0:T(8,128)} custom-call(f32[32,41,128]{2,1,0:T(8,128)} %all_to_all.10.got_ref), custom_call_target="tpu_custom_call" | custom-call | tf_op jit(solution)/shard_map/pallas_call | solution.py:101
  50.4 23.7 %all_to_all.11.carry_ref = f32[32,40,128]{2,1,0:T(8,128)} all-to-all(f32[32,40,128]{2,1,0:T(8,128)} %shard_map.105), channel_id=1, replica_groups=mesh['row'=16,'col'=32] {'col'}, dimensions={0} | all-to-all | bytes 1310720 | tf_op jit(solution)/shard_map/all_to_all | solution.py:176
  74.1 2.9 %shard_map.106 = (f32[2,640,128]{2,1,0:T(8,128)}, f32[2,640,128]{2,1,0:T(8,128)}) custom-call(f32[2,640,128]{2,1,0:T(8,128)} %bitcast.12, f32[2,640,128]{2,1,0:T(8,128)} %bitcast.14, f32[2,640,128]{2,1,0:T(8,128)} %broadcast_in_dim.9.decay_ref, f32[32,40,128]{2,1,0:T(8,128)} %all_to_all.11.carry_ref), custom_call_target="tpu_custom_call" | custom-call | tf_op jit(solution)/shard_map/pallas_call | solution.py:151
  77.0 0.0 copy-start.1
  77.0 3.0 %shard_map.107 = (bf16[2,8,128,128]{3,2,1,0:T(8,128)(2,1)}, bf16[2,5,128,128]{3,2,1,0:T(8,128)(2,1)}) custom-call(s32[16]{0:T(128)} %reshape.32.src_ref, s32[16]{0:T(128)} %reshape.33.dst_ref, s32[2]{0:T(128)} %bitcast.24, bf16[2,8,128,128]{3,2,1,0:T(8,128)(2,1)} %bitcast.18, bf16[2,5,128,128]{3,2,1,0:T(8,128)(2,1)} %broadcast_select_fusion.above_ref, ...), custom_call_target="tpu_custom_call" | custom-call | tf_op jit(solution)/shard_map/pallas_call | solution.py:69
  80.0 0.0 copy-start
  80.0 7.3 %collective-permute-start.1 = (bf16[2,5,128,128]{3,2,1,0:T(8,128)(2,1)}, bf16[2,5,128,128]{3,2,1,0:T(8,128)(2,1)S(1)}, u32[]{:S(2)}, u32[]{:S(2)}) collective-permute-start(bf16[2,5,128,128]{3,2,1,0:T(8,128)(2,1)} %get-tuple-element.9), channel_id=1, source_target_pairs={{32,0},{64,32},{96,64},{128,96},{160,128},{192,160},{224,192},{256... | collective-permute-start | bytes 983048 | tf_op jit(solution)/shard_map/ppermute | solution.py:12
  87.3 0.0 copy-done.1
  87.3 0.8 reduce_sum.9
  88.2 7.1 %collective-permute-done.1 = bf16[2,5,128,128]{3,2,1,0:T(8,128)(2,1)S(1)} collective-permute-done((bf16[2,5,128,128]{3,2,1,0:T(8,128)(2,1)}, bf16[2,5,128,128]{3,2,1,0:T(8,128)(2,1)S(1)}, u32[]{:S(2)}, u32[]{:S(2)}) %collective-permute-start.1) | collective-permute-done | bytes 327712 | tf_op jit(solution)/shard_map/ppermute | solution.py:12
  95.3 0.0 copy-done
  95.3 0.8 fusion
  (1 shorter events, 0.0 us)
Async XLA Ops:
  0.6 8.1 %collective-permute-start = (bf16[2,5,128,128]{3,2,1,0:T(8,128)(2,1)}, bf16[2,5,128,128]{3,2,1,0:T(8,128)(2,1)S(1)}, u32[]{:S(2)}, u32[]{:S(2)}) collective-permute-start(bf16[2,5,128,128]{3,2,1,0:T(8,128)(2,1)} %bitcast.19), channel_id=1, source_target_pairs={{0,32},{32,64},{64,96},{96,128},{128,160},{160,192},{192,224},{224... | collective-permute-start | bytes 983048 | tf_op jit(solution)/shard_map/ppermute | solution.py:12
  4.4 0.7 copy-start.3
  4.4 2.0 %copy-start.2 = (f32[1,2,5,128]{3,1,2,0:T(2,128)S(1)}, f32[1,2,5,128]{3,1,2,0:T(2,128)}, u32[]{:S(2)}) copy-start(f32[1,2,5,128]{3,1,2,0:T(2,128)} %param.14) | copy-start | bytes 15364
  5.1 0.7 copy-start.4
  77.0 10.3 %copy-start.1 = (f32[2,640,128]{2,1,0:T(8,128)S(1)}, f32[2,640,128]{2,1,0:T(8,128)}, u32[]{:S(2)}) copy-start(f32[2,640,128]{2,1,0:T(8,128)} %get-tuple-element.10) | copy-start | bytes 1966084
  80.0 15.3 %copy-start = (f32[2,640,128]{2,1,0:T(8,128)S(1)}, f32[2,640,128]{2,1,0:T(8,128)}, u32[]{:S(2)}) copy-start(f32[2,640,128]{2,1,0:T(8,128)} %get-tuple-element.7) | copy-start | bytes 1966084
  80.0 15.3 %collective-permute-start.1 = (bf16[2,5,128,128]{3,2,1,0:T(8,128)(2,1)}, bf16[2,5,128,128]{3,2,1,0:T(8,128)(2,1)S(1)}, u32[]{:S(2)}, u32[]{:S(2)}) collective-permute-start(bf16[2,5,128,128]{3,2,1,0:T(8,128)(2,1)} %get-tuple-element.9), channel_id=1, source_target_pairs={{32,0},{64,32},{96,64},{128,96},{160,128},{192,160},{224,192},{256... | collective-permute-start | bytes 983048 | tf_op jit(solution)/shard_map/ppermute | solution.py:12

commit v11 on v10

--- a/solution.py
+++ b/solution.py
@@ -12,37 +12,45 @@
     return lax.ppermute(value, axis, [(source, source + steps) for source in range(initial, last)])
 
 
-def forward_kernel(blocks, above_env, environment, sources, targets, counts):
+def forward_kernel(blocks, top_env, received_env, environment, decays, first, sources, targets, counts):
     site_count, slot_count = blocks.shape[:2]
-    sector_count = above_env.shape[1]
-
-    def body(src_ref, dst_ref, cnt_ref, blocks_ref, above_ref, env_ref, fresh_ref):
+    sector_count = environment.shape[1]
+
+    def body(
+        src_ref, dst_ref, cnt_ref, first_ref, blocks_ref, top_ref, recv_ref, env_ref, decay_ref,
+        fresh_ref, decay_out_ref,
+    ):
         for site in range(site_count):
+            for sector in range(sector_count):
+                row = decay_ref[site, pl.ds(sector, 1), :]
+                decay_out_ref[site, sector] = jnp.transpose(jnp.broadcast_to(row, decay_out_ref.shape[2:]))
             fresh_ref[site] = env_ref[site].astype(jnp.float32)
             for slot in range(slot_count):
                 place = site * slot_count + slot
                 source = jnp.clip(src_ref[place], 0, sector_count - 1)
                 target = jnp.clip(dst_ref[place], 0, sector_count - 1)
-                product = jnp.dot(
-                    blocks_ref[site, slot], above_ref[site, source], preferred_element_type=jnp.float32
-                )
+                above = jnp.where(first_ref[0] > 0, top_ref[site, source], recv_ref[site, source])
+                product = jnp.dot(blocks_ref[site, slot], above, preferred_element_type=jnp.float32)
                 fresh_ref[site, target] += jnp.where(slot < cnt_ref[site], product, 0.0)
 
     smem = pl.BlockSpec(memory_space=pltpu.SMEM)
     vmem = pl.BlockSpec(memory_space=pltpu.VMEM)
     return pl.pallas_call(
         body,
-        in_specs=[smem, smem, smem, vmem, vmem, vmem],
-        out_specs=vmem,
-        out_shape=jax.ShapeDtypeStruct(environment.shape, jnp.float32),
-    )(sources, targets, counts, blocks, above_env, environment)
-
-
-def backward_kernel(blocks, above_env, rounded, sources, targets, counts):
+        in_specs=[smem] * 4 + [vmem] * 5,
+        out_specs=(vmem, vmem),
+        out_shape=(
+            jax.ShapeDtypeStruct(environment.shape, jnp.float32),
+            jax.ShapeDtypeStruct(environment.shape, jnp.float32),
+        ),
+    )(sources, targets, counts, first, blocks, top_env, received_env, environment, decays)
+
+
+def backward_kernel(blocks, top_env, received_env, rounded, first, sources, targets, counts):
     site_count, slot_count = blocks.shape[:2]
-    sector_count = above_env.shape[1]
-
-    def body(src_ref, dst_ref, cnt_ref, blocks_ref, above_ref, rounded_ref, grads_ref, ret_ref, acc_ref):
+    sector_count = top_env.shape[1]
+
+    def body(src_ref, dst_ref, cnt_ref, first_ref, blocks_ref, top_ref, recv_ref, rounded_ref, grads_ref, ret_ref, acc_ref):
         for site in range(site_count):
             acc_ref[...] = jnp.zeros(acc_ref.shape, jnp.float32)
             for slot in range(slot_count):
@@ -51,7 +59,7 @@
                 target = jnp.clip(dst_ref[place], 0, sector_count - 1)
                 live = slot < cnt_ref[site]
                 picked = rounded_ref[site, target].astype(jnp.bfloat16)
-                gathered = above_ref[site, source]
+                gathered = jnp.where(first_ref[0] > 0, top_ref[site, source], recv_ref[site, source])
                 grad = lax.dot_general(
                     picked, gathered, (((1,), (1,)), ((), ())), preferred_element_type=jnp.float32
                 )
@@ -68,14 +76,14 @@
     vmem = pl.BlockSpec(memory_space=pltpu.VMEM)
     return pl.pallas_call(
         body,
-        in_specs=[smem, smem, smem, vmem, vmem, vmem],
+        in_specs=[smem] * 4 + [vmem] * 4,
         out_specs=(vmem, vmem),
         out_shape=(
             jax.ShapeDtypeStruct(blocks.shape, jnp.bfloat16),
-            jax.ShapeDtypeStruct(above_env.shape, jnp.bfloat16),
+            jax.ShapeDtypeStruct(top_env.shape, jnp.bfloat16),
         ),
-        scratch_shapes=[pltpu.VMEM(above_env.shape[1:], jnp.float32)],
-    )(sources, targets, counts, blocks, above_env, rounded)
+        scratch_shapes=[pltpu.VMEM(top_env.shape[1:], jnp.float32)],
+    )(sources, targets, counts, first, blocks, top_env, received_env, rounded)
 
 
 def carry_kernel(got, part):
@@ -155,7 +163,7 @@
     return (grads, jnp.sum(prods, -1))
 
 
-def chain_scan(fresh, decay_rows, cotangent):
+def chain_scan(fresh, decay_rows, decay_full, cotangent):
     row_count, col_count, flat_rows, channel_count = fresh.shape
     count = lax.axis_size("col")
     rows = row_count * flat_rows
@@ -167,7 +175,7 @@
 
     fresh_c = by_column(fresh)
     weight_c = by_column(cotangent)
-    decay_c = jnp.broadcast_to(by_column(decay_rows[..., None]), fresh_c.shape)
+    decay_c = by_column(decay_full)
     factor = jnp.prod(jnp.swapaxes(decay_rows, 0, 1).reshape(col_count, count, part), 0)
     factor_row = jnp.pad(factor, ((0, 0), (0, channel_count - part)))
     payload = summary_kernel(fresh_c, weight_c, decay_c, factor_row, count)
@@ -185,29 +193,37 @@
     flat_rows = sector_count * block_rows
     bottom = environment[row_count - 1]
     upper_env = from_behind(bottom, "row", 1)
-    upper_env = jnp.where(lax.axis_index("row") == 0, top_boundary, upper_env)
-    above_env = jnp.concatenate([upper_env[None], environment[: row_count - 1]], 0)
+    received_env = jnp.concatenate([upper_env[None], environment[: row_count - 1]], 0)
+    top_env = jnp.concatenate([top_boundary[None], environment[: row_count - 1]], 0)
+    first = (lax.axis_index("row") == 0).astype(jnp.int32).reshape(1)
     site_count = row_count * col_count
 
     def by_site(value):
         return value.reshape((site_count,) + value.shape[2:])
 
-    fresh = forward_kernel(
+    fresh, decay_full = forward_kernel(
         by_site(blocks),
-        by_site(above_env),
+        by_site(top_env),
+        by_site(received_env),
         by_site(environment),
+        by_site(decays),
+        first,
         sources.reshape(-1),
         targets.reshape(-1),
         counts.reshape(-1),
-    ).reshape(row_count, col_count, flat_rows, channel_count)
+    )
+    fresh = fresh.reshape(row_count, col_count, flat_rows, channel_count)
+    decay_full = decay_full.reshape(row_count, col_count, flat_rows, channel_count)
     decay_rows = decays.reshape(row_count, col_count, flat_rows)
     cotangent = weights.reshape(row_count, col_count, flat_rows, channel_count)
-    condition_derivative, gate_grad = chain_scan(fresh, decay_rows, cotangent)
+    condition_derivative, gate_grad = chain_scan(fresh, decay_rows, decay_full, cotangent)
     condition_derivative = condition_derivative.reshape(environment.shape)
     grad_blocks, returned = backward_kernel(
-        blocks.reshape((site_count,) + blocks.shape[2:]),
-        above_env.reshape((site_count,) + above_env.shape[2:]),
-        condition_derivative.reshape((site_count,) + condition_derivative.shape[2:]),
+        by_site(blocks),
+        by_site(top_env),
+        by_site(received_env),
+        by_site(condition_derivative),
+        first,
         sources.reshape(-1),
         targets.reshape(-1),
         counts.reshape(-1),

time: 96.7 us -> 96 us (level)
    unnamed x10 -> x13, local copies, waits for them, and re-layouts: 0.76 us -> 2.08 us
    broadcast_in_dim x1 -> x0, local copies, waits for them, and re-layouts: 1.08 us -> none  [chain_scan(): decay_c = jnp.broadcast_to(by_column(decay_rows[..., None]), fresh_c.shape)]
  transfers between devices with their start and end apart: 2 -> 2, of which waited for: 2 -> 2; matrix products, arithmetic and copies ran while one was open for 3% -> 4% of each run, Pallas kernels for 0% -> 0%
where the time goes in v11:
time: 96 us; the launch traced here: 95.5 us
  blocking collectives  56.5 us (59%)
  Pallas kernels  13.5 us (14%)
  starting transfers between devices  11.1 us (12%)
  waiting for transfers between devices  8.12 us (8%)
  local copies, waits for them, and re-layouts  3.97 us (4%)
  other arithmetic  1.66 us (2%)
    all_to_all x1, blocking collectives, chain_scan(): got = lax.all_to_all(payload, 'col', 0, 0, tiled=True)  32.8 us
    all_to_all x1, blocking collectives, chain_scan(): ret = lax.all_to_all(carries, 'col', 0, 0, tiled=True)  23.7 us
    ppermute x2, starting transfers between devices, from_behind(): lax.ppermute(value, axis, [(source, source + steps) for source in range(i...  11.1 us
    ppermute x2, waiting for transfers between devices, from_behind(): lax.ppermute(value, axis, [(source, source + steps) for source in range(i...  8.12 us
    pallas_call x1, Pallas kernels, backward_kernel(): pl.pallas_call(body, in_specs=[smem] * 4 + [vmem] * 4, out_specs=(vmem, v...  3.11 us
    pallas_call x1, Pallas kernels, fixup_kernel(): pl.pallas_call(body, out_shape=(jax.ShapeDtypeStruct((col_count, rows, ch...  2.89 us
    pallas_call x1, Pallas kernels, forward_kernel(): pl.pallas_call(body, in_specs=[smem] * 4 + [vmem] * 5, out_specs=(vmem, v...  2.77 us
    pallas_call x1, Pallas kernels, summary_kernel(): pl.pallas_call(body, out_shape=jax.ShapeDtypeStruct((count, 2 * part + 1,...  2.5 us
  transfers between devices with their start and end apart: 2, of which 2 were waited for; matrix products, arithmetic and copies ran while one was open for 4% of the time, Pallas kernels for 0%

profile of v11, /device:TPU:17, one launch (start us, length us, event | category | flops | bytes accessed | tf_op | source)
XLA Modules:
  0.0 95.5 jit_solution(17666808848173836276)
XLA Ops:
  0.6 3.8 %collective-permute-start = (bf16[2,5,128,128]{3,2,1,0:T(8,128)(2,1)}, bf16[2,5,128,128]{3,2,1,0:T(8,128)(2,1)S(1)}, u32[]{:S(2)}, u32[]{:S(2)}) collective-permute-start(bf16[2,5,128,128]{3,2,1,0:T(8,128)(2,1)} %bitcast.25), channel_id=1, source_target_pairs={{0,32},{32,64},{64,96},{96,128},{128,160},{160,192},{192,224},{224... | collective-permute-start | bytes 983048 | tf_op jit(solution)/shard_map/ppermute | solution.py:12
  4.4 0.0 copy-start.4
  4.4 0.0 copy-start.3
  4.4 0.7 copy-done.4
  5.1 0.0 copy-start.5
  5.1 0.6 reshape.39.src_ref
  5.7 0.1 copy-done.5
  5.8 0.6 reshape.40.dst_ref
  6.4 0.0 copy-done.3
  6.4 0.6 copy.14
  7.0 0.1 reduce_prod.12
  7.1 0.6 pad.4.factor_ref
  7.7 1.0 %collective-permute-done.recv_ref = bf16[2,5,128,128]{3,2,1,0:T(8,128)(2,1)S(1)} collective-permute-done((bf16[2,5,128,128]{3,2,1,0:T(8,128)(2,1)}, bf16[2,5,128,128]{3,2,1,0:T(8,128)(2,1)S(1)}, u32[]{:S(2)}, u32[]{:S(2)}) %collective-permute-start) | collective-permute-done | bytes 327712 | tf_op jit(solution)/shard_map/ppermute | solution.py:12
  8.7 0.0 copy-start.1
  8.7 0.7 copy-done.1
  9.4 2.8 %shard_map.103 = (f32[2,5,128,128]{3,2,1,0:T(8,128)}, f32[2,5,128,128]{3,2,1,0:T(8,128)}) custom-call(s32[16]{0:T(128)} %reshape.39.src_ref, s32[16]{0:T(128)} %reshape.40.dst_ref, s32[2]{0:T(128)} %bitcast.29, s32[1]{0:T(128)} %bitcast.1.first_ref, bf16[2,8,128,128]{3,2,1,0:T(8,128)(2,1)} %bitcast.23, bf16[2,5,128,128]{3,2,1,0:T(8,128)(2,1)} %top_ref.3, ...), custom_call_target="tpu_custom_call" | custom-call | tf_op jit(solution)/shard_map/pallas_call | solution.py:38
  12.2 2.5 %shard_map.104 = f32[32,41,128]{2,1,0:T(8,128)} custom-call(f32[2,640,128]{2,1,0:T(8,128)} %bitcast.19, f32[2,640,128]{2,1,0:T(8,128)} %bitcast.15, f32[2,640,128]{2,1,0:T(8,128)} %bitcast.21, f32[32,128]{1,0:T(8,128)} %pad.4.factor_ref), custom_call_target="tpu_custom_call" | custom-call | tf_op jit(solution)/shard_map/pallas_call | solution.py:133
  14.7 32.8 %all_to_all.10.got_ref = f32[32,41,128]{2,1,0:T(8,128)} all-to-all(f32[32,41,128]{2,1,0:T(8,128)} %shard_map.104), channel_id=1, replica_groups=mesh['row'=16,'col'=32] {'col'}, dimensions={0} | all-to-all | bytes 1343488 | tf_op jit(solution)/shard_map/all_to_all | solution.py:182
  47.5 2.2 %shard_map.105 = f32[32,40,128]{2,1,0:T(8,128)} custom-call(f32[32,41,128]{2,1,0:T(8,128)} %all_to_all.10.got_ref), custom_call_target="tpu_custom_call" | custom-call | tf_op jit(solution)/shard_map/pallas_call | solution.py:109
  49.7 23.7 %all_to_all.11.carry_ref = f32[32,40,128]{2,1,0:T(8,128)} all-to-all(f32[32,40,128]{2,1,0:T(8,128)} %shard_map.105), channel_id=1, replica_groups=mesh['row'=16,'col'=32] {'col'}, dimensions={0} | all-to-all | bytes 1310720 | tf_op jit(solution)/shard_map/all_to_all | solution.py:184
  73.4 2.9 %shard_map.106 = (f32[2,640,128]{2,1,0:T(8,128)}, f32[2,640,128]{2,1,0:T(8,128)}) custom-call(f32[2,640,128]{2,1,0:T(8,128)} %bitcast.20, f32[2,640,128]{2,1,0:T(8,128)} %bitcast.16, f32[2,640,128]{2,1,0:T(8,128)} %bitcast.22, f32[32,40,128]{2,1,0:T(8,128)} %all_to_all.11.carry_ref), custom_call_target="tpu_custom_call" | custom-call | tf_op jit(solution)/shard_map/pallas_call | solution.py:159
  76.3 0.0 copy-start.2
  76.3 3.1 %shard_map.107 = (bf16[2,8,128,128]{3,2,1,0:T(8,128)(2,1)}, bf16[2,5,128,128]{3,2,1,0:T(8,128)(2,1)}) custom-call(s32[16]{0:T(128)} %reshape.39.src_ref, s32[16]{0:T(128)} %reshape.40.dst_ref, s32[2]{0:T(128)} %bitcast.30, s32[1]{0:T(128)} %bitcast.1.first_ref, bf16[2,8,128,128]{3,2,1,0:T(8,128)(2,1)} %bitcast.24, bf16[2,5,128,128]{3,2,1,0:T(8,128)(2,1)} %top_ref.3, ...), custom_call_target="tpu_custom_call" | custom-call | tf_op jit(solution)/shard_map/pallas_call | solution.py:77
  79.4 0.0 copy-start
  79.4 7.3 %collective-permute-start.1 = (bf16[2,5,128,128]{3,2,1,0:T(8,128)(2,1)}, bf16[2,5,128,128]{3,2,1,0:T(8,128)(2,1)S(1)}, u32[]{:S(2)}, u32[]{:S(2)}) collective-permute-start(bf16[2,5,128,128]{3,2,1,0:T(8,128)(2,1)} %get-tuple-element.13), channel_id=1, source_target_pairs={{32,0},{64,32},{96,64},{128,96},{160,128},{192,160},{224,192},{256... | collective-permute-start | bytes 983048 | tf_op jit(solution)/shard_map/ppermute | solution.py:12
  86.7 0.0 copy-done.2
  86.7 0.8 reduce_sum.9
  87.5 7.1 %collective-permute-done.1 = bf16[2,5,128,128]{3,2,1,0:T(8,128)(2,1)S(1)} collective-permute-done((bf16[2,5,128,128]{3,2,1,0:T(8,128)(2,1)}, bf16[2,5,128,128]{3,2,1,0:T(8,128)(2,1)S(1)}, u32[]{:S(2)}, u32[]{:S(2)}) %collective-permute-start.1) | collective-permute-done | bytes 327712 | tf_op jit(solution)/shard_map/ppermute | solution.py:12
  94.6 0.0 copy-done
  94.6 0.8 fusion
  (1 shorter events, 0.0 us)
Async XLA Ops:
  0.6 8.1 %collective-permute-start = (bf16[2,5,128,128]{3,2,1,0:T(8,128)(2,1)}, bf16[2,5,128,128]{3,2,1,0:T(8,128)(2,1)S(1)}, u32[]{:S(2)}, u32[]{:S(2)}) collective-permute-start(bf16[2,5,128,128]{3,2,1,0:T(8,128)(2,1)} %bitcast.25), channel_id=1, source_target_pairs={{0,32},{32,64},{64,96},{96,128},{128,160},{160,192},{192,224},{224... | collective-permute-start | bytes 983048 | tf_op jit(solution)/shard_map/ppermute | solution.py:12
  4.4 0.7 copy-start.4
  4.4 1.9 %copy-start.3 = (f32[1,2,5,128]{3,1,2,0:T(2,128)S(1)}, f32[1,2,5,128]{3,1,2,0:T(2,128)}, u32[]{:S(2)}) copy-start(f32[1,2,5,128]{3,1,2,0:T(2,128)} %param.14) | copy-start | bytes 15364
  5.1 0.7 copy-start.5
  8.7 0.7 copy-start.1
  76.3 10.4 %copy-start.2 = (f32[2,640,128]{2,1,0:T(8,128)S(1)}, f32[2,640,128]{2,1,0:T(8,128)}, u32[]{:S(2)}) copy-start(f32[2,640,128]{2,1,0:T(8,128)} %get-tuple-element.14) | copy-start | bytes 1966084
  79.4 15.3 %copy-start = (f32[2,640,128]{2,1,0:T(8,128)S(1)}, f32[2,640,128]{2,1,0:T(8,128)}, u32[]{:S(2)}) copy-start(f32[2,640,128]{2,1,0:T(8,128)} %get-tuple-element.11) | copy-start | bytes 1966084
  79.4 15.3 %collective-permute-start.1 = (bf16[2,5,128,128]{3,2,1,0:T(8,128)(2,1)}, bf16[2,5,128,128]{3,2,1,0:T(8,128)(2,1)S(1)}, u32[]{:S(2)}, u32[]{:S(2)}) collective-permute-start(bf16[2,5,128,128]{3,2,1,0:T(8,128)(2,1)} %get-tuple-element.13), channel_id=1, source_target_pairs={{32,0},{64,32},{96,64},{128,96},{160,128},{192,160},{224,192},{256... | collective-permute-start | bytes 983048 | tf_op jit(solution)/shard_map/ppermute | solution.py:12

commit v12 on v11

--- a/solution.py
+++ b/solution.py
@@ -26,9 +26,8 @@
                 decay_out_ref[site, sector] = jnp.transpose(jnp.broadcast_to(row, decay_out_ref.shape[2:]))
             fresh_ref[site] = env_ref[site].astype(jnp.float32)
             for slot in range(slot_count):
-                place = site * slot_count + slot
-                source = jnp.clip(src_ref[place], 0, sector_count - 1)
-                target = jnp.clip(dst_ref[place], 0, sector_count - 1)
+                source = jnp.clip(src_ref[site, slot], 0, sector_count - 1)
+                target = jnp.clip(dst_ref[site, slot], 0, sector_count - 1)
                 above = jnp.where(first_ref[0] > 0, top_ref[site, source], recv_ref[site, source])
                 product = jnp.dot(blocks_ref[site, slot], above, preferred_element_type=jnp.float32)
                 fresh_ref[site, target] += jnp.where(slot < cnt_ref[site], product, 0.0)
@@ -54,9 +53,8 @@
         for site in range(site_count):
             acc_ref[...] = jnp.zeros(acc_ref.shape, jnp.float32)
             for slot in range(slot_count):
-                place = site * slot_count + slot
-                source = jnp.clip(src_ref[place], 0, sector_count - 1)
-                target = jnp.clip(dst_ref[place], 0, sector_count - 1)
+                source = jnp.clip(src_ref[site, slot], 0, sector_count - 1)
+                target = jnp.clip(dst_ref[site, slot], 0, sector_count - 1)
                 live = slot < cnt_ref[site]
                 picked = rounded_ref[site, target].astype(jnp.bfloat16)
                 gathered = jnp.where(first_ref[0] > 0, top_ref[site, source], recv_ref[site, source])
@@ -208,8 +206,8 @@
         by_site(environment),
         by_site(decays),
         first,
-        sources.reshape(-1),
-        targets.reshape(-1),
+        sources.reshape(site_count, -1),
+        targets.reshape(site_count, -1),
         counts.reshape(-1),
     )
     fresh = fresh.reshape(row_count, col_count, flat_rows, channel_count)
@@ -224,8 +222,8 @@
         by_site(received_env),
         by_site(condition_derivative),
         first,
-        sources.reshape(-1),
-        targets.reshape(-1),
+        sources.reshape(site_count, -1),
+        targets.reshape(site_count, -1),
         counts.reshape(-1),
     )
     grad_blocks = grad_blocks.reshape(blocks.shape)

time: 96 us -> 96 us (level)
  waiting for transfers between devices: 8.12 us -> 9.39 us
  local copies, waits for them, and re-layouts: 3.97 us -> 2.71 us
    ppermute x2, waiting for transfers between devices: 8.12 us -> 9.39 us  [from_behind(): lax.ppermute(value, axis, [(source, source + steps) for source in range(i...]
    reshape x2 -> x0, local copies, waits for them, and re-layouts: 1.18 us -> none  [the longest x1 0.59 us: local(): targets.reshape(-1)]
    unnamed x13 -> x9, local copies, waits for them, and re-layouts: 2.08 us -> 2 us
  transfers between devices with their start and end apart: 2 -> 2, of which waited for: 2 -> 2; matrix products, arithmetic and copies ran while one was open for 4% -> 2% of each run, Pallas kernels for 0% -> 0%
where the time goes in v12:
time: 96 us; the launch traced here: 95.4 us
  blocking collectives  56.5 us (59%)
  Pallas kernels  13.5 us (14%)
  starting transfers between devices  11.1 us (12%)
  waiting for transfers between devices  9.39 us (10%)
  local copies, waits for them, and re-layouts  2.71 us (3%)
  other arithmetic  1.66 us (2%)
    all_to_all x1, blocking collectives, chain_scan(): got = lax.all_to_all(payload, 'col', 0, 0, tiled=True)  32.8 us
    all_to_all x1, blocking collectives, chain_scan(): ret = lax.all_to_all(carries, 'col', 0, 0, tiled=True)  23.7 us
    ppermute x2, starting transfers between devices, from_behind(): lax.ppermute(value, axis, [(source, source + steps) for source in range(i...  11.1 us
    ppermute x2, waiting for transfers between devices, from_behind(): lax.ppermute(value, axis, [(source, source + steps) for source in range(i...  9.39 us
    pallas_call x1, Pallas kernels, backward_kernel(): pl.pallas_call(body, in_specs=[smem] * 4 + [vmem] * 4, out_specs=(vmem, v...  3.12 us
    pallas_call x1, Pallas kernels, fixup_kernel(): pl.pallas_call(body, out_shape=(jax.ShapeDtypeStruct((col_count, rows, ch...  2.88 us
    pallas_call x1, Pallas kernels, forward_kernel(): pl.pallas_call(body, in_specs=[smem] * 4 + [vmem] * 5, out_specs=(vmem, v...  2.77 us
    pallas_call x1, Pallas kernels, summary_kernel(): pl.pallas_call(body, out_shape=jax.ShapeDtypeStruct((count, 2 * part + 1,...  2.5 us
  transfers between devices with their start and end apart: 2, of which 2 were waited for; matrix products, arithmetic and copies ran while one was open for 2% of the time, Pallas kernels for 0%

profile of v12, /device:TPU:17, one launch (start us, length us, event | category | flops | bytes accessed | tf_op | source)
XLA Modules:
  0.0 95.4 jit_solution(18026059997035973004)
XLA Ops:
  0.6 3.8 %collective-permute-start = (bf16[2,5,128,128]{3,2,1,0:T(8,128)(2,1)}, bf16[2,5,128,128]{3,2,1,0:T(8,128)(2,1)S(1)}, u32[]{:S(2)}, u32[]{:S(2)}) collective-permute-start(bf16[2,5,128,128]{3,2,1,0:T(8,128)(2,1)} %bitcast.27), channel_id=1, source_target_pairs={{0,32},{32,64},{64,96},{96,128},{128,160},{160,192},{192,224},{224... | collective-permute-start | bytes 983048 | tf_op jit(solution)/shard_map/ppermute | solution.py:12
  4.4 0.0 copy-start.3
  4.4 0.7 copy-done.3
  5.1 0.6 copy.14
  5.7 0.1 reduce_prod.12
  5.8 0.6 pad.4.factor_ref
  6.4 2.3 %collective-permute-done.recv_ref = bf16[2,5,128,128]{3,2,1,0:T(8,128)(2,1)S(1)} collective-permute-done((bf16[2,5,128,128]{3,2,1,0:T(8,128)(2,1)}, bf16[2,5,128,128]{3,2,1,0:T(8,128)(2,1)S(1)}, u32[]{:S(2)}, u32[]{:S(2)}) %collective-permute-start) | collective-permute-done | bytes 327712 | tf_op jit(solution)/shard_map/ppermute | solution.py:12
  8.7 0.0 copy-start.1
  8.7 0.7 copy-done.1
  9.4 2.8 %shard_map.103 = (f32[2,5,128,128]{3,2,1,0:T(8,128)}, f32[2,5,128,128]{3,2,1,0:T(8,128)}) custom-call(s32[2,8]{1,0:T(2,128)} %bitcast.31, s32[2,8]{1,0:T(2,128)} %bitcast.33, s32[2]{0:T(128)} %bitcast.35, s32[1]{0:T(128)} %bitcast.3.first_ref, bf16[2,8,128,128]{3,2,1,0:T(8,128)(2,1)} %bitcast.25, bf16[2,5,128,128]{3,2,1,0:T(8,128)(2,1)} %top_ref.3, ...), custom_call_target="tpu_custom_call" | custom-call | tf_op jit(solution)/shard_map/pallas_call | solution.py:37
  12.2 2.5 %shard_map.104 = f32[32,41,128]{2,1,0:T(8,128)} custom-call(f32[2,640,128]{2,1,0:T(8,128)} %bitcast.21, f32[2,640,128]{2,1,0:T(8,128)} %bitcast.17, f32[2,640,128]{2,1,0:T(8,128)} %bitcast.23, f32[32,128]{1,0:T(8,128)} %pad.4.factor_ref), custom_call_target="tpu_custom_call" | custom-call | tf_op jit(solution)/shard_map/pallas_call | solution.py:131
  14.7 32.8 %all_to_all.10.got_ref = f32[32,41,128]{2,1,0:T(8,128)} all-to-all(f32[32,41,128]{2,1,0:T(8,128)} %shard_map.104), channel_id=1, replica_groups=mesh['row'=16,'col'=32] {'col'}, dimensions={0} | all-to-all | bytes 1343488 | tf_op jit(solution)/shard_map/all_to_all | solution.py:180
  47.5 2.2 %shard_map.105 = f32[32,40,128]{2,1,0:T(8,128)} custom-call(f32[32,41,128]{2,1,0:T(8,128)} %all_to_all.10.got_ref), custom_call_target="tpu_custom_call" | custom-call | tf_op jit(solution)/shard_map/pallas_call | solution.py:107
  49.7 23.7 %all_to_all.11.carry_ref = f32[32,40,128]{2,1,0:T(8,128)} all-to-all(f32[32,40,128]{2,1,0:T(8,128)} %shard_map.105), channel_id=1, replica_groups=mesh['row'=16,'col'=32] {'col'}, dimensions={0} | all-to-all | bytes 1310720 | tf_op jit(solution)/shard_map/all_to_all | solution.py:182
  73.4 2.9 %shard_map.106 = (f32[2,640,128]{2,1,0:T(8,128)}, f32[2,640,128]{2,1,0:T(8,128)}) custom-call(f32[2,640,128]{2,1,0:T(8,128)} %bitcast.22, f32[2,640,128]{2,1,0:T(8,128)} %bitcast.18, f32[2,640,128]{2,1,0:T(8,128)} %bitcast.24, f32[32,40,128]{2,1,0:T(8,128)} %all_to_all.11.carry_ref), custom_call_target="tpu_custom_call" | custom-call | tf_op jit(solution)/shard_map/pallas_call | solution.py:157
  76.3 0.0 copy-start.2
  76.3 3.1 %shard_map.107 = (bf16[2,8,128,128]{3,2,1,0:T(8,128)(2,1)}, bf16[2,5,128,128]{3,2,1,0:T(8,128)(2,1)}) custom-call(s32[2,8]{1,0:T(2,128)} %bitcast.32, s32[2,8]{1,0:T(2,128)} %bitcast.34, s32[2]{0:T(128)} %bitcast.36, s32[1]{0:T(128)} %bitcast.3.first_ref, bf16[2,8,128,128]{3,2,1,0:T(8,128)(2,1)} %bitcast.26, bf16[2,5,128,128]{3,2,1,0:T(8,128)(2,1)} %top_ref.3, ...), custom_call_target="tpu_custom_call" | custom-call | tf_op jit(solution)/shard_map/pallas_call | solution.py:75
  79.4 0.0 copy-start
  79.4 7.3 %collective-permute-start.1 = (bf16[2,5,128,128]{3,2,1,0:T(8,128)(2,1)}, bf16[2,5,128,128]{3,2,1,0:T(8,128)(2,1)S(1)}, u32[]{:S(2)}, u32[]{:S(2)}) collective-permute-start(bf16[2,5,128,128]{3,2,1,0:T(8,128)(2,1)} %get-tuple-element.13), channel_id=1, source_target_pairs={{32,0},{64,32},{96,64},{128,96},{160,128},{192,160},{224,192},{256... | collective-permute-start | bytes 983048 | tf_op jit(solution)/shard_map/ppermute | solution.py:12
  86.7 0.0 copy-done.2
  86.7 0.8 reduce_sum.9
  87.5 7.1 %collective-permute-done.1 = bf16[2,5,128,128]{3,2,1,0:T(8,128)(2,1)S(1)} collective-permute-done((bf16[2,5,128,128]{3,2,1,0:T(8,128)(2,1)}, bf16[2,5,128,128]{3,2,1,0:T(8,128)(2,1)S(1)}, u32[]{:S(2)}, u32[]{:S(2)}) %collective-permute-start.1) | collective-permute-done | bytes 327712 | tf_op jit(solution)/shard_map/ppermute | solution.py:12
  94.6 0.0 copy-done
  94.6 0.8 fusion
  (1 shorter events, 0.0 us)
Async XLA Ops:
  0.6 8.1 %collective-permute-start = (bf16[2,5,128,128]{3,2,1,0:T(8,128)(2,1)}, bf16[2,5,128,128]{3,2,1,0:T(8,128)(2,1)S(1)}, u32[]{:S(2)}, u32[]{:S(2)}) collective-permute-start(bf16[2,5,128,128]{3,2,1,0:T(8,128)(2,1)} %bitcast.27), channel_id=1, source_target_pairs={{0,32},{32,64},{64,96},{96,128},{128,160},{160,192},{192,224},{224... | collective-permute-start | bytes 983048 | tf_op jit(solution)/shard_map/ppermute | solution.py:12
  4.4 0.7 copy-start.3
  8.7 0.7 copy-start.1
  76.3 10.4 %copy-start.2 = (f32[2,640,128]{2,1,0:T(8,128)S(1)}, f32[2,640,128]{2,1,0:T(8,128)}, u32[]{:S(2)}) copy-start(f32[2,640,128]{2,1,0:T(8,128)} %get-tuple-element.14) | copy-start | bytes 1966084
  79.4 15.2 %copy-start = (f32[2,640,128]{2,1,0:T(8,128)S(1)}, f32[2,640,128]{2,1,0:T(8,128)}, u32[]{:S(2)}) copy-start(f32[2,640,128]{2,1,0:T(8,128)} %get-tuple-element.11) | copy-start | bytes 1966084
  79.4 15.2 %collective-permute-start.1 = (bf16[2,5,128,128]{3,2,1,0:T(8,128)(2,1)}, bf16[2,5,128,128]{3,2,1,0:T(8,128)(2,1)S(1)}, u32[]{:S(2)}, u32[]{:S(2)}) collective-permute-start(bf16[2,5,128,128]{3,2,1,0:T(8,128)(2,1)} %get-tuple-element.13), channel_id=1, source_target_pairs={{32,0},{64,32},{96,64},{128,96},{160,128},{192,160},{224,192},{256... | collective-permute-start | bytes 983048 | tf_op jit(solution)/shard_map/ppermute | solution.py:12

commit v13 on v12

--- a/solution.py
+++ b/solution.py
@@ -110,11 +110,14 @@
     )(got)
 
 
-def summary_kernel(fresh, cotangent, decay_col, factor_row, count):
+def summary_kernel(fresh, cotangent, decay_col, count):
     col_count, rows, channel_count = fresh.shape
     part = rows // count
 
-    def body(fresh_ref, weight_ref, decay_ref, factor_ref, out_ref):
+    def body(fresh_ref, weight_ref, decay_ref, out_ref):
+        diagonal = lax.broadcasted_iota(jnp.int32, (part, channel_count), 0) == lax.broadcasted_iota(
+            jnp.int32, (part, channel_count), 1
+        )
         for chunk in range(count):
             span = pl.ds(chunk * part, part)
             state = fresh_ref[0, span, :]
@@ -126,12 +129,17 @@
             grad = decay_ref[0, span, :] * grad
             out_ref[chunk, pl.ds(0, part), :] = state
             out_ref[chunk, pl.ds(part, part), :] = grad
-            out_ref[chunk, pl.ds(2 * part, 1), :] = factor_ref[pl.ds(chunk, 1), :]
+            factor = decay_ref[0, span, :]
+            for column in range(1, col_count):
+                factor = factor * decay_ref[column, span, :]
+            out_ref[chunk, pl.ds(2 * part, 1), :] = jnp.sum(
+                jnp.where(diagonal, factor, 0.0), axis=0, keepdims=True
+            )
 
     return pl.pallas_call(
         body,
         out_shape=jax.ShapeDtypeStruct((count, 2 * part + 1, channel_count), jnp.float32),
-    )(fresh, cotangent, decay_col, factor_row)
+    )(fresh, cotangent, decay_col)
 
 
 def fixup_kernel(fresh, cotangent, decay_full, carries):
@@ -174,9 +182,7 @@
     fresh_c = by_column(fresh)
     weight_c = by_column(cotangent)
     decay_c = by_column(decay_full)
-    factor = jnp.prod(jnp.swapaxes(decay_rows, 0, 1).reshape(col_count, count, part), 0)
-    factor_row = jnp.pad(factor, ((0, 0), (0, channel_count - part)))
-    payload = summary_kernel(fresh_c, weight_c, decay_c, factor_row, count)
+    payload = summary_kernel(fresh_c, weight_c, decay_c, count)
     got = lax.all_to_all(payload, "col", 0, 0, tiled=True)
     carries = carry_kernel(got, part)
     ret = lax.all_to_all(carries, "col", 0, 0, tiled=True)

time: 96 us -> 96 us (level)
  no operation moved by 1% of the time
where the time goes in v13:
time: 96 us; the launch traced here: 95.5 us
  blocking collectives  56.5 us (59%)
  Pallas kernels  13.5 us (14%)
  starting transfers between devices  11.1 us (12%)
  waiting for transfers between devices  10.1 us (11%)
  local copies, waits for them, and re-layouts  2.01 us (2%)
  other arithmetic  1.65 us (2%)
    all_to_all x1, blocking collectives, chain_scan(): got = lax.all_to_all(payload, 'col', 0, 0, tiled=True)  32.8 us
    all_to_all x1, blocking collectives, chain_scan(): ret = lax.all_to_all(carries, 'col', 0, 0, tiled=True)  23.7 us
    ppermute x2, starting transfers between devices, from_behind(): lax.ppermute(value, axis, [(source, source + steps) for source in range(i...  11.1 us
    ppermute x2, waiting for transfers between devices, from_behind(): lax.ppermute(value, axis, [(source, source + steps) for source in range(i...  10.1 us
    pallas_call x1, Pallas kernels, backward_kernel(): pl.pallas_call(body, in_specs=[smem] * 4 + [vmem] * 4, out_specs=(vmem, v...  3.12 us
    pallas_call x1, Pallas kernels, fixup_kernel(): pl.pallas_call(body, out_shape=(jax.ShapeDtypeStruct((col_count, rows, ch...  2.9 us
    pallas_call x1, Pallas kernels, forward_kernel(): pl.pallas_call(body, in_specs=[smem] * 4 + [vmem] * 5, out_specs=(vmem, v...  2.78 us
    pallas_call x1, Pallas kernels, summary_kernel(): pl.pallas_call(body, out_shape=jax.ShapeDtypeStruct((count, 2 * part + 1,...  2.51 us
  transfers between devices with their start and end apart: 2, of which 2 were waited for; matrix products, arithmetic and copies ran while one was open for 2% of the time, Pallas kernels for 0%

profile of v13, /device:TPU:17, one launch (start us, length us, event | category | flops | bytes accessed | tf_op | source)
XLA Modules:
  0.0 95.5 jit_solution(8244029932822197228)
XLA Ops:
  0.6 3.8 %collective-permute-start = (bf16[2,5,128,128]{3,2,1,0:T(8,128)(2,1)}, bf16[2,5,128,128]{3,2,1,0:T(8,128)(2,1)S(1)}, u32[]{:S(2)}, u32[]{:S(2)}) collective-permute-start(bf16[2,5,128,128]{3,2,1,0:T(8,128)(2,1)} %bitcast.27), channel_id=1, source_target_pairs={{0,32},{32,64},{64,96},{96,128},{128,160},{160,192},{192,224},{224... | collective-permute-start | bytes 983048 | tf_op jit(solution)/shard_map/ppermute | solution.py:12
  4.4 0.0 copy-start.3
  4.4 0.7 copy-done.3
  5.1 0.6 copy.13
  5.7 3.0 %collective-permute-done.recv_ref = bf16[2,5,128,128]{3,2,1,0:T(8,128)(2,1)S(1)} collective-permute-done((bf16[2,5,128,128]{3,2,1,0:T(8,128)(2,1)}, bf16[2,5,128,128]{3,2,1,0:T(8,128)(2,1)S(1)}, u32[]{:S(2)}, u32[]{:S(2)}) %collective-permute-start) | collective-permute-done | bytes 327712 | tf_op jit(solution)/shard_map/ppermute | solution.py:12
  8.7 0.0 copy-start.1
  8.7 0.7 copy-done.1
  9.4 2.8 %shard_map.103 = (f32[2,5,128,128]{3,2,1,0:T(8,128)}, f32[2,5,128,128]{3,2,1,0:T(8,128)}) custom-call(s32[2,8]{1,0:T(2,128)} %bitcast.31, s32[2,8]{1,0:T(2,128)} %bitcast.33, s32[2]{0:T(128)} %bitcast.35, s32[1]{0:T(128)} %bitcast.3.first_ref, bf16[2,8,128,128]{3,2,1,0:T(8,128)(2,1)} %bitcast.25, bf16[2,5,128,128]{3,2,1,0:T(8,128)(2,1)} %top_ref.3, ...), custom_call_target="tpu_custom_call" | custom-call | tf_op jit(solution)/shard_map/pallas_call | solution.py:37
  12.2 2.5 %shard_map.104 = f32[32,41,128]{2,1,0:T(8,128)} custom-call(f32[2,640,128]{2,1,0:T(8,128)} %bitcast.21, f32[2,640,128]{2,1,0:T(8,128)} %bitcast.17, f32[2,640,128]{2,1,0:T(8,128)} %bitcast.23), custom_call_target="tpu_custom_call" | custom-call | tf_op jit(solution)/shard_map/pallas_call | solution.py:139
  14.7 32.8 %all_to_all.10.got_ref = f32[32,41,128]{2,1,0:T(8,128)} all-to-all(f32[32,41,128]{2,1,0:T(8,128)} %shard_map.104), channel_id=1, replica_groups=mesh['row'=16,'col'=32] {'col'}, dimensions={0} | all-to-all | bytes 1343488 | tf_op jit(solution)/shard_map/all_to_all | solution.py:186
  47.5 2.2 %shard_map.105 = f32[32,40,128]{2,1,0:T(8,128)} custom-call(f32[32,41,128]{2,1,0:T(8,128)} %all_to_all.10.got_ref), custom_call_target="tpu_custom_call" | custom-call | tf_op jit(solution)/shard_map/pallas_call | solution.py:107
  49.7 23.7 %all_to_all.11.carry_ref = f32[32,40,128]{2,1,0:T(8,128)} all-to-all(f32[32,40,128]{2,1,0:T(8,128)} %shard_map.105), channel_id=1, replica_groups=mesh['row'=16,'col'=32] {'col'}, dimensions={0} | all-to-all | bytes 1310720 | tf_op jit(solution)/shard_map/all_to_all | solution.py:188
  73.4 2.9 %shard_map.106 = (f32[2,640,128]{2,1,0:T(8,128)}, f32[2,640,128]{2,1,0:T(8,128)}) custom-call(f32[2,640,128]{2,1,0:T(8,128)} %bitcast.22, f32[2,640,128]{2,1,0:T(8,128)} %bitcast.18, f32[2,640,128]{2,1,0:T(8,128)} %bitcast.24, f32[32,40,128]{2,1,0:T(8,128)} %all_to_all.11.carry_ref), custom_call_target="tpu_custom_call" | custom-call | tf_op jit(solution)/shard_map/pallas_call | solution.py:165
  76.3 0.0 copy-start.2
  76.3 3.1 %shard_map.107 = (bf16[2,8,128,128]{3,2,1,0:T(8,128)(2,1)}, bf16[2,5,128,128]{3,2,1,0:T(8,128)(2,1)}) custom-call(s32[2,8]{1,0:T(2,128)} %bitcast.32, s32[2,8]{1,0:T(2,128)} %bitcast.34, s32[2]{0:T(128)} %bitcast.36, s32[1]{0:T(128)} %bitcast.3.first_ref, bf16[2,8,128,128]{3,2,1,0:T(8,128)(2,1)} %bitcast.26, bf16[2,5,128,128]{3,2,1,0:T(8,128)(2,1)} %top_ref.3, ...), custom_call_target="tpu_custom_call" | custom-call | tf_op jit(solution)/shard_map/pallas_call | solution.py:75
  79.4 0.0 copy-start
  79.4 7.3 %collective-permute-start.1 = (bf16[2,5,128,128]{3,2,1,0:T(8,128)(2,1)}, bf16[2,5,128,128]{3,2,1,0:T(8,128)(2,1)S(1)}, u32[]{:S(2)}, u32[]{:S(2)}) collective-permute-start(bf16[2,5,128,128]{3,2,1,0:T(8,128)(2,1)} %get-tuple-element.13), channel_id=1, source_target_pairs={{32,0},{64,32},{96,64},{128,96},{160,128},{192,160},{224,192},{256... | collective-permute-start | bytes 983048 | tf_op jit(solution)/shard_map/ppermute | solution.py:12
  86.7 0.0 copy-done.2
  86.7 0.8 reduce_sum.9
  87.6 7.1 %collective-permute-done.1 = bf16[2,5,128,128]{3,2,1,0:T(8,128)(2,1)S(1)} collective-permute-done((bf16[2,5,128,128]{3,2,1,0:T(8,128)(2,1)}, bf16[2,5,128,128]{3,2,1,0:T(8,128)(2,1)S(1)}, u32[]{:S(2)}, u32[]{:S(2)}) %collective-permute-start.1) | collective-permute-done | bytes 327712 | tf_op jit(solution)/shard_map/ppermute | solution.py:12
  94.7 0.0 copy-done
  94.7 0.8 fusion
Async XLA Ops:
  0.6 8.1 %collective-permute-start = (bf16[2,5,128,128]{3,2,1,0:T(8,128)(2,1)}, bf16[2,5,128,128]{3,2,1,0:T(8,128)(2,1)S(1)}, u32[]{:S(2)}, u32[]{:S(2)}) collective-permute-start(bf16[2,5,128,128]{3,2,1,0:T(8,128)(2,1)} %bitcast.27), channel_id=1, source_target_pairs={{0,32},{32,64},{64,96},{96,128},{128,160},{160,192},{192,224},{224... | collective-permute-start | bytes 983048 | tf_op jit(solution)/shard_map/ppermute | solution.py:12
  4.4 0.7 copy-start.3
  8.7 0.7 copy-start.1
  76.3 10.4 %copy-start.2 = (f32[2,640,128]{2,1,0:T(8,128)S(1)}, f32[2,640,128]{2,1,0:T(8,128)}, u32[]{:S(2)}) copy-start(f32[2,640,128]{2,1,0:T(8,128)} %get-tuple-element.14) | copy-start | bytes 1966084
  79.4 15.3 %copy-start = (f32[2,640,128]{2,1,0:T(8,128)S(1)}, f32[2,640,128]{2,1,0:T(8,128)}, u32[]{:S(2)}) copy-start(f32[2,640,128]{2,1,0:T(8,128)} %get-tuple-element.11) | copy-start | bytes 1966084
  79.4 15.2 %collective-permute-start.1 = (bf16[2,5,128,128]{3,2,1,0:T(8,128)(2,1)}, bf16[2,5,128,128]{3,2,1,0:T(8,128)(2,1)S(1)}, u32[]{:S(2)}, u32[]{:S(2)}) collective-permute-start(bf16[2,5,128,128]{3,2,1,0:T(8,128)(2,1)} %get-tuple-element.13), channel_id=1, source_target_pairs={{32,0},{64,32},{96,64},{128,96},{160,128},{192,160},{224,192},{256... | collective-permute-start | bytes 983048 | tf_op jit(solution)/shard_map/ppermute | solution.py:12

commit v14 on v13

--- a/solution.py
+++ b/solution.py
@@ -45,42 +45,43 @@
     )(sources, targets, counts, first, blocks, top_env, received_env, environment, decays)
 
 
-def backward_kernel(blocks, top_env, received_env, rounded, first, sources, targets, counts):
+def backward_kernel(blocks, top_env, received_env, rounded, first, sources, targets, counts, want_returned):
     site_count, slot_count = blocks.shape[:2]
     sector_count = top_env.shape[1]
 
-    def body(src_ref, dst_ref, cnt_ref, first_ref, blocks_ref, top_ref, recv_ref, rounded_ref, grads_ref, ret_ref, acc_ref):
+    def body(src_ref, dst_ref, cnt_ref, first_ref, blocks_ref, top_ref, recv_ref, rounded_ref, out_ref, *scratch):
         for site in range(site_count):
-            acc_ref[...] = jnp.zeros(acc_ref.shape, jnp.float32)
+            if want_returned:
+                scratch[0][...] = jnp.zeros(scratch[0].shape, jnp.float32)
             for slot in range(slot_count):
                 source = jnp.clip(src_ref[site, slot], 0, sector_count - 1)
                 target = jnp.clip(dst_ref[site, slot], 0, sector_count - 1)
                 live = slot < cnt_ref[site]
                 picked = rounded_ref[site, target].astype(jnp.bfloat16)
-                gathered = jnp.where(first_ref[0] > 0, top_ref[site, source], recv_ref[site, source])
-                grad = lax.dot_general(
-                    picked, gathered, (((1,), (1,)), ((), ())), preferred_element_type=jnp.float32
-                )
-                grads_ref[site, slot] = jnp.where(live, grad, 0.0).astype(grads_ref.dtype)
-                contrib = lax.dot_general(
-                    blocks_ref[site, slot], picked, (((0,), (0,)), ((), ())),
-                    preferred_element_type=jnp.float32,
-                )
-                acc_ref[source] += jnp.where(live, contrib, 0.0)
-
-            ret_ref[site] = acc_ref[...].astype(ret_ref.dtype)
+                if want_returned:
+                    contrib = lax.dot_general(
+                        blocks_ref[site, slot], picked, (((0,), (0,)), ((), ())),
+                        preferred_element_type=jnp.float32,
+                    )
+                    scratch[0][source] += jnp.where(live, contrib, 0.0)
+                else:
+                    gathered = jnp.where(first_ref[0] > 0, top_ref[site, source], recv_ref[site, source])
+                    grad = lax.dot_general(
+                        picked, gathered, (((1,), (1,)), ((), ())), preferred_element_type=jnp.float32
+                    )
+                    out_ref[site, slot] = jnp.where(live, grad, 0.0).astype(out_ref.dtype)
+            if want_returned:
+                out_ref[site] = scratch[0][...].astype(out_ref.dtype)
 
     smem = pl.BlockSpec(memory_space=pltpu.SMEM)
     vmem = pl.BlockSpec(memory_space=pltpu.VMEM)
+    shape = top_env.shape if want_returned else blocks.shape
     return pl.pallas_call(
         body,
         in_specs=[smem] * 4 + [vmem] * 4,
-        out_specs=(vmem, vmem),
-        out_shape=(
-            jax.ShapeDtypeStruct(blocks.shape, jnp.bfloat16),
-            jax.ShapeDtypeStruct(top_env.shape, jnp.bfloat16),
-        ),
-        scratch_shapes=[pltpu.VMEM(top_env.shape[1:], jnp.float32)],
+        out_specs=vmem,
+        out_shape=jax.ShapeDtypeStruct(shape, jnp.bfloat16),
+        scratch_shapes=[pltpu.VMEM(top_env.shape[1:], jnp.float32)] if want_returned else [],
     )(sources, targets, counts, first, blocks, top_env, received_env, rounded)
 
 
@@ -222,7 +223,7 @@
     cotangent = weights.reshape(row_count, col_count, flat_rows, channel_count)
     condition_derivative, gate_grad = chain_scan(fresh, decay_rows, decay_full, cotangent)
     condition_derivative = condition_derivative.reshape(environment.shape)
-    grad_blocks, returned = backward_kernel(
+    backward_args = (
         by_site(blocks),
         by_site(top_env),
         by_site(received_env),
@@ -232,6 +233,8 @@
         targets.reshape(site_count, -1),
         counts.reshape(-1),
     )
+    returned = backward_kernel(*backward_args, True)
+    grad_blocks = backward_kernel(*backward_args, False)
     grad_blocks = grad_blocks.reshape(blocks.shape)
     returned = returned.reshape(environment.shape)
     below_rows = from_behind(returned[0], "row", -1)

time: 96 us -> 95.4 us (level)
  waiting for transfers between devices: 10.1 us -> 7.31 us
  Pallas kernels: 13.5 us -> 15.8 us
    ppermute x2, waiting for transfers between devices: 10.1 us -> 7.31 us  [from_behind(): lax.ppermute(value, axis, [(source, source + steps) for source in range(i...]
    pallas_call x1 -> x2, Pallas kernels: 3.12 us -> 5.46 us  [backward_kernel(): pl.pallas_call(body, in_specs=[smem] * 4 + [vmem] * 4, out_specs=vmem, ou...]
  transfers between devices with their start and end apart: 2 -> 2, of which waited for: 2 -> 2; matrix products, arithmetic and copies ran while one was open for 2% -> 2% of each run, Pallas kernels for 0% -> 3%
where the time goes in v14:
time: 95.4 us; the launch traced here: 94.9 us
  blocking collectives  56.5 us (59%)
  Pallas kernels  15.8 us (17%)
  starting transfers between devices  10.9 us (11%)
  waiting for transfers between devices  7.31 us (8%)
  local copies, waits for them, and re-layouts  2.01 us (2%)
  other arithmetic  1.65 us (2%)
    all_to_all x1, blocking collectives, chain_scan(): got = lax.all_to_all(payload, 'col', 0, 0, tiled=True)  32.8 us
    all_to_all x1, blocking collectives, chain_scan(): ret = lax.all_to_all(carries, 'col', 0, 0, tiled=True)  23.7 us
    ppermute x2, starting transfers between devices, from_behind(): lax.ppermute(value, axis, [(source, source + steps) for source in range(i...  10.9 us
    ppermute x2, waiting for transfers between devices, from_behind(): lax.ppermute(value, axis, [(source, source + steps) for source in range(i...  7.31 us
    pallas_call x2, Pallas kernels, backward_kernel(): pl.pallas_call(body, in_specs=[smem] * 4 + [vmem] * 4, out_specs=vmem, ou...  5.46 us
    pallas_call x1, Pallas kernels, fixup_kernel(): pl.pallas_call(body, out_shape=(jax.ShapeDtypeStruct((col_count, rows, ch...  2.9 us
    pallas_call x1, Pallas kernels, forward_kernel(): pl.pallas_call(body, in_specs=[smem] * 4 + [vmem] * 5, out_specs=(vmem, v...  2.78 us
    pallas_call x1, Pallas kernels, summary_kernel(): pl.pallas_call(body, out_shape=jax.ShapeDtypeStruct((count, 2 * part + 1,...  2.51 us
  transfers between devices with their start and end apart: 2, of which 2 were waited for; matrix products, arithmetic and copies ran while one was open for 2% of the time, Pallas kernels for 3%

profile of v14, /device:TPU:17, one launch (start us, length us, event | category | flops | bytes accessed | tf_op | source)
XLA Modules:
  0.0 94.9 jit_solution(776865904009702126)
XLA Ops:
  0.6 3.8 %collective-permute-start = (bf16[2,5,128,128]{3,2,1,0:T(8,128)(2,1)}, bf16[2,5,128,128]{3,2,1,0:T(8,128)(2,1)S(1)}, u32[]{:S(2)}, u32[]{:S(2)}) collective-permute-start(bf16[2,5,128,128]{3,2,1,0:T(8,128)(2,1)} %bitcast.30), channel_id=1, source_target_pairs={{0,32},{32,64},{64,96},{96,128},{128,160},{160,192},{192,224},{224... | collective-permute-start | bytes 983048 | tf_op jit(solution)/shard_map/ppermute | solution.py:12
  4.4 0.0 copy-start.3
  4.4 0.7 copy-done.3
  5.1 0.6 copy.13
  5.7 3.0 %collective-permute-done.recv_ref = bf16[2,5,128,128]{3,2,1,0:T(8,128)(2,1)S(1)} collective-permute-done((bf16[2,5,128,128]{3,2,1,0:T(8,128)(2,1)}, bf16[2,5,128,128]{3,2,1,0:T(8,128)(2,1)S(1)}, u32[]{:S(2)}, u32[]{:S(2)}) %collective-permute-start) | collective-permute-done | bytes 327712 | tf_op jit(solution)/shard_map/ppermute | solution.py:12
  8.7 0.0 copy-start.1
  8.7 0.7 copy-done.1
  9.4 2.8 %shard_map.103 = (f32[2,5,128,128]{3,2,1,0:T(8,128)}, f32[2,5,128,128]{3,2,1,0:T(8,128)}) custom-call(s32[2,8]{1,0:T(2,128)} %bitcast.33, s32[2,8]{1,0:T(2,128)} %bitcast.36, s32[2]{0:T(128)} %bitcast.40, s32[1]{0:T(128)} %bitcast.3.first_ref, bf16[2,8,128,128]{3,2,1,0:T(8,128)(2,1)} %bitcast.20, bf16[2,5,128,128]{3,2,1,0:T(8,128)(2,1)} %top_ref.5, ...), custom_call_target="tpu_custom_call" | custom-call | tf_op jit(solution)/shard_map/pallas_call | solution.py:37
  12.2 2.5 %shard_map.104 = f32[32,41,128]{2,1,0:T(8,128)} custom-call(f32[2,640,128]{2,1,0:T(8,128)} %bitcast.25, f32[2,640,128]{2,1,0:T(8,128)} %bitcast.23, f32[2,640,128]{2,1,0:T(8,128)} %bitcast.27), custom_call_target="tpu_custom_call" | custom-call | tf_op jit(solution)/shard_map/pallas_call | solution.py:140
  14.7 32.8 %all_to_all.10.got_ref = f32[32,41,128]{2,1,0:T(8,128)} all-to-all(f32[32,41,128]{2,1,0:T(8,128)} %shard_map.104), channel_id=1, replica_groups=mesh['row'=16,'col'=32] {'col'}, dimensions={0} | all-to-all | bytes 1343488 | tf_op jit(solution)/shard_map/all_to_all | solution.py:187
  47.5 2.2 %shard_map.105 = f32[32,40,128]{2,1,0:T(8,128)} custom-call(f32[32,41,128]{2,1,0:T(8,128)} %all_to_all.10.got_ref), custom_call_target="tpu_custom_call" | custom-call | tf_op jit(solution)/shard_map/pallas_call | solution.py:108
  49.7 23.7 %all_to_all.11.carry_ref = f32[32,40,128]{2,1,0:T(8,128)} all-to-all(f32[32,40,128]{2,1,0:T(8,128)} %shard_map.105), channel_id=1, replica_groups=mesh['row'=16,'col'=32] {'col'}, dimensions={0} | all-to-all | bytes 1310720 | tf_op jit(solution)/shard_map/all_to_all | solution.py:189
  73.4 2.9 %shard_map.106 = (f32[2,640,128]{2,1,0:T(8,128)}, f32[2,640,128]{2,1,0:T(8,128)}) custom-call(f32[2,640,128]{2,1,0:T(8,128)} %bitcast.26, f32[2,640,128]{2,1,0:T(8,128)} %bitcast.24, f32[2,640,128]{2,1,0:T(8,128)} %bitcast.28, f32[32,40,128]{2,1,0:T(8,128)} %all_to_all.11.carry_ref), custom_call_target="tpu_custom_call" | custom-call | tf_op jit(solution)/shard_map/pallas_call | solution.py:166
  76.3 0.0 copy-start.2
  76.3 2.7 %shard_map.108 = bf16[2,5,128,128]{3,2,1,0:T(8,128)(2,1)} custom-call(s32[2,8]{1,0:T(2,128)} %bitcast.34, s32[2,8]{1,0:T(2,128)} %bitcast.37, s32[2]{0:T(128)} %bitcast.41, s32[1]{0:T(128)} %bitcast.3.first_ref, bf16[2,8,128,128]{3,2,1,0:T(8,128)(2,1)} %bitcast.21, bf16[2,5,128,128]{3,2,1,0:T(8,128)(2,1)} %top_ref.5, bf16[2,5,128,128]{3,2,1,0:T(8,128)(2,1)} %copy-done.1, ...), custom_call_target="tpu_custom_call" | custom-call | tf_op jit(solution)/shard_map/pallas_call | solution.py:79
  79.0 7.2 %collective-permute-start.1 = (bf16[2,5,128,128]{3,2,1,0:T(8,128)(2,1)}, bf16[2,5,128,128]{3,2,1,0:T(8,128)(2,1)S(1)}, u32[]{:S(2)}, u32[]{:S(2)}) collective-permute-start(bf16[2,5,128,128]{3,2,1,0:T(8,128)(2,1)} %shard_map.108), channel_id=1, source_target_pairs={{32,0},{64,32},{96,64},{128,96},{160,128},{192,160},{224,192},{256... | collective-permute-start | bytes 983048 | tf_op jit(solution)/shard_map/ppermute | solution.py:12
  86.1 0.0 copy-done.2
  86.1 0.8 reduce_sum.9
  87.0 0.0 copy-start
  87.0 2.8 %shard_map.107 = bf16[2,8,128,128]{3,2,1,0:T(8,128)(2,1)} custom-call(s32[2,8]{1,0:T(2,128)} %bitcast.35, s32[2,8]{1,0:T(2,128)} %bitcast.38, s32[2]{0:T(128)} %bitcast.42, s32[1]{0:T(128)} %bitcast.3.first_ref, bf16[2,8,128,128]{3,2,1,0:T(8,128)(2,1)} %bitcast.22, bf16[2,5,128,128]{3,2,1,0:T(8,128)(2,1)} %top_ref.5, bf16[2,5,128,128]{3,2,1,0:T(8,128)(2,1)} %copy-done.1, ...), custom_call_target="tpu_custom_call" | custom-call | tf_op jit(solution)/shard_map/pallas_call | solution.py:79
  89.8 4.3 %collective-permute-done.1 = bf16[2,5,128,128]{3,2,1,0:T(8,128)(2,1)S(1)} collective-permute-done((bf16[2,5,128,128]{3,2,1,0:T(8,128)(2,1)}, bf16[2,5,128,128]{3,2,1,0:T(8,128)(2,1)S(1)}, u32[]{:S(2)}, u32[]{:S(2)}) %collective-permute-start.1) | collective-permute-done | bytes 327712 | tf_op jit(solution)/shard_map/ppermute | solution.py:12
  94.1 0.0 copy-done
  94.1 0.8 fusion
Async XLA Ops:
  0.6 8.1 %collective-permute-start = (bf16[2,5,128,128]{3,2,1,0:T(8,128)(2,1)}, bf16[2,5,128,128]{3,2,1,0:T(8,128)(2,1)S(1)}, u32[]{:S(2)}, u32[]{:S(2)}) collective-permute-start(bf16[2,5,128,128]{3,2,1,0:T(8,128)(2,1)} %bitcast.30), channel_id=1, source_target_pairs={{0,32},{32,64},{64,96},{96,128},{128,160},{160,192},{192,224},{224... | collective-permute-start | bytes 983048 | tf_op jit(solution)/shard_map/ppermute | solution.py:12
  4.4 0.7 copy-start.3
  8.7 0.7 copy-start.1
  76.3 9.8 %copy-start.2 = (f32[2,640,128]{2,1,0:T(8,128)S(1)}, f32[2,640,128]{2,1,0:T(8,128)}, u32[]{:S(2)}) copy-start(f32[2,640,128]{2,1,0:T(8,128)} %get-tuple-element.10) | copy-start | bytes 1966084
  79.0 15.1 %collective-permute-start.1 = (bf16[2,5,128,128]{3,2,1,0:T(8,128)(2,1)}, bf16[2,5,128,128]{3,2,1,0:T(8,128)(2,1)S(1)}, u32[]{:S(2)}, u32[]{:S(2)}) collective-permute-start(bf16[2,5,128,128]{3,2,1,0:T(8,128)(2,1)} %shard_map.108), channel_id=1, source_target_pairs={{32,0},{64,32},{96,64},{128,96},{160,128},{192,160},{224,192},{256... | collective-permute-start | bytes 983048 | tf_op jit(solution)/shard_map/ppermute | solution.py:12
  87.0 7.1 %copy-start = (f32[2,640,128]{2,1,0:T(8,128)S(1)}, f32[2,640,128]{2,1,0:T(8,128)}, u32[]{:S(2)}) copy-start(f32[2,640,128]{2,1,0:T(8,128)} %get-tuple-element.9) | copy-start | bytes 1966084

commit v15 on v14

--- a/solution.py
+++ b/solution.py
@@ -143,12 +143,12 @@
     )(fresh, cotangent, decay_col)
 
 
-def fixup_kernel(fresh, cotangent, decay_full, carries):
+def fixup_kernel(fresh, cotangent, decay_full, carries, want_products):
     col_count, rows, channel_count = fresh.shape
     count = carries.shape[0]
     part = rows // count
 
-    def body(fresh_ref, weight_ref, decay_ref, carry_ref, grad_ref, prod_ref):
+    def body(fresh_ref, weight_ref, decay_ref, carry_ref, out_ref):
         for chunk in range(count):
             span = pl.ds(chunk * part, part)
             grad = carry_ref[chunk, pl.ds(part, part), :]
@@ -156,18 +156,19 @@
             for column in reversed(range(col_count)):
                 grad = weight_ref[column, span, :] + grad
                 grads[column] = grad
-                grad_ref[column, span, :] = grad
+                if not want_products:
+                    out_ref[column, span, :] = grad
                 grad = decay_ref[column, span, :] * grad
-            state = carry_ref[chunk, pl.ds(0, part), :]
-            for column in range(col_count):
-                prod_ref[column, span, :] = grads[column] * state
-                state = decay_ref[column, span, :] * state + fresh_ref[column, span, :]
-
-    grads, prods = pl.pallas_call(
-        body,
-        out_shape=(jax.ShapeDtypeStruct((col_count, rows, channel_count), jnp.float32),) * 2,
+            if want_products:
+                state = carry_ref[chunk, pl.ds(0, part), :]
+                for column in range(col_count):
+                    out_ref[column, span, :] = grads[column] * state
+                    state = decay_ref[column, span, :] * state + fresh_ref[column, span, :]
+
+    return pl.pallas_call(
+        body,
+        out_shape=jax.ShapeDtypeStruct((col_count, rows, channel_count), jnp.float32),
     )(fresh, cotangent, decay_full, carries)
-    return (grads, jnp.sum(prods, -1))
 
 
 def chain_scan(fresh, decay_rows, decay_full, cotangent):
@@ -187,7 +188,8 @@
     got = lax.all_to_all(payload, "col", 0, 0, tiled=True)
     carries = carry_kernel(got, part)
     ret = lax.all_to_all(carries, "col", 0, 0, tiled=True)
-    grads, gates = fixup_kernel(fresh_c, weight_c, decay_c, ret)
+    grads = fixup_kernel(fresh_c, weight_c, decay_c, ret, False)
+    gates = jnp.sum(fixup_kernel(fresh_c, weight_c, decay_c, ret, True), -1)
     grads = jnp.swapaxes(grads.reshape(col_count, row_count, flat_rows, channel_count), 0, 1)
     gates = jnp.swapaxes(gates.reshape(col_count, row_count, flat_rows), 0, 1)
     return (grads, gates)

time: 95.4 us -> 96.4 us (1.010)
  the two profiles are of different devices: /device:TPU:17 before, /device:TPU:25 now
where the time goes in v15:
time: 96.4 us; the launch traced here: 95.8 us
  blocking collectives  57.5 us (60%)
  Pallas kernels  18.1 us (19%)
  starting transfers between devices  11.7 us (12%)
  waiting for transfers between devices  3.02 us (3%)
  other arithmetic  2.73 us (3%)
  local copies, waits for them, and re-layouts  2 us (2%)
    all_to_all x1, blocking collectives, chain_scan(): got = lax.all_to_all(payload, 'col', 0, 0, tiled=True)  33.5 us
    all_to_all x1, blocking collectives, chain_scan(): ret = lax.all_to_all(carries, 'col', 0, 0, tiled=True)  24 us
    ppermute x2, starting transfers between devices, from_behind(): lax.ppermute(value, axis, [(source, source + steps) for source in range(i...  11.7 us
    pallas_call x2, Pallas kernels, backward_kernel(): pl.pallas_call(body, in_specs=[smem] * 4 + [vmem] * 4, out_specs=vmem, ou...  5.37 us
    pallas_call x2, Pallas kernels, fixup_kernel(): pl.pallas_call(body, out_shape=jax.ShapeDtypeStruct((col_count, rows, cha...  5.27 us
    ppermute x2, waiting for transfers between devices, from_behind(): lax.ppermute(value, axis, [(source, source + steps) for source in range(i...  3.02 us
    pallas_call x1, Pallas kernels, forward_kernel(): pl.pallas_call(body, in_specs=[smem] * 4 + [vmem] * 5, out_specs=(vmem, v...  2.78 us
    pallas_call x1, Pallas kernels, summary_kernel(): pl.pallas_call(body, out_shape=jax.ShapeDtypeStruct((count, 2 * part + 1,...  2.51 us
  transfers between devices with their start and end apart: 2, of which 1 were waited for; matrix products, arithmetic and copies ran while one was open for 3% of the time, Pallas kernels for 6%

profile of v15, /device:TPU:25, one launch (start us, length us, event | category | flops | bytes accessed | tf_op | source)
XLA Modules:
  0.0 95.8 jit_solution(12052865423250366963)
XLA Ops:
  0.6 5.0 %collective-permute-start = (bf16[2,5,128,128]{3,2,1,0:T(8,128)(2,1)}, bf16[2,5,128,128]{3,2,1,0:T(8,128)(2,1)S(1)}, u32[]{:S(2)}, u32[]{:S(2)}) collective-permute-start(bf16[2,5,128,128]{3,2,1,0:T(8,128)(2,1)} %bitcast.33), channel_id=1, source_target_pairs={{0,32},{32,64},{64,96},{96,128},{128,160},{160,192},{192,224},{224... | collective-permute-start | bytes 983048 | tf_op jit(solution)/shard_map/ppermute | solution.py:12
  5.6 0.0 copy-start.2
  5.6 0.7 copy-done.2
  6.3 0.6 copy.13
  6.9 3.0 %collective-permute-done.recv_ref = bf16[2,5,128,128]{3,2,1,0:T(8,128)(2,1)S(1)} collective-permute-done((bf16[2,5,128,128]{3,2,1,0:T(8,128)(2,1)}, bf16[2,5,128,128]{3,2,1,0:T(8,128)(2,1)S(1)}, u32[]{:S(2)}, u32[]{:S(2)}) %collective-permute-start) | collective-permute-done | bytes 327712 | tf_op jit(solution)/shard_map/ppermute | solution.py:12
  9.9 0.0 copy-start.1
  9.9 0.7 copy-done.1
  10.7 2.8 %shard_map.103 = (f32[2,5,128,128]{3,2,1,0:T(8,128)}, f32[2,5,128,128]{3,2,1,0:T(8,128)}) custom-call(s32[2,8]{1,0:T(2,128)} %bitcast.36, s32[2,8]{1,0:T(2,128)} %bitcast.39, s32[2]{0:T(128)} %bitcast.43, s32[1]{0:T(128)} %bitcast.3.first_ref, bf16[2,8,128,128]{3,2,1,0:T(8,128)(2,1)} %bitcast.29, bf16[2,5,128,128]{3,2,1,0:T(8,128)(2,1)} %top_ref.5, ...), custom_call_target="tpu_custom_call" | custom-call | tf_op jit(solution)/shard_map/pallas_call | solution.py:37
  13.4 2.5 %shard_map.104 = f32[32,41,128]{2,1,0:T(8,128)} custom-call(f32[2,640,128]{2,1,0:T(8,128)} %bitcast.23, f32[2,640,128]{2,1,0:T(8,128)} %bitcast.20, f32[2,640,128]{2,1,0:T(8,128)} %bitcast.26), custom_call_target="tpu_custom_call" | custom-call | tf_op jit(solution)/shard_map/pallas_call | solution.py:140
  15.9 33.5 %all_to_all.10.got_ref = f32[32,41,128]{2,1,0:T(8,128)} all-to-all(f32[32,41,128]{2,1,0:T(8,128)} %shard_map.104), channel_id=1, replica_groups=mesh['row'=16,'col'=32] {'col'}, dimensions={0} | all-to-all | bytes 1343488 | tf_op jit(solution)/shard_map/all_to_all | solution.py:188
  49.5 2.2 %shard_map.105 = f32[32,40,128]{2,1,0:T(8,128)} custom-call(f32[32,41,128]{2,1,0:T(8,128)} %all_to_all.10.got_ref), custom_call_target="tpu_custom_call" | custom-call | tf_op jit(solution)/shard_map/pallas_call | solution.py:108
  51.7 24.0 %all_to_all.11.carry_ref = f32[32,40,128]{2,1,0:T(8,128)} all-to-all(f32[32,40,128]{2,1,0:T(8,128)} %shard_map.105), channel_id=1, replica_groups=mesh['row'=16,'col'=32] {'col'}, dimensions={0} | all-to-all | bytes 1310720 | tf_op jit(solution)/shard_map/all_to_all | solution.py:190
  75.7 2.6 %shard_map.106 = f32[2,640,128]{2,1,0:T(8,128)} custom-call(f32[2,640,128]{2,1,0:T(8,128)} %bitcast.24, f32[2,640,128]{2,1,0:T(8,128)} %bitcast.21, f32[2,640,128]{2,1,0:T(8,128)} %bitcast.27, f32[32,40,128]{2,1,0:T(8,128)} %all_to_all.11.carry_ref), custom_call_target="tpu_custom_call" | custom-call | tf_op jit(solution)/shard_map/pallas_call | solution.py:168
  78.3 2.6 %shard_map.108 = bf16[2,5,128,128]{3,2,1,0:T(8,128)(2,1)} custom-call(s32[2,8]{1,0:T(2,128)} %bitcast.37, s32[2,8]{1,0:T(2,128)} %bitcast.40, s32[2]{0:T(128)} %bitcast.44, s32[1]{0:T(128)} %bitcast.3.first_ref, bf16[2,8,128,128]{3,2,1,0:T(8,128)(2,1)} %bitcast.30, bf16[2,5,128,128]{3,2,1,0:T(8,128)(2,1)} %top_ref.5, bf16[2,5,128,128]{3,2,1,0:T(8,128)(2,1)} %copy-done.1, ...), custom_call_target="tpu_custom_call" | custom-call | tf_op jit(solution)/shard_map/pallas_call | solution.py:79
  80.8 6.7 %collective-permute-start.1 = (bf16[2,5,128,128]{3,2,1,0:T(8,128)(2,1)}, bf16[2,5,128,128]{3,2,1,0:T(8,128)(2,1)S(1)}, u32[]{:S(2)}, u32[]{:S(2)}) collective-permute-start(bf16[2,5,128,128]{3,2,1,0:T(8,128)(2,1)} %shard_map.108), channel_id=1, source_target_pairs={{32,0},{64,32},{96,64},{128,96},{160,128},{192,160},{224,192},{256... | collective-permute-start | bytes 983048 | tf_op jit(solution)/shard_map/ppermute | solution.py:12
  87.6 2.7 %shard_map.109 = f32[2,640,128]{2,1,0:T(8,128)} custom-call(f32[2,640,128]{2,1,0:T(8,128)} %bitcast.25, f32[2,640,128]{2,1,0:T(8,128)} %bitcast.22, f32[2,640,128]{2,1,0:T(8,128)} %bitcast.28, f32[32,40,128]{2,1,0:T(8,128)} %all_to_all.11.carry_ref), custom_call_target="tpu_custom_call" | custom-call | tf_op jit(solution)/shard_map/pallas_call | solution.py:168
  90.2 1.9 %reduce_sum.9 = f32[2,640]{1,0:T(2,128)} reduce(f32[2,640,128]{2,1,0:T(8,128)} %shard_map.109, f32[]{:T(128)} %constant.9.clone.1), dimensions={2}, to_apply=%region_0.0 | reduce | flops 162560 | bytes 660484 | tf_op jit(solution)/shard_map/reduce_sum | solution.py:192
  92.2 0.0 copy-start
  92.2 2.8 %shard_map.107 = bf16[2,8,128,128]{3,2,1,0:T(8,128)(2,1)} custom-call(s32[2,8]{1,0:T(2,128)} %bitcast.38, s32[2,8]{1,0:T(2,128)} %bitcast.41, s32[2]{0:T(128)} %bitcast.45, s32[1]{0:T(128)} %bitcast.3.first_ref, bf16[2,8,128,128]{3,2,1,0:T(8,128)(2,1)} %bitcast.31, bf16[2,5,128,128]{3,2,1,0:T(8,128)(2,1)} %top_ref.5, bf16[2,5,128,128]{3,2,1,0:T(8,128)(2,1)} %copy-done.1, ...), custom_call_target="tpu_custom_call" | custom-call | tf_op jit(solution)/shard_map/pallas_call | solution.py:79
  95.0 0.0 collective-permute-done.1
  95.0 0.0 copy-done
  95.0 0.8 fusion
Async XLA Ops:
  0.6 9.3 %collective-permute-start = (bf16[2,5,128,128]{3,2,1,0:T(8,128)(2,1)}, bf16[2,5,128,128]{3,2,1,0:T(8,128)(2,1)S(1)}, u32[]{:S(2)}, u32[]{:S(2)}) collective-permute-start(bf16[2,5,128,128]{3,2,1,0:T(8,128)(2,1)} %bitcast.33), channel_id=1, source_target_pairs={{0,32},{32,64},{64,96},{96,128},{128,160},{160,192},{192,224},{224... | collective-permute-start | bytes 983048 | tf_op jit(solution)/shard_map/ppermute | solution.py:12
  5.6 0.7 copy-start.2
  9.9 0.7 copy-start.1
  80.8 14.1 %collective-permute-start.1 = (bf16[2,5,128,128]{3,2,1,0:T(8,128)(2,1)}, bf16[2,5,128,128]{3,2,1,0:T(8,128)(2,1)S(1)}, u32[]{:S(2)}, u32[]{:S(2)}) collective-permute-start(bf16[2,5,128,128]{3,2,1,0:T(8,128)(2,1)} %shard_map.108), channel_id=1, source_target_pairs={{32,0},{64,32},{96,64},{128,96},{160,128},{192,160},{224,192},{256... | collective-permute-start | bytes 983048 | tf_op jit(solution)/shard_map/ppermute | solution.py:12
  92.2 2.8 %copy-start = (f32[2,640,128]{2,1,0:T(8,128)S(1)}, f32[2,640,128]{2,1,0:T(8,128)}, u32[]{:S(2)}) copy-start(f32[2,640,128]{2,1,0:T(8,128)} %shard_map.106) | copy-start | bytes 1966084
